TPU v7x, 512 devices: a whole 4x8x8 slice. The times are simulated.
512 devices in a mesh: ctx: 64 (over y, x, z_hi), head: 8 (over z_lo, core).
Axes of the slice: x: 4, y: 8, z: 8 (z_hi: 2, z_lo: 4; z = z_hi * 4 + z_lo), core: 2. Of those that a mesh axis runs over, the one named last changes fastest.
Arguments:
- head_inputs: bfloat16 [8192, 2048], P('ctx', 'head'), may hold values from -0.125 to 0.125
- write_keys: bfloat16 [8192, 128], P('ctx'), may hold values from -0.1875 to 0.1875
- read_queries: bfloat16 [8192, 128], P('ctx'), may hold values from -0.1875 to 0.1875
- log_decay: float32 [64, 8192], P('head', 'ctx'), may hold values from -1 to 0, as said below
- out_grad: bfloat16 [8192, 2048], P('ctx', 'head'), may hold values from -16 to 16
Outputs:
- input_grad: bfloat16 [8192, 2048], P('ctx', 'head')
- write_grad: bfloat16 [8192, 128], P(('ctx', 'head'))
- read_grad: bfloat16 [8192, 128], P(('ctx', 'head'))
Inputs may be any that keep to these rules, and one draw needn't show every extreme that they name: `log_decay`: negative everywhere.
All inputs are finite; a program needn't handle non-finite values.
Results may differ from a plain program's by a relative error of at most 0.0063.
Values sent between devices are 32-bit elements; how exact they have to be, the bound alone decides.
No kernel may reach another device: no remote copies, remote signals or barrier semaphores. Data moves between devices by JAX's collectives and lax.ppermute only.
A program may use at most 64 MiB of HBM per device.

v0:
```python
import jax
import jax.numpy as jnp
from jax import lax
from jax.sharding import PartitionSpec as P

L = 128


def carried_in(shard, axis, combine, identity, reverse):
    devices, mine = (lax.axis_size(axis), lax.axis_index(axis))
    everything = jax.tree.map(lambda part: lax.all_gather(part, axis), shard)
    start = jax.tree.map(
        lambda part, zero: jnp.broadcast_to(jnp.asarray(zero, part.dtype), part.shape),
        shard,
        identity,
    )

    def turn(k, before):
        at = devices - 1 - k if reverse else k
        reached = at > mine if reverse else at < mine
        new = combine(before, jax.tree.map(lambda part: part[at], everything))
        return jax.tree.map(lambda a, b: jnp.where(reached, a, b), new, before)

    return lax.fori_loop(0, devices, turn, start)


def decay_table(cumulative):
    length = cumulative.shape[1]
    causal = jnp.arange(length)[:, None] >= jnp.arange(length)[None, :]
    spread = cumulative[:, :, None] - cumulative[:, None, :]
    return jnp.exp(jnp.where(causal[None], spread, -jnp.inf))


def scaled_rows(values, factor):
    head_count = factor.shape[0]
    length = factor.shape[1]
    shaped = values.reshape(length, head_count, -1) * factor.T[:, :, None]
    return shaped.astype(jnp.bfloat16).reshape(length, -1)


def mixing_terms(element):
    block_inputs, block_grads, block_write, block_read, block_cum = element
    head_count = block_cum.shape[0]
    length = block_cum.shape[1]
    decay_mat = decay_table(block_cum)
    scores = jnp.dot(block_read, block_write.T, preferred_element_type=jnp.float32)
    mixing = (scores[None] * decay_mat).astype(jnp.bfloat16)
    inputs_heads = block_inputs.reshape(length, head_count, -1)
    grads_heads = block_grads.reshape(length, head_count, -1)
    input_mix = jnp.einsum(
        "hts,thp->shp", mixing, grads_heads, preferred_element_type=jnp.float32
    ).reshape(length, -1)
    pair_grad = jnp.einsum(
        "thp,shp->hts", grads_heads, inputs_heads, preferred_element_type=jnp.float32
    )
    score_grad = jnp.sum(pair_grad * decay_mat, axis=0)
    write_mix = jnp.dot(
        score_grad.T, block_read.astype(jnp.float32), precision=lax.Precision.HIGHEST
    )
    read_mix = jnp.dot(score_grad, block_write.astype(jnp.float32), precision=lax.Precision.HIGHEST)
    return (input_mix, write_mix, read_mix)


def block_sources(element):
    block_inputs, block_grads, block_write, block_read, block_cum = element
    head_count = block_cum.shape[0]
    block_end = block_cum[:, -1:]
    weighted_inputs = scaled_rows(block_inputs, jnp.exp(block_end - block_cum))
    weighted_grads = scaled_rows(block_grads, jnp.exp(block_cum))
    through = jnp.repeat(jnp.exp(block_end[:, 0]), block_inputs.shape[1] // head_count)
    own_state = jnp.dot(block_write.T, weighted_inputs, preferred_element_type=jnp.float32)
    own_grad = jnp.dot(block_read.T, weighted_grads, preferred_element_type=jnp.float32)
    return (own_state, own_grad, through)


def forward_combine(earlier, latter):
    return (earlier[0] * latter[0], latter[0][None, :] * earlier[1] + latter[1])


def backward_combine(earlier, latter):
    return (latter[0] * earlier[0], latter[1] + latter[0][None, :] * earlier[1])


def per_device(head_inputs, write_keys, read_queries, log_decay, out_grad):
    tokens, feature_width = head_inputs.shape
    head_count = log_decay.shape[0]
    states = write_keys.shape[1]
    blocks = tokens // L
    cumulative = jnp.cumsum(log_decay.reshape(head_count, blocks, L), axis=2).transpose(1, 0, 2)
    inputs_blk = head_inputs.reshape(blocks, L, feature_width)
    grads_blk = out_grad.reshape(blocks, L, feature_width)
    write_blk = write_keys.reshape(blocks, L, states)
    read_blk = read_queries.reshape(blocks, L, states)
    pieces = (inputs_blk, grads_blk, write_blk, read_blk, cumulative)
    own_state, own_grad, through = lax.map(block_sources, pieces)

    def fold_step(carry, element):
        decay_acc, state_acc, grad_acc = carry
        state_piece, grad_piece, factor = element
        return (
            (
                decay_acc * factor,
                factor[None, :] * state_acc + state_piece,
                grad_acc + decay_acc[None, :] * grad_piece,
            ),
            None,
        )

    unit_decay = jnp.ones((feature_width,), jnp.float32)
    empty_state = jnp.zeros((states, feature_width), jnp.float32)
    (device_decay, device_state, device_grad), _ = lax.scan(
        fold_step, (unit_decay, empty_state, empty_state), (own_state, own_grad, through)
    )
    _, state_entry = carried_in(
        (device_decay, device_state), "ctx", forward_combine, (unit_decay, empty_state), False
    )
    _, grad_exit = carried_in(
        (device_decay, device_grad), "ctx", backward_combine, (unit_decay, empty_state), True
    )

    def state_step(current, element):
        state_piece, factor = element
        return (factor[None, :] * current + state_piece, current.astype(jnp.bfloat16))

    _, entries_bf = lax.scan(state_step, state_entry, (own_state, through))

    def grad_step(current, element):
        grad_piece, factor = element
        return (grad_piece + factor[None, :] * current, current.astype(jnp.bfloat16))

    _, exits_bf = lax.scan(grad_step, grad_exit, (own_grad, through), reverse=True)
    input_mix, write_mix, read_mix = lax.map(mixing_terms, pieces)

    def finish_step(element):
        block_inputs, block_grads, block_write, block_cum, entry_bf, exit_bf = element
        block_end = block_cum[:, -1:]
        forward_w = jnp.exp(block_end - block_cum)
        weighted_inputs = scaled_rows(block_inputs, forward_w)
        weighted_grads = scaled_rows(block_grads, jnp.exp(block_cum))
        input_state = (
            jnp.dot(block_write, exit_bf, preferred_element_type=jnp.float32).reshape(
                L, head_count, -1
            )
            * forward_w.T[:, :, None]
        )
        write_state = jnp.dot(weighted_inputs, exit_bf.T, preferred_element_type=jnp.float32)
        read_state = jnp.dot(weighted_grads, entry_bf.T, preferred_element_type=jnp.float32)
        return (input_state.reshape(L, -1), write_state, read_state)

    input_state, write_state, read_state = lax.map(
        finish_step, (inputs_blk, grads_blk, write_blk, cumulative, entries_bf, exits_bf)
    )
    input_grad = (input_mix + input_state).astype(jnp.bfloat16).reshape(tokens, feature_width)
    write_carried = write_state.reshape(tokens, states)
    read_carried = read_state.reshape(tokens, states)
    write_mix_sum, read_mix_sum, write_state_sum, read_state_sum = (
        lax.psum_scatter(
            write_mix.reshape(tokens, states), "head", scatter_dimension=0, tiled=True
        ),
        lax.psum_scatter(read_mix.reshape(tokens, states), "head", scatter_dimension=0, tiled=True),
        lax.psum_scatter(write_carried, "head", scatter_dimension=0, tiled=True),
        lax.psum_scatter(read_carried, "head", scatter_dimension=0, tiled=True),
    )
    write_sum = write_mix_sum + write_state_sum
    read_sum = read_mix_sum + read_state_sum
    return (input_grad, write_sum.astype(jnp.bfloat16), read_sum.astype(jnp.bfloat16))


def solution(mesh):
    placed = (P("ctx", "head"), P("ctx", None), P("ctx", None), P("head", "ctx"), P("ctx", "head"))
    return jax.shard_map(
        per_device,
        mesh=mesh,
        in_specs=placed,
        out_specs=(P("ctx", "head"), P(("ctx", "head"), None), P(("ctx", "head"), None)),
        check_vma=False,
    )
```

profile of v0, /device:TPU:1, one launch (start us, length us, event | category | flops | bytes accessed | tf_op | source)
XLA Modules:
  0.0 596.3 jit_solution(15345392027020652110)
XLA Ops:
  11.5 1.6 convolution_bitcast_fusion.1
  13.7 1.0 fusion.20
  15.8 214.7 %all-gather.2 = f32[64,1,256]{2,1,0:T(1,128)S(1)} all-gather(f32[1,1,256]{2,1,0:T(1,128)S(1)} %reshape.122), channel_id=1, replica_groups=mesh['ctx'=64,'head'=8] {'ctx'}, dimensions={0}, use_global_device_ids=true | all-gather | bytes 66560 | tf_op jit(solution)/shard_map/all_gather | solution.py:11
  230.8 16.3 %all-gather.8.cloned.1.call-done = f32[8192,256]{0,1:T(8,128)} async-done(((f32[128,256]{0,1:T(8,128)}), f32[8192,256]{0,1:T(8,128)}) %all-gather.8.cloned.1.call-update) | async-done | bytes 8388624 | tf_op jit(solution)/shard_map/all_gather | solution.py:11
  247.1 9.0 %copy.31 = f32[8192,256]{1,0:T(8,128)} copy(f32[8192,256]{0,1:T(8,128)} %all-gather.8.cloned.1.call-done) | data formatting | bytes 16777216
  256.1 65.5 %while.21 = (s32[]{:T(128)}, f32[128,256]{1,0:T(8,128)S(1)}, s32[]{:T(128)}, f32[64,256]{1,0:T(8,128)S(1)}, f32[64,128,256]{2,1,0:T(8,128)}, /*index=5*/s32[]{:T(128)}, s32[]{:T(128)}) while((s32[]{:T(128)}, f32[128,256]{1,0:T(8,128)S(1)}, s32[]{:T(128)}, f32[64,256]{1,0:T(8,128)S(1)}, f32[64,128,256]{2,1,0:T(8,128)}, ...), condition=%wide.region_8.9_spmd.clone, body=%wide.region_7.8_spmd.clone.sunk | while | flops 131076 | bytes 396393 | solution.py:24
  258.2 1.0 fusion.41
  259.2 1.0 fusion.41
  260.2 1.0 fusion.41
  261.2 1.0 fusion.41
  263.3 1.0 fusion.41
  264.3 1.0 fusion.41
  265.3 1.0 fusion.41
  266.3 1.0 fusion.41
  267.4 1.0 fusion.41
  268.4 1.0 fusion.41
  269.4 1.0 fusion.41
  270.4 1.0 fusion.41
  271.5 1.0 fusion.41
  272.5 1.0 fusion.41
  275.6 1.0 fusion.41
  279.7 1.0 fusion.41
  282.7 1.0 fusion.41
  303.2 1.0 fusion.41
  304.2 1.0 fusion.41
  310.4 1.0 fusion.41
  322.5 156.3 %all-gather.6.cloned.1.call-done = f32[8192,256]{0,1:T(8,128)} async-done(((f32[128,256]{0,1:T(8,128)}), f32[8192,256]{0,1:T(8,128)}) %all-gather.6.cloned.1.call-update) | async-done | bytes 8388624 | tf_op jit(solution)/shard_map/all_gather | solution.py:11
  478.8 9.0 %copy.30 = f32[8192,256]{1,0:T(8,128)} copy(f32[8192,256]{0,1:T(8,128)} %all-gather.6.cloned.1.call-done) | data formatting | bytes 16777216
  487.8 65.1 %while.20 = (s32[]{:T(128)}, f32[128,256]{1,0:T(8,128)S(1)}, s32[]{:T(128)}, f32[64,128,256]{2,1,0:T(8,128)}, f32[64,256]{1,0:T(8,128)S(1)}, /*index=5*/s32[]{:T(128)}, s32[]{:T(128)}, s32[]{:T(128)}, s32[]{:T(128)}) while((s32[]{:T(128)}, f32[128,256]{1,0:T(8,128)S(1)}, s32[]{:T(128)}, f32[64,128,256]{2,1,0:T(8,128)}, ...), condition=%wide.region_2.3_spmd.clone, body=%wide.region_1.2_spmd.clone.sunk | while | flops 131080 | bytes 396455 | solution.py:24
  554.7 1.3 convert_element_type.63
  556.0 32.5 %reduce-scatter.3.cloned.1.call-done = f32[16,128]{1,0:T(8,128)} async-done(((f32[128,128]{1,0:T(8,128)}), f32[16,128]{1,0:T(8,128)}) %reduce-scatter.3.cloned.1.call-update) | async-done | bytes 8208 | tf_op jit(solution)/shard_map/reduce_scatter | solution.py:157
  588.5 1.3 convert_element_type.61
  (273 shorter events, 115.2 us)
Async XLA Ops:
  7.2 2.4 copy-start
  7.2 239.9 %all-gather.8.cloned.1.call-start = ((), (), s32[]{:S(2)}) async-start(), calls=%async_computation.3 | async-start | bytes 8519680 | tf_op jit(solution)/shard_map/all_gather | solution.py:11
  10.5 468.3 %all-gather.6.cloned.1.call-start = ((), (), s32[]{:S(2)}) async-start(), calls=%async_computation.2 | async-start | bytes 8519680 | tf_op jit(solution)/shard_map/all_gather | solution.py:11
  13.1 541.6 %reduce-scatter.5.cloned.1.call-start = ((), (), s32[]{:S(2)}) async-start(), calls=%async_computation.5 | async-start | bytes 73728 | tf_op jit(solution)/shard_map/reduce_scatter | solution.py:160
  322.5 266.0 %reduce-scatter.3.cloned.1.call-start = ((), (), s32[]{:S(2)}) async-start(), calls=%async_computation.4 | async-start | bytes 73728 | tf_op jit(solution)/shard_map/reduce_scatter | solution.py:157
Sparse Core Ops, SparseCore 0:
  12.3 234.7 all-gather.7
  251.4 227.3 all-gather.5
  481.6 34.5 reduce-scatter.4
  553.8 34.6 reduce-scatter.2
where the time goes:
time: 601 us; the launch traced here: 596 us
  blocking collectives  215 us (36%)
  waiting for transfers between devices  205 us (34%)
  other arithmetic  129 us (21%)
  local copies, waits for them, and re-layouts  22.4 us (4%)
  between operations  13.9 us (2%)
  matrix products  6.96 us (1%)
    all_gather x1, blocking collectives, carried_in(): everything = jax.tree.map(lambda part: lax.all_gather(part, axis), shard)  215 us
    all_gather x2, waiting for transfers between devices, carried_in(): everything = jax.tree.map(lambda part: lax.all_gather(part, axis), shard)  173 us
    select_n x128, other arithmetic, turn(): return jax.tree.map(lambda a, b: jnp.where(reached, a, b), new, before)  125 us
    reduce_scatter x1, waiting for transfers between devices, per_device(): lax.psum_scatter(write_mix.reshape(tokens, states), 'head', scatter_dimen...  32.5 us
    unnamed x9, local copies, waits for them, and re-layouts  20.8 us
  transfers between devices with their start and end apart: 4, of which 3 were waited for; matrix products, arithmetic and copies ran while one was open for 26% of the time, Pallas kernels for 0%

commit v1 on v0

v1 whole, which is shorter than its diff:
```python
import jax
import jax.numpy as jnp
from jax import lax
from jax.sharding import PartitionSpec as P


def scan_exclusive(decay, state, axis, reverse):
    devices, mine = lax.axis_size(axis), lax.axis_index(axis)
    window = jnp.concatenate([decay[None, :], state], axis=0)
    outer_decay = jnp.ones_like(decay)
    outer_state = jnp.zeros_like(state)
    shift = 1
    while shift < devices:
        if reverse:
            pairs = [(i + shift, i) for i in range(devices - shift)]
            valid = mine < devices - shift
        else:
            pairs = [(i, i + shift) for i in range(devices - shift)]
            valid = mine >= shift
        got = lax.ppermute(window, axis, pairs)
        got_decay, got_state = got[0], got[1:]
        outer_state = outer_decay[None, :] * got_state + outer_state
        outer_decay = jnp.where(valid, got_decay * outer_decay, outer_decay)
        shift *= 2
        if shift < devices:
            win_decay, win_state = window[0], window[1:]
            new_state = win_decay[None, :] * got_state + win_state
            new_decay = jnp.where(valid, got_decay * win_decay, win_decay)
            window = jnp.concatenate([new_decay[None, :], new_state], axis=0)
    return outer_state


def heads_scaled(values, factor):
    head_count, length = factor.shape
    shaped = values.astype(jnp.float32).reshape(length, head_count, -1) * factor.T[:, :, None]
    return shaped.astype(jnp.bfloat16).reshape(length, -1)


def per_device(head_inputs, write_keys, read_queries, log_decay, out_grad):
    length, feature_width = head_inputs.shape
    head_count = log_decay.shape[0]
    head_size = feature_width // head_count
    cumulative = jnp.cumsum(log_decay, axis=1)
    block_end = cumulative[:, -1:]
    forward_w = jnp.exp(block_end - cumulative)
    backward_w = jnp.exp(cumulative)
    weighted_inputs = heads_scaled(head_inputs, forward_w)
    weighted_grads = heads_scaled(out_grad, backward_w)
    through = jnp.repeat(jnp.exp(block_end[:, 0]), head_size)
    own_state = jnp.dot(write_keys.T, weighted_inputs, preferred_element_type=jnp.float32)
    own_grad = jnp.dot(read_queries.T, weighted_grads, preferred_element_type=jnp.float32)

    entry = scan_exclusive(through, own_state, "ctx", reverse=False)
    exit_ = scan_exclusive(through, own_grad, "ctx", reverse=True)
    entry_bf = entry.astype(jnp.bfloat16)
    exit_bf = exit_.astype(jnp.bfloat16)

    causal = jnp.arange(length)[:, None] >= jnp.arange(length)[None, :]
    spread = cumulative[:, :, None] - cumulative[:, None, :]
    decay_mat = jnp.exp(jnp.where(causal[None], spread, -jnp.inf))
    scores = jnp.dot(read_queries, write_keys.T, preferred_element_type=jnp.float32)
    mixing = (scores[None] * decay_mat).astype(jnp.bfloat16)
    inputs_heads = head_inputs.reshape(length, head_count, head_size)
    grads_heads = out_grad.reshape(length, head_count, head_size)
    input_mix = jnp.einsum(
        "hts,thp->shp", mixing, grads_heads, preferred_element_type=jnp.float32
    )
    pair_grad = jnp.einsum(
        "thp,shp->hts", grads_heads, inputs_heads, preferred_element_type=jnp.float32
    )
    score_grad = jnp.sum(pair_grad * decay_mat, axis=0)
    write_mix = jnp.dot(
        score_grad.T, read_queries.astype(jnp.float32), precision=lax.Precision.HIGHEST
    )
    read_mix = jnp.dot(
        score_grad, write_keys.astype(jnp.float32), precision=lax.Precision.HIGHEST
    )

    input_state = (
        jnp.dot(write_keys, exit_bf, preferred_element_type=jnp.float32).reshape(
            length, head_count, head_size
        )
        * forward_w.T[:, :, None]
    )
    input_grad = (input_mix + input_state).astype(jnp.bfloat16).reshape(length, feature_width)
    write_state = jnp.dot(weighted_inputs, exit_bf.T, preferred_element_type=jnp.float32)
    read_state = jnp.dot(weighted_grads, entry_bf.T, preferred_element_type=jnp.float32)
    both = jnp.concatenate([write_mix + write_state, read_mix + read_state], axis=1)
    summed = lax.psum_scatter(both, "head", scatter_dimension=0, tiled=True)
    states = write_keys.shape[1]
    write_sum, read_sum = summed[:, :states], summed[:, states:]
    return (input_grad, write_sum.astype(jnp.bfloat16), read_sum.astype(jnp.bfloat16))


def solution(mesh):
    placed = (P("ctx", "head"), P("ctx", None), P("ctx", None), P("head", "ctx"), P("ctx", "head"))
    return jax.shard_map(
        per_device,
        mesh=mesh,
        in_specs=placed,
        out_specs=(P("ctx", "head"), P(("ctx", "head"), None), P(("ctx", "head"), None)),
        check_vma=False,
    )
```

time: 601 us -> 147 us (0.24)
  blocking collectives: 215 us -> 0 us
  waiting for transfers between devices: 205 us -> 59.8 us
  other arithmetic: 129 us -> 1.72 us
  starting transfers between devices: 0.16 us -> 59.3 us
  local copies, waits for them, and re-layouts: 22.4 us -> 6.53 us
    all_gather x1 -> x0, blocking collectives: 215 us -> none  [carried_in(): everything = jax.tree.map(lambda part: lax.all_gather(part, axis), shard)]
    all_gather x2 -> x0, waiting for transfers between devices: 173 us -> none  [carried_in(): everything = jax.tree.map(lambda part: lax.all_gather(part, axis), shard)]
    select_n x128 -> x9, other arithmetic: 125 us -> 0.07 us  [the longest x7 0.04 us: scan_exclusive(): new_decay = jnp.where(valid, got_decay * win_decay, win_decay)]
    ppermute x0 -> x12, starting transfers between devices: none -> 59.3 us  [scan_exclusive(): got = lax.ppermute(window, axis, pairs)]
    unnamed x4 -> x2, waiting for transfers between devices: 0.07 us -> 42.6 us
    reduce_scatter x2 -> x0, waiting for transfers between devices: 32.5 us -> none  [the longest x1 32.5 us: per_device(): lax.psum_scatter(write_mix.reshape(tokens, states), 'head', scatter_dimen...]
    ppermute x0 -> x12, waiting for transfers between devices: none -> 17.2 us  [scan_exclusive(): got = lax.ppermute(window, axis, pairs)]
    unnamed x9 -> x15, local copies, waits for them, and re-layouts: 20.8 us -> 5.99 us
  transfers between devices with their start and end apart: 4 -> 13, of which waited for: 3 -> 9; matrix products, arithmetic and copies ran while one was open for 26% -> 2% of each run, Pallas kernels for 0% -> 0%
where the time goes in v1:
time: 147 us; the launch traced here: 144 us
  waiting for transfers between devices  59.8 us (41%)
  starting transfers between devices  59.3 us (40%)
  between operations  14.5 us (10%)
  local copies, waits for them, and re-layouts  6.53 us (4%)
  matrix products  2.25 us (2%)
  other arithmetic  1.72 us (1%)
    ppermute x12, starting transfers between devices, scan_exclusive(): got = lax.ppermute(window, axis, pairs)  59.3 us
    unnamed x2, waiting for transfers between devices  42.6 us
    ppermute x12, waiting for transfers between devices, scan_exclusive(): got = lax.ppermute(window, axis, pairs)  17.2 us
    unnamed x15, local copies, waits for them, and re-layouts  5.99 us
  transfers between devices with their start and end apart: 13, of which 9 were waited for; matrix products, arithmetic and copies ran while one was open for 2% of the time, Pallas kernels for 0%

profile of v1, /device:TPU:1, one launch (start us, length us, event | category | flops | bytes accessed | tf_op | source)
XLA Modules:
  0.0 144.1 jit_solution(573883299172494004)
XLA Ops:
  7.2 1.0 reduce_window_sum.11
  8.6 0.7 copy-done.3
  9.6 0.7 copy-done.2
  10.6 0.6 copy-done.1
  11.5 1.3 collective-permute-start
  12.7 12.1 %collective-permute-start.6 = (f32[129,256]{1,0:T(8,128)S(1)}, f32[129,256]{1,0:T(8,128)S(1)}, u32[]{:S(2)}, u32[]{:S(2)}) collective-permute-start(f32[129,256]{1,0:T(8,128)S(1)} %get-tuple-element.32), channel_id=1, source_target_pairs={{0,8},{8,16},{16,24},{24,32},{32,40},{40,48},{48,56},{56,64},{64,7... | collective-permute-start | bytes 396296 | tf_op jit(solution)/shard_map/ppermute | solution.py:20
  25.1 0.3 fusion
  25.9 10.1 %collective-permute-done.6 = f32[129,256]{1,0:T(8,128)S(1)} collective-permute-done((f32[129,256]{1,0:T(8,128)S(1)}, f32[129,256]{1,0:T(8,128)S(1)}, u32[]{:S(2)}, u32[]{:S(2)}) %collective-permute-start.6) | collective-permute-done | bytes 132128 | tf_op jit(solution)/shard_map/ppermute | solution.py:20
  36.1 1.3 collective-permute-start.1
  37.6 4.2 %collective-permute-start.7 = (f32[129,256]{1,0:T(8,128)S(1)}, f32[129,256]{1,0:T(8,128)S(1)}, u32[]{:S(2)}, u32[]{:S(2)}) collective-permute-start(f32[129,256]{1,0:T(8,128)S(1)} %pad_maximum_fusion.7), channel_id=1, source_target_pairs={{0,16},{8,24},{16,32},{24,40},{32,48},{40,56},{48,64},{56,72},{64,... | collective-permute-start | bytes 396296 | tf_op jit(solution)/shard_map/ppermute | solution.py:20
  41.9 0.3 collective-permute-done.1
  42.2 1.3 collective-permute-start.2
  43.5 0.3 collective-permute-done.7
  43.9 10.4 %collective-permute-start.8 = (f32[129,256]{1,0:T(8,128)S(1)}, f32[129,256]{1,0:T(8,128)S(1)}, u32[]{:S(2)}, u32[]{:S(2)}) collective-permute-start(f32[129,256]{1,0:T(8,128)S(1)} %pad_maximum_fusion.8), channel_id=1, source_target_pairs={{0,32},{8,40},{16,48},{24,56},{32,64},{40,72},{48,80},{56,88},{64,... | collective-permute-start | bytes 396296 | tf_op jit(solution)/shard_map/ppermute | solution.py:20
  54.3 0.3 collective-permute-done.2
  54.7 1.3 collective-permute-start.3
  56.0 3.1 %collective-permute-done.8 = f32[129,256]{1,0:T(8,128)S(1)} collective-permute-done((f32[129,256]{1,0:T(8,128)S(1)}, f32[129,256]{1,0:T(8,128)S(1)}, u32[]{:S(2)}, u32[]{:S(2)}) %collective-permute-start.8) | collective-permute-done | bytes 132128 | tf_op jit(solution)/shard_map/ppermute | solution.py:20
  59.2 6.4 %collective-permute-start.9 = (f32[129,256]{1,0:T(8,128)S(1)}, f32[129,256]{1,0:T(8,128)S(1)}, u32[]{:S(2)}, u32[]{:S(2)}) collective-permute-start(f32[129,256]{1,0:T(8,128)S(1)} %pad_maximum_fusion.9), channel_id=1, source_target_pairs={{0,64},{8,72},{16,80},{24,88},{32,96},{40,104},{48,112},{56,120},{... | collective-permute-start | bytes 396296 | tf_op jit(solution)/shard_map/ppermute | solution.py:20
  65.6 1.3 collective-permute-start.4
  66.9 0.6 collective-permute-done.9
  67.6 4.8 %collective-permute-start.10 = (f32[129,256]{1,0:T(8,128)S(1)}, f32[129,256]{1,0:T(8,128)S(1)}, u32[]{:S(2)}, u32[]{:S(2)}) collective-permute-start(f32[129,256]{1,0:T(8,128)S(1)} %pad_maximum_fusion.10), channel_id=1, source_target_pairs={{0,128},{8,136},{16,144},{24,152},{32,160},{40,168},{48,176},{56,1... | collective-permute-start | bytes 396296 | tf_op jit(solution)/shard_map/ppermute | solution.py:20
  72.5 1.3 collective-permute-start.5
  73.8 0.6 collective-permute-done.10
  74.5 13.6 %collective-permute-start.11 = (f32[129,256]{1,0:T(8,128)S(1)}, f32[129,256]{1,0:T(8,128)S(1)}, u32[]{:S(2)}, u32[]{:S(2)}) collective-permute-start(f32[129,256]{1,0:T(8,128)S(1)} %pad_maximum_fusion.11), channel_id=1, source_target_pairs={{0,256},{8,264},{16,272},{24,280},{32,288},{40,296},{48,304},{56,3... | collective-permute-start | bytes 396296 | tf_op jit(solution)/shard_map/ppermute | solution.py:20
  88.5 1.7 %collective-permute-done.11 = f32[129,256]{1,0:T(8,128)S(1)} collective-permute-done((f32[129,256]{1,0:T(8,128)S(1)}, f32[129,256]{1,0:T(8,128)S(1)}, u32[]{:S(2)}, u32[]{:S(2)}) %collective-permute-start.11) | collective-permute-done | bytes 132128 | tf_op jit(solution)/shard_map/ppermute | solution.py:20
  90.4 0.8 copy.30
  91.4 0.3 fusion.2
  91.7 0.7 copy.27
  92.5 42.6 %reduce-scatter.4.cloned.1.call-done = f32[16,256]{1,0:T(8,128)} async-done(((f32[128,256]{1,0:T(8,128)}), f32[16,256]{1,0:T(8,128)}) %reduce-scatter.4.cloned.1.call-update) | async-done | bytes 16400
  135.1 0.8 copy.31
  135.9 0.7 copy.28
  136.6 0.7 copy.29
  (63 shorter events, 3.2 us)
Async XLA Ops:
  7.2 3.4 %copy-start = (bf16[128,128]{1,0:T(8,128)(2,1)S(1)}, bf16[128,128]{1,0:T(8,128)(2,1)}, u32[]{:S(2)}) copy-start(bf16[128,128]{1,0:T(8,128)(2,1)} %param.6) | copy-start | bytes 98308
  7.2 127.9 %reduce-scatter.4.cloned.1.call-start = ((), (), s32[]{:S(2)}) async-start(), calls=%async_computation.1 | async-start | bytes 147456
  8.5 0.8 copy-start.3
  9.6 0.8 copy-start.2
  10.4 0.8 copy-start.1
  11.5 14.5 %collective-permute-start = (f32[129,256]{1,0:T(8,128)S(1)}, f32[129,256]{1,0:T(8,128)S(1)}, u32[]{:S(2)}, u32[]{:S(2)}) collective-permute-start(f32[129,256]{1,0:T(8,128)S(1)} %get-tuple-element.33), channel_id=1, source_target_pairs={{8,0},{16,8},{24,16},{32,24},{40,32},{48,40},{56,48},{64,56},{72,6... | collective-permute-start | bytes 396296 | tf_op jit(solution)/shard_map/ppermute | solution.py:20
  12.7 23.3 %collective-permute-start.6 = (f32[129,256]{1,0:T(8,128)S(1)}, f32[129,256]{1,0:T(8,128)S(1)}, u32[]{:S(2)}, u32[]{:S(2)}) collective-permute-start(f32[129,256]{1,0:T(8,128)S(1)} %get-tuple-element.32), channel_id=1, source_target_pairs={{0,8},{8,16},{16,24},{24,32},{32,40},{40,48},{48,56},{56,64},{64,7... | collective-permute-start | bytes 396296 | tf_op jit(solution)/shard_map/ppermute | solution.py:20
  36.1 6.0 %collective-permute-start.1 = (f32[129,256]{1,0:T(8,128)S(1)}, f32[129,256]{1,0:T(8,128)S(1)}, u32[]{:S(2)}, u32[]{:S(2)}) collective-permute-start(f32[129,256]{1,0:T(8,128)S(1)} %pad_maximum_fusion.2), channel_id=1, source_target_pairs={{16,0},{24,8},{32,16},{40,24},{48,32},{56,40},{64,48},{72,56},{80,... | collective-permute-start | bytes 396296 | tf_op jit(solution)/shard_map/ppermute | solution.py:20
  37.6 6.2 %collective-permute-start.7 = (f32[129,256]{1,0:T(8,128)S(1)}, f32[129,256]{1,0:T(8,128)S(1)}, u32[]{:S(2)}, u32[]{:S(2)}) collective-permute-start(f32[129,256]{1,0:T(8,128)S(1)} %pad_maximum_fusion.7), channel_id=1, source_target_pairs={{0,16},{8,24},{16,32},{24,40},{32,48},{40,56},{48,64},{56,72},{64,... | collective-permute-start | bytes 396296 | tf_op jit(solution)/shard_map/ppermute | solution.py:20
  42.2 12.4 %collective-permute-start.2 = (f32[129,256]{1,0:T(8,128)S(1)}, f32[129,256]{1,0:T(8,128)S(1)}, u32[]{:S(2)}, u32[]{:S(2)}) collective-permute-start(f32[129,256]{1,0:T(8,128)S(1)} %pad_maximum_fusion.3), channel_id=1, source_target_pairs={{32,0},{40,8},{48,16},{56,24},{64,32},{72,40},{80,48},{88,56},{96,... | collective-permute-start | bytes 396296 | tf_op jit(solution)/shard_map/ppermute | solution.py:20
  43.9 15.2 %collective-permute-start.8 = (f32[129,256]{1,0:T(8,128)S(1)}, f32[129,256]{1,0:T(8,128)S(1)}, u32[]{:S(2)}, u32[]{:S(2)}) collective-permute-start(f32[129,256]{1,0:T(8,128)S(1)} %pad_maximum_fusion.8), channel_id=1, source_target_pairs={{0,32},{8,40},{16,48},{24,56},{32,64},{40,72},{48,80},{56,88},{64,... | collective-permute-start | bytes 396296 | tf_op jit(solution)/shard_map/ppermute | solution.py:20
  54.7 10.9 %collective-permute-start.3 = (f32[129,256]{1,0:T(8,128)S(1)}, f32[129,256]{1,0:T(8,128)S(1)}, u32[]{:S(2)}, u32[]{:S(2)}) collective-permute-start(f32[129,256]{1,0:T(8,128)S(1)} %pad_maximum_fusion.4), channel_id=1, source_target_pairs={{64,0},{72,8},{80,16},{88,24},{96,32},{104,40},{112,48},{120,56},{... | collective-permute-start | bytes 396296 | tf_op jit(solution)/shard_map/ppermute | solution.py:20
  59.2 8.4 %collective-permute-start.9 = (f32[129,256]{1,0:T(8,128)S(1)}, f32[129,256]{1,0:T(8,128)S(1)}, u32[]{:S(2)}, u32[]{:S(2)}) collective-permute-start(f32[129,256]{1,0:T(8,128)S(1)} %pad_maximum_fusion.9), channel_id=1, source_target_pairs={{0,64},{8,72},{16,80},{24,88},{32,96},{40,104},{48,112},{56,120},{... | collective-permute-start | bytes 396296 | tf_op jit(solution)/shard_map/ppermute | solution.py:20
  65.6 6.8 %collective-permute-start.4 = (f32[129,256]{1,0:T(8,128)S(1)}, f32[129,256]{1,0:T(8,128)S(1)}, u32[]{:S(2)}, u32[]{:S(2)}) collective-permute-start(f32[129,256]{1,0:T(8,128)S(1)} %pad_maximum_fusion.5), channel_id=1, source_target_pairs={{128,0},{136,8},{144,16},{152,24},{160,32},{168,40},{176,48},{184,... | collective-permute-start | bytes 396296 | tf_op jit(solution)/shard_map/ppermute | solution.py:20
  67.6 6.8 %collective-permute-start.10 = (f32[129,256]{1,0:T(8,128)S(1)}, f32[129,256]{1,0:T(8,128)S(1)}, u32[]{:S(2)}, u32[]{:S(2)}) collective-permute-start(f32[129,256]{1,0:T(8,128)S(1)} %pad_maximum_fusion.10), channel_id=1, source_target_pairs={{0,128},{8,136},{16,144},{24,152},{32,160},{40,168},{48,176},{56,1... | collective-permute-start | bytes 396296 | tf_op jit(solution)/shard_map/ppermute | solution.py:20
  72.5 15.6 %collective-permute-start.5 = (f32[129,256]{1,0:T(8,128)S(1)}, f32[129,256]{1,0:T(8,128)S(1)}, u32[]{:S(2)}, u32[]{:S(2)}) collective-permute-start(f32[129,256]{1,0:T(8,128)S(1)} %pad_maximum_fusion.6), channel_id=1, source_target_pairs={{256,0},{264,8},{272,16},{280,24},{288,32},{296,40},{304,48},{312,... | collective-permute-start | bytes 396296 | tf_op jit(solution)/shard_map/ppermute | solution.py:20
  74.5 15.6 %collective-permute-start.11 = (f32[129,256]{1,0:T(8,128)S(1)}, f32[129,256]{1,0:T(8,128)S(1)}, u32[]{:S(2)}, u32[]{:S(2)}) collective-permute-start(f32[129,256]{1,0:T(8,128)S(1)} %pad_maximum_fusion.11), channel_id=1, source_target_pairs={{0,256},{8,264},{16,272},{24,280},{32,288},{40,296},{48,304},{56,3... | collective-permute-start | bytes 396296 | tf_op jit(solution)/shard_map/ppermute | solution.py:20
Sparse Core Ops, SparseCore 0:
  91.3 43.7 reduce-scatter.3

commit v2 on v1

--- a/solution.py
+++ b/solution.py
@@ -4,30 +4,56 @@
 from jax.sharding import PartitionSpec as P
 
 
-def scan_exclusive(decay, state, axis, reverse):
+def scan_both(decay, state, grad, axis):
     devices, mine = lax.axis_size(axis), lax.axis_index(axis)
-    window = jnp.concatenate([decay[None, :], state], axis=0)
-    outer_decay = jnp.ones_like(decay)
-    outer_state = jnp.zeros_like(state)
+    block_decay, block_state, block_grad = decay, state, grad
+    prefix_decay, prefix_state = jnp.ones_like(decay), jnp.zeros_like(state)
+    suffix_decay, suffix_grad = jnp.ones_like(decay), jnp.zeros_like(grad)
+    rows = state.shape[0]
     shift = 1
     while shift < devices:
-        if reverse:
-            pairs = [(i + shift, i) for i in range(devices - shift)]
-            valid = mine < devices - shift
-        else:
-            pairs = [(i, i + shift) for i in range(devices - shift)]
-            valid = mine >= shift
-        got = lax.ppermute(window, axis, pairs)
-        got_decay, got_state = got[0], got[1:]
-        outer_state = outer_decay[None, :] * got_state + outer_state
-        outer_decay = jnp.where(valid, got_decay * outer_decay, outer_decay)
+        pairs = [(i, i ^ shift) for i in range(devices)]
+        message = jnp.concatenate([block_decay[None, :], block_state, block_grad], axis=0)
+        got = lax.ppermute(message, axis, pairs)
+        got_decay, got_state, got_grad = got[0], got[1 : rows + 1], got[rows + 1 :]
+        later = (mine & shift) != 0
+        prefix_state = jnp.where(later, prefix_decay[None, :] * got_state + prefix_state, prefix_state)
+        prefix_decay = jnp.where(later, got_decay * prefix_decay, prefix_decay)
+        suffix_grad = jnp.where(later, suffix_grad, suffix_decay[None, :] * got_grad + suffix_grad)
+        suffix_decay = jnp.where(later, suffix_decay, got_decay * suffix_decay)
         shift *= 2
         if shift < devices:
-            win_decay, win_state = window[0], window[1:]
-            new_state = win_decay[None, :] * got_state + win_state
-            new_decay = jnp.where(valid, got_decay * win_decay, win_decay)
-            window = jnp.concatenate([new_decay[None, :], new_state], axis=0)
-    return outer_state
+            block_state = jnp.where(
+                later,
+                block_decay[None, :] * got_state + block_state,
+                got_decay[None, :] * block_state + got_state,
+            )
+            block_grad = jnp.where(
+                later,
+                got_decay[None, :] * block_grad + got_grad,
+                block_decay[None, :] * got_grad + block_grad,
+            )
+            block_decay = got_decay * block_decay
+    return prefix_state, suffix_grad
+
+
+def scatter_sum(values, axis):
+    devices, mine = lax.axis_size(axis), lax.axis_index(axis)
+    bits = devices.bit_length() - 1
+    rows, cols = values.shape
+    piece = rows // devices
+    x = values.reshape((2,) * bits + (piece, cols))
+    x = x.transpose(tuple(range(bits - 1, -1, -1)) + (bits, bits + 1)).reshape(rows, cols)
+    shift = 1
+    while shift < devices:
+        half = x.shape[0] // 2
+        upper = (mine & shift) != 0
+        keep = jnp.where(upper, x[half:], x[:half])
+        send = jnp.where(upper, x[:half], x[half:])
+        got = lax.ppermute(send, axis, [(i, i ^ shift) for i in range(devices)])
+        x = keep + got
+        shift *= 2
+    return x
 
 
 def heads_scaled(values, factor):
@@ -50,8 +76,7 @@
     own_state = jnp.dot(write_keys.T, weighted_inputs, preferred_element_type=jnp.float32)
     own_grad = jnp.dot(read_queries.T, weighted_grads, preferred_element_type=jnp.float32)
 
-    entry = scan_exclusive(through, own_state, "ctx", reverse=False)
-    exit_ = scan_exclusive(through, own_grad, "ctx", reverse=True)
+    entry, exit_ = scan_both(through, own_state, own_grad, "ctx")
     entry_bf = entry.astype(jnp.bfloat16)
     exit_bf = exit_.astype(jnp.bfloat16)
 
@@ -86,7 +111,7 @@
     write_state = jnp.dot(weighted_inputs, exit_bf.T, preferred_element_type=jnp.float32)
     read_state = jnp.dot(weighted_grads, entry_bf.T, preferred_element_type=jnp.float32)
     both = jnp.concatenate([write_mix + write_state, read_mix + read_state], axis=1)
-    summed = lax.psum_scatter(both, "head", scatter_dimension=0, tiled=True)
+    summed = scatter_sum(both, "head")
     states = write_keys.shape[1]
     write_sum, read_sum = summed[:, :states], summed[:, states:]
     return (input_grad, write_sum.astype(jnp.bfloat16), read_sum.astype(jnp.bfloat16))

time: 147 us -> 109 us (0.74)
  waiting for transfers between devices: 59.8 us -> 37.4 us
  between operations: 14.5 us -> 1 us
  local copies, waits for them, and re-layouts: 6.53 us -> 4.32 us
    unnamed x2 -> x0, waiting for transfers between devices: 42.6 us -> none
    ppermute x12 -> x9, waiting for transfers between devices: 17.2 us -> 37.4 us  [the longest x6 35.6 us: scan_both(): got = lax.ppermute(message, axis, pairs)]
    unnamed x15 -> x11, local copies, waits for them, and re-layouts: 5.99 us -> 3.06 us
    ppermute x12 -> x9, starting transfers between devices: 59.3 us -> 60.4 us  [the longest x6 35.8 us: scan_both(): got = lax.ppermute(message, axis, pairs)]
  transfers between devices with their start and end apart: 13 -> 9, of which waited for: 9 -> 8; matrix products, arithmetic and copies ran while one was open for 2% -> 2% of each run, Pallas kernels for 0% -> 0%
where the time goes in v2:
time: 109 us; the launch traced here: 107 us
  starting transfers between devices  60.4 us (55%)
  waiting for transfers between devices  37.4 us (34%)
  local copies, waits for them, and re-layouts  4.32 us (4%)
  matrix products  2.27 us (2%)
  other arithmetic  1.8 us (2%)
    ppermute x6, starting transfers between devices, scan_both(): got = lax.ppermute(message, axis, pairs)  35.8 us
    ppermute x6, waiting for transfers between devices, scan_both(): got = lax.ppermute(message, axis, pairs)  35.6 us
    ppermute x3, starting transfers between devices, scatter_sum(): got = lax.ppermute(send, axis, [(i, i ^ shift) for i in range(devices)])  24.7 us
    unnamed x11, local copies, waits for them, and re-layouts  3.06 us
  transfers between devices with their start and end apart: 9, of which 8 were waited for; matrix products, arithmetic and copies ran while one was open for 2% of the time, Pallas kernels for 0%

profile of v2, /device:TPU:1, one launch (start us, length us, event | category | flops | bytes accessed | tf_op | source)
XLA Modules:
  0.0 107.3 jit_solution(10171070863486744825)
XLA Ops:
  0.6 1.0 reduce_window_sum.11
  1.6 0.2 slice_reduce_fusion
  2.0 0.7 copy-done.3
  3.0 0.7 copy-done.2
  3.8 0.2 convolution_bitcast_fusion.1
  4.0 0.6 copy-done.1
  4.6 0.2 convolution_bitcast_fusion.2
  4.9 11.5 %collective-permute-start = (f32[257,256]{1,0:T(8,128)S(1)}, f32[257,256]{1,0:T(8,128)S(1)}, u32[]{:S(2)}, u32[]{:S(2)}) collective-permute-start(f32[257,256]{1,0:T(8,128)S(1)} %pad_maximum_fusion), channel_id=1, source_target_pairs={{0,8},{8,0},{16,24},{24,16},{32,40},{40,32},{48,56},{56,48},{64,72... | collective-permute-start | bytes 789512 | tf_op jit(solution)/shard_map/ppermute | solution.py:17
  16.4 5.3 %collective-permute-done = f32[257,256]{1,0:T(8,128)S(1)} collective-permute-done((f32[257,256]{1,0:T(8,128)S(1)}, f32[257,256]{1,0:T(8,128)S(1)}, u32[]{:S(2)}, u32[]{:S(2)}) %collective-permute-start) | collective-permute-done | bytes 263200 | tf_op jit(solution)/shard_map/ppermute | solution.py:17
  21.9 3.9 %collective-permute-start.1 = (f32[257,256]{1,0:T(8,128)S(1)}, f32[257,256]{1,0:T(8,128)S(1)}, u32[]{:S(2)}, u32[]{:S(2)}) collective-permute-start(f32[257,256]{1,0:T(8,128)S(1)} %pad_maximum_fusion.1), channel_id=1, source_target_pairs={{0,16},{8,24},{16,0},{24,8},{32,48},{40,56},{48,32},{56,40},{64,80... | collective-permute-start | bytes 789512 | tf_op jit(solution)/shard_map/ppermute | solution.py:17
  25.8 4.7 %collective-permute-done.1 = f32[257,256]{1,0:T(8,128)S(1)} collective-permute-done((f32[257,256]{1,0:T(8,128)S(1)}, f32[257,256]{1,0:T(8,128)S(1)}, u32[]{:S(2)}, u32[]{:S(2)}) %collective-permute-start.1) | collective-permute-done | bytes 263200 | tf_op jit(solution)/shard_map/ppermute | solution.py:17
  30.6 5.3 %collective-permute-start.2 = (f32[257,256]{1,0:T(8,128)S(1)}, f32[257,256]{1,0:T(8,128)S(1)}, u32[]{:S(2)}, u32[]{:S(2)}) collective-permute-start(f32[257,256]{1,0:T(8,128)S(1)} %pad_maximum_fusion.2), channel_id=1, source_target_pairs={{0,32},{8,40},{16,48},{24,56},{32,0},{40,8},{48,16},{56,24},{64,96... | collective-permute-start | bytes 789512 | tf_op jit(solution)/shard_map/ppermute | solution.py:17
  35.9 4.2 %collective-permute-done.2 = f32[257,256]{1,0:T(8,128)S(1)} collective-permute-done((f32[257,256]{1,0:T(8,128)S(1)}, f32[257,256]{1,0:T(8,128)S(1)}, u32[]{:S(2)}, u32[]{:S(2)}) %collective-permute-start.2) | collective-permute-done | bytes 263200 | tf_op jit(solution)/shard_map/ppermute | solution.py:17
  40.2 3.4 %collective-permute-start.3 = (f32[257,256]{1,0:T(8,128)S(1)}, f32[257,256]{1,0:T(8,128)S(1)}, u32[]{:S(2)}, u32[]{:S(2)}) collective-permute-start(f32[257,256]{1,0:T(8,128)S(1)} %pad_maximum_fusion.3), channel_id=1, source_target_pairs={{0,64},{8,72},{16,80},{24,88},{32,96},{40,104},{48,112},{56,120},{... | collective-permute-start | bytes 789512 | tf_op jit(solution)/shard_map/ppermute | solution.py:17
  43.6 3.8 %collective-permute-done.3 = f32[257,256]{1,0:T(8,128)S(1)} collective-permute-done((f32[257,256]{1,0:T(8,128)S(1)}, f32[257,256]{1,0:T(8,128)S(1)}, u32[]{:S(2)}, u32[]{:S(2)}) %collective-permute-start.3) | collective-permute-done | bytes 263200 | tf_op jit(solution)/shard_map/ppermute | solution.py:17
  47.6 4.4 %collective-permute-start.4 = (f32[257,256]{1,0:T(8,128)S(1)}, f32[257,256]{1,0:T(8,128)S(1)}, u32[]{:S(2)}, u32[]{:S(2)}) collective-permute-start(f32[257,256]{1,0:T(8,128)S(1)} %pad_maximum_fusion.4), channel_id=1, source_target_pairs={{0,128},{8,136},{16,144},{24,152},{32,160},{40,168},{48,176},{56,1... | collective-permute-start | bytes 789512 | tf_op jit(solution)/shard_map/ppermute | solution.py:17
  52.1 0.3 fusion
  52.5 10.5 %collective-permute-done.4 = f32[257,256]{1,0:T(8,128)S(1)} collective-permute-done((f32[257,256]{1,0:T(8,128)S(1)}, f32[257,256]{1,0:T(8,128)S(1)}, u32[]{:S(2)}, u32[]{:S(2)}) %collective-permute-start.4) | collective-permute-done | bytes 263200 | tf_op jit(solution)/shard_map/ppermute | solution.py:17
  63.1 7.3 %collective-permute-start.5 = (f32[257,256]{1,0:T(8,128)S(1)}, f32[257,256]{1,0:T(8,128)S(1)}, u32[]{:S(2)}, u32[]{:S(2)}) collective-permute-start(f32[257,256]{1,0:T(8,128)S(1)} %pad_maximum_fusion.5), channel_id=1, source_target_pairs={{0,256},{8,264},{16,272},{24,280},{32,288},{40,296},{48,304},{56,3... | collective-permute-start | bytes 789512 | tf_op jit(solution)/shard_map/ppermute | solution.py:17
  70.4 0.2 fusion.23
  70.7 0.2 fusion.24
  70.9 7.0 %collective-permute-done.5 = f32[257,256]{1,0:T(8,128)S(1)} collective-permute-done((f32[257,256]{1,0:T(8,128)S(1)}, f32[257,256]{1,0:T(8,128)S(1)}, u32[]{:S(2)}, u32[]{:S(2)}) %collective-permute-start.5) | collective-permute-done | bytes 263200 | tf_op jit(solution)/shard_map/ppermute | solution.py:17
  78.2 0.3 convolution_add_fusion
  78.7 7.7 %collective-permute-start.6 = (f32[64,256]{1,0:T(8,128)S(1)}, f32[64,256]{1,0:T(8,128)S(1)}, u32[]{:S(2)}, u32[]{:S(2)}) collective-permute-start(f32[64,256]{1,0:T(8,128)S(1)} %bitcast.71), channel_id=1, source_target_pairs={{0,1},{1,0},{2,3},{3,2},{4,5},{5,4},{6,7},{7,6},{8,9},{9,8},{10,11... | collective-permute-start | bytes 196616 | tf_op jit(solution)/shard_map/ppermute | solution.py:53
  86.5 0.7 collective-permute-done.6
  87.2 8.9 %collective-permute-start.7 = (f32[32,256]{1,0:T(8,128)S(1)}, f32[32,256]{1,0:T(8,128)S(1)}, u32[]{:S(2)}, u32[]{:S(2)}) collective-permute-start(f32[32,256]{1,0:T(8,128)S(1)} %slice_select_fusion.2), channel_id=1, source_target_pairs={{0,2},{1,3},{2,0},{3,1},{4,6},{5,7},{6,4},{7,5},{8,10},{9,11},{10,... | collective-permute-start | bytes 98312 | tf_op jit(solution)/shard_map/ppermute | solution.py:53
  96.1 0.2 fusion.22
  96.3 1.1 %collective-permute-done.7 = f32[32,256]{1,0:T(8,128)S(1)} collective-permute-done((f32[32,256]{1,0:T(8,128)S(1)}, f32[32,256]{1,0:T(8,128)S(1)}, u32[]{:S(2)}, u32[]{:S(2)}) %collective-permute-start.7) | collective-permute-done | bytes 32800 | tf_op jit(solution)/shard_map/ppermute | solution.py:53
  97.4 8.1 %collective-permute-start.8 = (f32[16,256]{1,0:T(8,128)S(1)}, f32[16,256]{1,0:T(8,128)S(1)}, u32[]{:S(2)}, u32[]{:S(2)}) collective-permute-start(f32[16,256]{1,0:T(8,128)S(1)} %slice_select_fusion.3), channel_id=1, source_target_pairs={{0,4},{1,5},{2,6},{3,7},{4,0},{5,1},{6,2},{7,3},{8,12},{9,13},{10,... | collective-permute-start | bytes 49160 | tf_op jit(solution)/shard_map/ppermute | solution.py:53
  105.5 0.3 fusion.2
  105.9 0.7 copy.29
  106.7 0.6 fusion.20
  (46 shorter events, 1.9 us)
Async XLA Ops:
  0.6 3.4 %copy-start = (bf16[128,128]{1,0:T(8,128)(2,1)S(1)}, bf16[128,128]{1,0:T(8,128)(2,1)}, u32[]{:S(2)}) copy-start(bf16[128,128]{1,0:T(8,128)(2,1)} %param.6) | copy-start | bytes 98308
  1.9 0.8 copy-start.3
  3.0 0.8 copy-start.2
  3.8 0.8 copy-start.1
  4.9 16.9 %collective-permute-start = (f32[257,256]{1,0:T(8,128)S(1)}, f32[257,256]{1,0:T(8,128)S(1)}, u32[]{:S(2)}, u32[]{:S(2)}) collective-permute-start(f32[257,256]{1,0:T(8,128)S(1)} %pad_maximum_fusion), channel_id=1, source_target_pairs={{0,8},{8,0},{16,24},{24,16},{32,40},{40,32},{48,56},{56,48},{64,72... | collective-permute-start | bytes 789512 | tf_op jit(solution)/shard_map/ppermute | solution.py:17
  21.9 8.6 %collective-permute-start.1 = (f32[257,256]{1,0:T(8,128)S(1)}, f32[257,256]{1,0:T(8,128)S(1)}, u32[]{:S(2)}, u32[]{:S(2)}) collective-permute-start(f32[257,256]{1,0:T(8,128)S(1)} %pad_maximum_fusion.1), channel_id=1, source_target_pairs={{0,16},{8,24},{16,0},{24,8},{32,48},{40,56},{48,32},{56,40},{64,80... | collective-permute-start | bytes 789512 | tf_op jit(solution)/shard_map/ppermute | solution.py:17
  30.6 9.6 %collective-permute-start.2 = (f32[257,256]{1,0:T(8,128)S(1)}, f32[257,256]{1,0:T(8,128)S(1)}, u32[]{:S(2)}, u32[]{:S(2)}) collective-permute-start(f32[257,256]{1,0:T(8,128)S(1)} %pad_maximum_fusion.2), channel_id=1, source_target_pairs={{0,32},{8,40},{16,48},{24,56},{32,0},{40,8},{48,16},{56,24},{64,96... | collective-permute-start | bytes 789512 | tf_op jit(solution)/shard_map/ppermute | solution.py:17
  40.2 7.2 %collective-permute-start.3 = (f32[257,256]{1,0:T(8,128)S(1)}, f32[257,256]{1,0:T(8,128)S(1)}, u32[]{:S(2)}, u32[]{:S(2)}) collective-permute-start(f32[257,256]{1,0:T(8,128)S(1)} %pad_maximum_fusion.3), channel_id=1, source_target_pairs={{0,64},{8,72},{16,80},{24,88},{32,96},{40,104},{48,112},{56,120},{... | collective-permute-start | bytes 789512 | tf_op jit(solution)/shard_map/ppermute | solution.py:17
  47.6 15.4 %collective-permute-start.4 = (f32[257,256]{1,0:T(8,128)S(1)}, f32[257,256]{1,0:T(8,128)S(1)}, u32[]{:S(2)}, u32[]{:S(2)}) collective-permute-start(f32[257,256]{1,0:T(8,128)S(1)} %pad_maximum_fusion.4), channel_id=1, source_target_pairs={{0,128},{8,136},{16,144},{24,152},{32,160},{40,168},{48,176},{56,1... | collective-permute-start | bytes 789512 | tf_op jit(solution)/shard_map/ppermute | solution.py:17
  63.1 14.8 %collective-permute-start.5 = (f32[257,256]{1,0:T(8,128)S(1)}, f32[257,256]{1,0:T(8,128)S(1)}, u32[]{:S(2)}, u32[]{:S(2)}) collective-permute-start(f32[257,256]{1,0:T(8,128)S(1)} %pad_maximum_fusion.5), channel_id=1, source_target_pairs={{0,256},{8,264},{16,272},{24,280},{32,288},{40,296},{48,304},{56,3... | collective-permute-start | bytes 789512 | tf_op jit(solution)/shard_map/ppermute | solution.py:17
  78.7 8.5 %collective-permute-start.6 = (f32[64,256]{1,0:T(8,128)S(1)}, f32[64,256]{1,0:T(8,128)S(1)}, u32[]{:S(2)}, u32[]{:S(2)}) collective-permute-start(f32[64,256]{1,0:T(8,128)S(1)} %bitcast.71), channel_id=1, source_target_pairs={{0,1},{1,0},{2,3},{3,2},{4,5},{5,4},{6,7},{7,6},{8,9},{9,8},{10,11... | collective-permute-start | bytes 196616 | tf_op jit(solution)/shard_map/ppermute | solution.py:53
  87.2 10.2 %collective-permute-start.7 = (f32[32,256]{1,0:T(8,128)S(1)}, f32[32,256]{1,0:T(8,128)S(1)}, u32[]{:S(2)}, u32[]{:S(2)}) collective-permute-start(f32[32,256]{1,0:T(8,128)S(1)} %slice_select_fusion.2), channel_id=1, source_target_pairs={{0,2},{1,3},{2,0},{3,1},{4,6},{5,7},{6,4},{7,5},{8,10},{9,11},{10,... | collective-permute-start | bytes 98312 | tf_op jit(solution)/shard_map/ppermute | solution.py:53
  97.4 9.3 %collective-permute-start.8 = (f32[16,256]{1,0:T(8,128)S(1)}, f32[16,256]{1,0:T(8,128)S(1)}, u32[]{:S(2)}, u32[]{:S(2)}) collective-permute-start(f32[16,256]{1,0:T(8,128)S(1)} %slice_select_fusion.3), channel_id=1, source_target_pairs={{0,4},{1,5},{2,6},{3,7},{4,0},{5,1},{6,2},{7,3},{8,12},{9,13},{10,... | collective-permute-start | bytes 49160 | tf_op jit(solution)/shard_map/ppermute | solution.py:53

commit v3 on v1

v3 whole, which is shorter than its diff:
```python
import functools

import jax
import jax.numpy as jnp
from jax import lax
from jax.sharding import PartitionSpec as P


def joined(earlier, later):
    a1, s1, g1 = earlier
    a2, s2, g2 = later
    return (a1 * a2, a2[None, :] * s1 + s2, a1[None, :] * g2 + g1)


def chosen(flag, yes, no):
    return tuple(jnp.where(flag, y, n) for y, n in zip(yes, no))


def scan_groups(decay, state, grad, axes):
    rows = state.shape[0]
    identity = (jnp.ones_like(decay), jnp.zeros_like(state), jnp.zeros_like(grad))
    block = (decay, state, grad)
    prefix, suffix = identity, identity
    for at, axis in enumerate(axes):
        size, mine = lax.axis_size(axis), lax.axis_index(axis)
        message = jnp.concatenate([block[0][None, :], block[1], block[2]], axis=0)
        spread = jnp.broadcast_to(message[None], (size,) + message.shape)
        got = lax.all_to_all(spread, axis, 0, 0)
        before, after, total = identity, identity, identity
        for member in range(size):
            piece = (got[member, 0], got[member, 1 : rows + 1], got[member, rows + 1 :])
            before = chosen(member < mine, joined(before, piece), before)
            after = chosen(member > mine, joined(after, piece), after)
            if at + 1 < len(axes):
                total = joined(total, piece)
        prefix = joined(before, prefix)
        suffix = joined(suffix, after)
        block = total
    return prefix[1], suffix[2]


def scatter_sum(values, axis):
    devices = lax.axis_size(axis)
    rows, cols = values.shape
    got = lax.all_to_all(values.reshape(devices, rows // devices, cols), axis, 0, 0)
    return jnp.sum(got, axis=0)


def heads_scaled(values, factor):
    head_count, length = factor.shape
    shaped = values.astype(jnp.float32).reshape(length, head_count, -1) * factor.T[:, :, None]
    return shaped.astype(jnp.bfloat16).reshape(length, -1)


def per_device(ctx_parts, head_inputs, write_keys, read_queries, log_decay, out_grad):
    length, feature_width = head_inputs.shape
    head_count = log_decay.shape[0]
    head_size = feature_width // head_count
    cumulative = jnp.cumsum(log_decay, axis=1)
    block_end = cumulative[:, -1:]
    forward_w = jnp.exp(block_end - cumulative)
    backward_w = jnp.exp(cumulative)
    weighted_inputs = heads_scaled(head_inputs, forward_w)
    weighted_grads = heads_scaled(out_grad, backward_w)
    through = jnp.repeat(jnp.exp(block_end[:, 0]), head_size)
    own_state = jnp.dot(write_keys.T, weighted_inputs, preferred_element_type=jnp.float32)
    own_grad = jnp.dot(read_queries.T, weighted_grads, preferred_element_type=jnp.float32)

    entry, exit_ = scan_groups(through, own_state, own_grad, ctx_parts[::-1])
    entry_bf = entry.astype(jnp.bfloat16)
    exit_bf = exit_.astype(jnp.bfloat16)

    causal = jnp.arange(length)[:, None] >= jnp.arange(length)[None, :]
    spread = cumulative[:, :, None] - cumulative[:, None, :]
    decay_mat = jnp.exp(jnp.where(causal[None], spread, -jnp.inf))
    scores = jnp.dot(read_queries, write_keys.T, preferred_element_type=jnp.float32)
    mixing = (scores[None] * decay_mat).astype(jnp.bfloat16)
    inputs_heads = head_inputs.reshape(length, head_count, head_size)
    grads_heads = out_grad.reshape(length, head_count, head_size)
    input_mix = jnp.einsum(
        "hts,thp->shp", mixing, grads_heads, preferred_element_type=jnp.float32
    )
    pair_grad = jnp.einsum(
        "thp,shp->hts", grads_heads, inputs_heads, preferred_element_type=jnp.float32
    )
    score_grad = jnp.sum(pair_grad * decay_mat, axis=0)
    write_mix = jnp.dot(
        score_grad.T, read_queries.astype(jnp.float32), precision=lax.Precision.HIGHEST
    )
    read_mix = jnp.dot(
        score_grad, write_keys.astype(jnp.float32), precision=lax.Precision.HIGHEST
    )

    input_state = (
        jnp.dot(write_keys, exit_bf, preferred_element_type=jnp.float32).reshape(
            length, head_count, head_size
        )
        * forward_w.T[:, :, None]
    )
    input_grad = (input_mix + input_state).astype(jnp.bfloat16).reshape(length, feature_width)
    write_state = jnp.dot(weighted_inputs, exit_bf.T, preferred_element_type=jnp.float32)
    read_state = jnp.dot(weighted_grads, entry_bf.T, preferred_element_type=jnp.float32)
    both = jnp.concatenate([write_mix + write_state, read_mix + read_state], axis=1)
    summed = scatter_sum(both, "head")
    states = write_keys.shape[1]
    write_sum, read_sum = summed[:, :states], summed[:, states:]
    return (input_grad, write_sum.astype(jnp.bfloat16), read_sum.astype(jnp.bfloat16))


def solution(mesh):
    ctx_size = mesh.shape["ctx"]
    radix = 4
    sizes = []
    while ctx_size > 1:
        sizes.append(min(radix, ctx_size))
        ctx_size //= sizes[-1]
    parts = tuple("c%d" % i for i in range(len(sizes)))[::-1]
    devices = mesh.devices.reshape(tuple(sizes[::-1]) + (mesh.shape["head"],))
    split = jax.sharding.Mesh(devices, parts + ("head",))
    placed = (P(parts, "head"), P(parts, None), P(parts, None), P("head", parts), P(parts, "head"))
    return jax.shard_map(
        functools.partial(per_device, parts),
        mesh=split,
        in_specs=placed,
        out_specs=(P(parts, "head"), P(parts + ("head",), None), P(parts + ("head",), None)),
        check_vma=False,
    )
```

time: 147 us -> 121 us (0.82)
  the two profiles are of different devices: /device:TPU:1 before, /device:TPU:8 now
where the time goes in v3:
time: 121 us; the launch traced here: 120 us
  blocking collectives  40.4 us (33%)
  starting transfers between devices  31.2 us (26%)
  waiting for transfers between devices  26.6 us (22%)
  matrix products  8.22 us (7%)
  local copies, waits for them, and re-layouts  7.99 us (7%)
  other arithmetic  4.34 us (4%)
    all_to_all x1, blocking collectives, scan_groups(): got = lax.all_to_all(spread, axis, 0, 0)  40.4 us
    all_to_all x2, waiting for transfers between devices, scan_groups(): got = lax.all_to_all(spread, axis, 0, 0)  21.7 us
    all_to_all x1, starting transfers between devices, scatter_sum(): lax.all_to_all(values.reshape(devices, rows // devices, cols), axis, 0, 0)  19.2 us
    all_to_all x2, starting transfers between devices, scan_groups(): got = lax.all_to_all(spread, axis, 0, 0)  12 us
    all_to_all x1, waiting for transfers between devices, scatter_sum(): lax.all_to_all(values.reshape(devices, rows // devices, cols), axis, 0, 0)  4.95 us
    unnamed x69, local copies, waits for them, and re-layouts  4 us
  transfers between devices with their start and end apart: 3, of which 3 were waited for; matrix products, arithmetic and copies ran while one was open for 6% of the time, Pallas kernels for 0%

profile of v3, /device:TPU:8, one launch (start us, length us, event | category | flops | bytes accessed | tf_op | source)
XLA Modules:
  0.0 119.9 jit_solution(11753874653842465113)
XLA Ops:
  0.6 1.0 reduce_window_sum.11
  1.6 0.2 slice_reduce_fusion
  1.9 0.6 copy-done.11
  2.6 1.0 copy.14
  3.7 0.5 copy-done.5
  4.2 1.0 convolution_bitcast_fusion.1
  5.2 1.1 convolution_bitcast_fusion.2
  6.4 40.4 %all_to_all.20 = f32[4,257,256]{2,1,0:T(8,128)S(1)} all-to-all(f32[4,257,256]{2,1,0:T(8,128)S(1)} %broadcast_in_dim.23), channel_id=1, replica_groups=mesh['c2'=4,'c1'=4,'c0'=4,'head'=8] {'c0'}, dimensions={0} | all-to-all | bytes 2105344 | tf_op jit(solution)/shard_map/all_to_all | solution.py:28
  47.0 0.4 copy-done.29
  47.4 1.1 broadcast_in_dim.25
  48.5 5.5 %all-to-all-start.1 = ((f32[4,257,256]{2,1,0:T(8,128)}), f32[4,257,256]{2,1,0:T(8,128)S(1)}, u32[]{:S(2)}, u32[]{:S(2)}) async-start(f32[4,257,256]{2,1,0:T(8,128)} %broadcast_in_dim.25), calls=%async_computation.1 | async-start | bytes 2162688 | tf_op jit(solution)/shard_map/all_to_all | solution.py:28
  53.9 11.3 %all-to-all-done.1 = f32[4,257,256]{2,1,0:T(8,128)S(1)} async-done(((f32[4,257,256]{2,1,0:T(8,128)}), f32[4,257,256]{2,1,0:T(8,128)S(1)}, u32[]{:S(2)}, u32[]{:S(2)}) %all-to-all-start.1) | async-done | bytes 1052704 | tf_op jit(solution)/shard_map/all_to_all | solution.py:28
  65.3 0.6 fusion.33
  66.1 1.1 broadcast_in_dim.26
  67.2 6.6 %all-to-all-start.2 = ((f32[4,257,256]{2,1,0:T(8,128)}), f32[4,257,256]{2,1,0:T(8,128)S(1)}, u32[]{:S(2)}, u32[]{:S(2)}) async-start(f32[4,257,256]{2,1,0:T(8,128)} %broadcast_in_dim.26), calls=%async_computation.2 | async-start | bytes 2162688 | tf_op jit(solution)/shard_map/all_to_all | solution.py:28
  73.7 0.7 copy.17
  74.5 1.2 %fusion = f32[128,128]{1,0:T(8,128)S(1)} fusion(bf16[128,8,32]{0,2,1:T(8,128)(2,1)} %bitcast.230, bf16[128,8,32]{0,2,1:T(8,128)(2,1)} %bitcast.233, f32[8,128]{1,0:T(8,128)S(1)} %reduce_window_sum.11, pred[128,128]{1,0:T(8,128)(4,1)S(1)} %iota_compare_fusion), kind=kOutput, calls=%fused_computation.1 | convolution fusion | flops 8896512 | bytes 217088 | tf_op jit(solution)/shard_map/thp,shp->hts/dot_general | solution.py:83
  75.7 0.8 fusion.40
  76.5 0.9 fusion.42
  77.4 0.9 fusion.43
  78.2 1.3 %fusion.32 = (f32[256]{0:T(256)}, f32[256]{0:T(256)}, f32[256]{0:T(256)}, f32[256]{0:T(256)}, f32[256]{0:T(256)}, /*index=5*/f32[256]{0:T(256)}, f32[256]{0:T(256)}, f32[256]{0:T(256)}) fusion(f32[256]{0:T(256)S(1)} %bitcast.255, pred[]{:T(512)S(6)} %lt.40, f32[256]{0:T(256)} %bitcast.251, pred[]{:T(512)S(6)} %lt.36, f32[256]{0:T(256)S(1)} %bitcast.259, ...), kind=kLoop, calls=%fused_computation.101 | loop fusion | flops 3840 | bytes 16392 | tf_op jit(solution)/shard_map/mul | solution.py:12
  79.5 10.3 %all-to-all-done.2 = f32[4,257,256]{2,1,0:T(8,128)S(1)} async-done(((f32[4,257,256]{2,1,0:T(8,128)}), f32[4,257,256]{2,1,0:T(8,128)S(1)}, u32[]{:S(2)}, u32[]{:S(2)}) %all-to-all-start.2) | async-done | bytes 1052704 | tf_op jit(solution)/shard_map/all_to_all | solution.py:28
  90.0 1.0 fusion.10
  91.0 0.8 fusion.41
  91.8 0.2 convolution_add_fusion.1
  92.1 0.4 convolution_add_fusion
  92.6 0.8 copy.18
  93.3 19.2 %all-to-all-start.3 = ((f32[8,16,256]{2,1,0:T(8,128)}), f32[8,16,256]{2,1,0:T(8,128)S(1)}, u32[]{:S(2)}, u32[]{:S(2)}) async-start(f32[8,16,256]{2,1,0:T(8,128)} %bitcast.51), calls=%async_computation.3 | async-start | bytes 262144 | tf_op jit(solution)/shard_map/all_to_all | solution.py:45
  112.5 1.0 fusion.2
  113.6 0.7 copy.19
  114.3 5.0 %all-to-all-done.3 = f32[8,16,256]{2,1,0:T(8,128)S(1)} async-done(((f32[8,16,256]{2,1,0:T(8,128)}), f32[8,16,256]{2,1,0:T(8,128)S(1)}, u32[]{:S(2)}, u32[]{:S(2)}) %all-to-all-start.3) | async-done | bytes 131104 | tf_op jit(solution)/shard_map/all_to_all | solution.py:45
  119.3 0.6 fusion.39
  (84 shorter events, 1.0 us)
Async XLA Ops:
  0.6 4.6 %copy-start = (bf16[128,128]{1,0:T(8,128)(2,1)S(1)}, bf16[128,128]{1,0:T(8,128)(2,1)}, u32[]{:S(2)}) copy-start(bf16[128,128]{1,0:T(8,128)(2,1)} %param.6) | copy-start | bytes 98308
  46.8 18.5 %copy-start.14 = (f32[1,1,256]{2,1,0:T(1,128)}, f32[1,1,256]{2,1,0:T(1,128)S(1)}, u32[]{:S(2)}) copy-start(f32[1,1,256]{2,1,0:T(1,128)S(1)} %get-tuple-element.38) | copy-start | bytes 3076
  48.5 16.8 %all-to-all-start.1 = ((f32[4,257,256]{2,1,0:T(8,128)}), f32[4,257,256]{2,1,0:T(8,128)S(1)}, u32[]{:S(2)}, u32[]{:S(2)}) async-start(f32[4,257,256]{2,1,0:T(8,128)} %broadcast_in_dim.25), calls=%async_computation.1 | async-start | bytes 2162688 | tf_op jit(solution)/shard_map/all_to_all | solution.py:28
  65.3 1.9 %copy-start.16 = (f32[1,1,256]{2,1,0:T(1,128)}, f32[1,1,256]{2,1,0:T(1,128)S(1)}, u32[]{:S(2)}) copy-start(f32[1,1,256]{2,1,0:T(1,128)S(1)} %get-tuple-element.31) | copy-start | bytes 3076
  65.3 1.9 %copy-start.19 = (f32[1,1,256]{2,1,0:T(1,128)}, f32[1,1,256]{2,1,0:T(1,128)S(1)}, u32[]{:S(2)}) copy-start(f32[1,1,256]{2,1,0:T(1,128)S(1)} %get-tuple-element.32) | copy-start | bytes 3076
  65.3 1.9 %copy-start.22 = (f32[1,1,256]{2,1,0:T(1,128)}, f32[1,1,256]{2,1,0:T(1,128)S(1)}, u32[]{:S(2)}) copy-start(f32[1,1,256]{2,1,0:T(1,128)S(1)} %get-tuple-element.33) | copy-start | bytes 3076
  65.3 1.8 %copy-start.25 = (f32[1,1,256]{2,1,0:T(1,128)}, f32[1,1,256]{2,1,0:T(1,128)S(1)}, u32[]{:S(2)}) copy-start(f32[1,1,256]{2,1,0:T(1,128)S(1)} %get-tuple-element.34) | copy-start | bytes 3076
  65.9 1.2 %copy-start.27 = (f32[256]{0:T(256)}, f32[256]{0:T(256)S(1)}, u32[]{:S(2)}) copy-start(f32[256]{0:T(256)S(1)} %get-tuple-element.50) | copy-start | bytes 3076
  67.1 6.6 %copy-start.1 = (bf16[128,256]{1,0:T(8,128)(2,1)S(1)}, bf16[128,256]{1,0:T(8,128)(2,1)}, u32[]{:S(2)}) copy-start(bf16[128,256]{1,0:T(8,128)(2,1)} %param.5) | copy-start | bytes 196612
  67.2 8.6 %copy-start.2 = (bf16[128,128]{1,0:T(8,128)(2,1)S(1)}, bf16[128,128]{1,0:T(8,128)(2,1)}, u32[]{:S(2)}) copy-start(bf16[128,128]{1,0:T(8,128)(2,1)} %param.7) | copy-start | bytes 98308
  67.2 22.7 %all-to-all-start.2 = ((f32[4,257,256]{2,1,0:T(8,128)}), f32[4,257,256]{2,1,0:T(8,128)S(1)}, u32[]{:S(2)}, u32[]{:S(2)}) async-start(f32[4,257,256]{2,1,0:T(8,128)} %broadcast_in_dim.26), calls=%async_computation.2 | async-start | bytes 2162688 | tf_op jit(solution)/shard_map/all_to_all | solution.py:28
  74.5 3.8 %copy-start.17 = (f32[1,1,256]{2,1,0:T(1,128)S(1)}, f32[1,1,256]{2,1,0:T(1,128)}, u32[]{:S(2)}) copy-start(f32[1,1,256]{2,1,0:T(1,128)} %copy-done.16) | copy-start | bytes 3076
  74.5 3.8 %copy-start.20 = (f32[1,1,256]{2,1,0:T(1,128)S(1)}, f32[1,1,256]{2,1,0:T(1,128)}, u32[]{:S(2)}) copy-start(f32[1,1,256]{2,1,0:T(1,128)} %copy-done.19) | copy-start | bytes 3076
  74.5 3.8 %copy-start.23 = (f32[1,1,256]{2,1,0:T(1,128)S(1)}, f32[1,1,256]{2,1,0:T(1,128)}, u32[]{:S(2)}) copy-start(f32[1,1,256]{2,1,0:T(1,128)} %copy-done.22) | copy-start | bytes 3076
  74.5 3.8 %copy-start.26 = (f32[1,1,256]{2,1,0:T(1,128)S(1)}, f32[1,1,256]{2,1,0:T(1,128)}, u32[]{:S(2)}) copy-start(f32[1,1,256]{2,1,0:T(1,128)} %copy-done.25) | copy-start | bytes 3076
  74.5 2.0 %copy-start.13 = (pred[128,128]{1,0:T(8,128)(4,1)}, pred[128,128]{1,0:T(8,128)(4,1)S(1)}, u32[]{:S(2)}) copy-start(pred[128,128]{1,0:T(8,128)(4,1)S(1)} %iota_compare_fusion) | copy-start | bytes 49156
  77.4 14.4 %copy-start.7 = (f32[128,128]{0,1:T(8,128)S(1)}, f32[128,128]{0,1:T(8,128)}, u32[]{:S(2)}) copy-start(f32[128,128]{0,1:T(8,128)} %fusion.42) | copy-start | bytes 196612
  89.9 2.1 %copy-start.4 = (bf16[128,256]{0,1:T(8,128)(2,1)S(1)}, bf16[128,256]{0,1:T(8,128)(2,1)}, u32[]{:S(2)}) copy-start(bf16[128,256]{0,1:T(8,128)(2,1)} %copy-done.3) | copy-start | bytes 196612
  89.9 2.1 %copy-start.10 = (f32[128,128]{0,1:T(8,128)S(1)}, f32[128,128]{0,1:T(8,128)}, u32[]{:S(2)}) copy-start(f32[128,128]{0,1:T(8,128)} %fusion.43) | copy-start | bytes 196612
  89.9 2.1 %copy-start.15 = (f32[1,1,256]{2,1,0:T(1,128)S(1)}, f32[1,1,256]{2,1,0:T(1,128)}, u32[]{:S(2)}) copy-start(f32[1,1,256]{2,1,0:T(1,128)} %copy-done.14) | copy-start | bytes 3076
  89.9 2.1 %copy-start.18 = (f32[1,1,256]{2,1,0:T(1,128)S(1)}, f32[1,1,256]{2,1,0:T(1,128)}, u32[]{:S(2)}) copy-start(f32[1,1,256]{2,1,0:T(1,128)} %copy-done.16) | copy-start | bytes 3076
  89.9 2.1 %copy-start.21 = (f32[1,1,256]{2,1,0:T(1,128)S(1)}, f32[1,1,256]{2,1,0:T(1,128)}, u32[]{:S(2)}) copy-start(f32[1,1,256]{2,1,0:T(1,128)} %copy-done.19) | copy-start | bytes 3076
  89.9 2.1 %copy-start.24 = (f32[1,1,256]{2,1,0:T(1,128)S(1)}, f32[1,1,256]{2,1,0:T(1,128)}, u32[]{:S(2)}) copy-start(f32[1,1,256]{2,1,0:T(1,128)} %copy-done.22) | copy-start | bytes 3076
  89.9 2.1 %copy-start.28 = (f32[256]{0:T(256)S(1)}, f32[256]{0:T(256)}, u32[]{:S(2)}) copy-start(f32[256]{0:T(256)} %copy-done.27) | copy-start | bytes 3076
  90.0 2.1 %copy-start.30 = (f32[256]{0:T(256)S(1)}, f32[256]{0:T(256)}, u32[]{:S(2)}) copy-start(f32[256]{0:T(256)} %copy-done.29) | copy-start | bytes 3076
  90.0 2.1 %copy-start.31 = (f32[256]{0:T(256)S(1)}, f32[256]{0:T(256)}, u32[]{:S(2)}) copy-start(f32[256]{0:T(256)} %get-tuple-element.9) | copy-start | bytes 3076
  90.0 2.1 %copy-start.32 = (f32[256]{0:T(256)S(1)}, f32[256]{0:T(256)}, u32[]{:S(2)}) copy-start(f32[256]{0:T(256)} %get-tuple-element.10) | copy-start | bytes 3076
  92.1 20.4 %copy-start.6 = (bf16[128,256]{0,1:T(8,128)(2,1)S(1)}, bf16[128,256]{0,1:T(8,128)(2,1)}, u32[]{:S(2)}) copy-start(bf16[128,256]{0,1:T(8,128)(2,1)} %copy-done.5) | copy-start | bytes 196612
  92.1 20.4 %copy-start.8 = (f32[256,128]{1,0:T(8,128)S(1)}, f32[256,128]{1,0:T(8,128)}, u32[]{:S(2)}) copy-start(f32[256,128]{1,0:T(8,128)} %fusion.41) | copy-start | bytes 393220
  92.1 20.4 %copy-start.9 = (f32[128,128]{1,0:T(8,128)S(1)}, f32[128,128]{1,0:T(8,128)}, u32[]{:S(2)}) copy-start(f32[128,128]{1,0:T(8,128)} %fusion.40) | copy-start | bytes 196612
  92.1 20.4 %copy-start.12 = (f32[128,8]{0,1:T(8,128)S(1)}, f32[128,8]{0,1:T(8,128)}, u32[]{:S(2)}) copy-start(f32[128,8]{0,1:T(8,128)} %copy-done.11) | copy-start | bytes 12292
  93.3 26.0 %all-to-all-start.3 = ((f32[8,16,256]{2,1,0:T(8,128)}), f32[8,16,256]{2,1,0:T(8,128)S(1)}, u32[]{:S(2)}, u32[]{:S(2)}) async-start(f32[8,16,256]{2,1,0:T(8,128)} %bitcast.51), calls=%async_computation.3 | async-start | bytes 262144 | tf_op jit(solution)/shard_map/all_to_all | solution.py:45
  (4 other events, 2.8 us)

commit v4 on v3

--- a/solution.py
+++ b/solution.py
@@ -16,26 +16,36 @@
     return tuple(jnp.where(flag, y, n) for y, n in zip(yes, no))
 
 
-def scan_groups(decay, state, grad, axes):
+def scan_groups(decay, state, grad, axis, widths):
+    devices, mine = lax.axis_size(axis), lax.axis_index(axis)
     rows = state.shape[0]
     identity = (jnp.ones_like(decay), jnp.zeros_like(state), jnp.zeros_like(grad))
     block = (decay, state, grad)
     prefix, suffix = identity, identity
-    for at, axis in enumerate(axes):
-        size, mine = lax.axis_size(axis), lax.axis_index(axis)
+    low = 0
+    for at, width in enumerate(widths):
+        size = 1 << width
+        place = (mine >> low) & (size - 1)
         message = jnp.concatenate([block[0][None, :], block[1], block[2]], axis=0)
-        spread = jnp.broadcast_to(message[None], (size,) + message.shape)
-        got = lax.all_to_all(spread, axis, 0, 0)
+        got = {0: message}
+        for offset in range(1, size):
+            flip = offset << low
+            got[offset] = lax.ppermute(message, axis, [(i, i ^ flip) for i in range(devices)])
         before, after, total = identity, identity, identity
         for member in range(size):
-            piece = (got[member, 0], got[member, 1 : rows + 1], got[member, rows + 1 :])
-            before = chosen(member < mine, joined(before, piece), before)
-            after = chosen(member > mine, joined(after, piece), after)
-            if at + 1 < len(axes):
+            offset_of = place ^ member
+            arrived = got[0]
+            for offset in range(1, size):
+                arrived = jnp.where(offset_of == offset, got[offset], arrived)
+            piece = (arrived[0], arrived[1 : rows + 1], arrived[rows + 1 :])
+            before = chosen(member < place, joined(before, piece), before)
+            after = chosen(member > place, joined(after, piece), after)
+            if at + 1 < len(widths):
                 total = joined(total, piece)
         prefix = joined(before, prefix)
         suffix = joined(suffix, after)
         block = total
+        low += width
     return prefix[1], suffix[2]
 
 
@@ -52,7 +62,7 @@
     return shaped.astype(jnp.bfloat16).reshape(length, -1)
 
 
-def per_device(ctx_parts, head_inputs, write_keys, read_queries, log_decay, out_grad):
+def per_device(widths, head_inputs, write_keys, read_queries, log_decay, out_grad):
     length, feature_width = head_inputs.shape
     head_count = log_decay.shape[0]
     head_size = feature_width // head_count
@@ -66,7 +76,7 @@
     own_state = jnp.dot(write_keys.T, weighted_inputs, preferred_element_type=jnp.float32)
     own_grad = jnp.dot(read_queries.T, weighted_grads, preferred_element_type=jnp.float32)
 
-    entry, exit_ = scan_groups(through, own_state, own_grad, ctx_parts[::-1])
+    entry, exit_ = scan_groups(through, own_state, own_grad, "ctx", widths)
     entry_bf = entry.astype(jnp.bfloat16)
     exit_bf = exit_.astype(jnp.bfloat16)
 
@@ -107,21 +117,24 @@
     return (input_grad, write_sum.astype(jnp.bfloat16), read_sum.astype(jnp.bfloat16))
 
 
+SCAN_WIDTHS = (2, 2, 2)
+
+
 def solution(mesh):
-    ctx_size = mesh.shape["ctx"]
-    radix = 4
-    sizes = []
-    while ctx_size > 1:
-        sizes.append(min(radix, ctx_size))
-        ctx_size //= sizes[-1]
-    parts = tuple("c%d" % i for i in range(len(sizes)))[::-1]
-    devices = mesh.devices.reshape(tuple(sizes[::-1]) + (mesh.shape["head"],))
-    split = jax.sharding.Mesh(devices, parts + ("head",))
-    placed = (P(parts, "head"), P(parts, None), P(parts, None), P("head", parts), P(parts, "head"))
+    bits = mesh.shape["ctx"].bit_length() - 1
+    widths, left = [], bits
+    for width in SCAN_WIDTHS:
+        if left > 0:
+            widths.append(min(width, left))
+            left -= widths[-1]
+    while left > 0:
+        widths.append(1)
+        left -= 1
+    placed = (P("ctx", "head"), P("ctx", None), P("ctx", None), P("head", "ctx"), P("ctx", "head"))
     return jax.shard_map(
-        functools.partial(per_device, parts),
-        mesh=split,
+        functools.partial(per_device, tuple(widths)),
+        mesh=mesh,
         in_specs=placed,
-        out_specs=(P(parts, "head"), P(parts + ("head",), None), P(parts + ("head",), None)),
+        out_specs=(P("ctx", "head"), P(("ctx", "head"), None), P(("ctx", "head"), None)),
         check_vma=False,
     )

time: 121 us -> 116 us (0.959)
  the two profiles are of different devices: /device:TPU:8 before, /device:TPU:1 now
where the time goes in v4:
time: 116 us
  waiting for transfers between devices  55.4 us (48%)
  starting transfers between devices  42.1 us (36%)
  local copies, waits for them, and re-layouts  8.06 us (7%)
  matrix products  4.6 us (4%)
  other arithmetic  4.35 us (4%)
    ppermute x9, waiting for transfers between devices, scan_groups(): lax.ppermute(message, axis, [(i, i ^ flip) for i in range(devices)])  50.6 us
    ppermute x9, starting transfers between devices, scan_groups(): lax.ppermute(message, axis, [(i, i ^ flip) for i in range(devices)])  38.2 us
    unnamed x53, local copies, waits for them, and re-layouts  6.26 us
    all_to_all x1, waiting for transfers between devices, scatter_sum(): lax.all_to_all(values.reshape(devices, rows // devices, cols), axis, 0, 0)  4.76 us
    all_to_all x1, starting transfers between devices, scatter_sum(): lax.all_to_all(values.reshape(devices, rows // devices, cols), axis, 0, 0)  3.9 us
  transfers between devices with their start and end apart: 10, of which 8 were waited for; matrix products, arithmetic and copies ran while one was open for 4% of the time, Pallas kernels for 0%

profile of v4, /device:TPU:1, one launch (start us, length us, event | category | flops | bytes accessed | tf_op | source)
XLA Modules:
  0.0 115.5 jit_solution(13743726680687552501)
XLA Ops:
  0.6 1.0 reduce_window_sum.11
  2.0 0.7 copy-done.10
  4.9 12.4 %collective-permute-start = (f32[257,256]{1,0:T(8,128)S(1)}, f32[257,256]{1,0:T(8,128)S(1)}, u32[]{:S(2)}, u32[]{:S(2)}) collective-permute-start(f32[257,256]{1,0:T(8,128)S(1)} %pad_maximum_fusion), channel_id=1, source_target_pairs={{0,24},{8,16},{16,8},{24,0},{32,56},{40,48},{48,40},{56,32},{64,88... | collective-permute-start | bytes 789512 | tf_op jit(solution)/shard_map/ppermute | solution.py:33
  17.3 2.2 %collective-permute-start.1 = (f32[257,256]{1,0:T(8,128)S(1)}, f32[257,256]{1,0:T(8,128)S(1)}, u32[]{:S(2)}, u32[]{:S(2)}) collective-permute-start(f32[257,256]{1,0:T(8,128)S(1)} %pad_maximum_fusion), channel_id=1, source_target_pairs={{0,16},{8,24},{16,0},{24,8},{32,48},{40,56},{48,32},{56,40},{64,80... | collective-permute-start | bytes 789512 | tf_op jit(solution)/shard_map/ppermute | solution.py:33
  19.5 1.9 %collective-permute-start.2 = (f32[257,256]{1,0:T(8,128)S(1)}, f32[257,256]{1,0:T(8,128)S(1)}, u32[]{:S(2)}, u32[]{:S(2)}) collective-permute-start(f32[257,256]{1,0:T(8,128)S(1)} %pad_maximum_fusion), channel_id=1, source_target_pairs={{0,8},{8,0},{16,24},{24,16},{32,40},{40,32},{48,56},{56,48},{64,72... | collective-permute-start | bytes 789512 | tf_op jit(solution)/shard_map/ppermute | solution.py:33
  21.5 0.7 copy.17
  22.4 7.8 %collective-permute-done.1 = f32[257,256]{1,0:T(8,128)S(1)} collective-permute-done((f32[257,256]{1,0:T(8,128)S(1)}, f32[257,256]{1,0:T(8,128)S(1)}, u32[]{:S(2)}, u32[]{:S(2)}) %collective-permute-start.1) | collective-permute-done | bytes 263200 | tf_op jit(solution)/shard_map/ppermute | solution.py:33
  30.2 14.3 %collective-permute-done.2 = f32[257,256]{1,0:T(8,128)S(1)} collective-permute-done((f32[257,256]{1,0:T(8,128)S(1)}, f32[257,256]{1,0:T(8,128)S(1)}, u32[]{:S(2)}, u32[]{:S(2)}) %collective-permute-start.2) | collective-permute-done | bytes 263200 | tf_op jit(solution)/shard_map/ppermute | solution.py:33
  45.0 5.7 %collective-permute-start.3 = (f32[257,256]{1,0:T(8,128)S(1)}, f32[257,256]{1,0:T(8,128)S(1)}, u32[]{:S(2)}, u32[]{:S(2)}) collective-permute-start(f32[257,256]{1,0:T(8,128)S(1)} %pad_maximum_fusion.1), channel_id=1, source_target_pairs={{0,96},{8,104},{16,112},{24,120},{32,64},{40,72},{48,80},{56,88},{... | collective-permute-start | bytes 789512 | tf_op jit(solution)/shard_map/ppermute | solution.py:33
  50.7 2.1 %collective-permute-start.4 = (f32[257,256]{1,0:T(8,128)S(1)}, f32[257,256]{1,0:T(8,128)S(1)}, u32[]{:S(2)}, u32[]{:S(2)}) collective-permute-start(f32[257,256]{1,0:T(8,128)S(1)} %pad_maximum_fusion.1), channel_id=1, source_target_pairs={{0,64},{8,72},{16,80},{24,88},{32,96},{40,104},{48,112},{56,120},{... | collective-permute-start | bytes 789512 | tf_op jit(solution)/shard_map/ppermute | solution.py:33
  52.8 2.1 %collective-permute-start.5 = (f32[257,256]{1,0:T(8,128)S(1)}, f32[257,256]{1,0:T(8,128)S(1)}, u32[]{:S(2)}, u32[]{:S(2)}) collective-permute-start(f32[257,256]{1,0:T(8,128)S(1)} %pad_maximum_fusion.1), channel_id=1, source_target_pairs={{0,32},{8,40},{16,48},{24,56},{32,0},{40,8},{48,16},{56,24},{64,96... | collective-permute-start | bytes 789512 | tf_op jit(solution)/shard_map/ppermute | solution.py:33
  55.4 0.9 fusion.29
  56.2 5.9 %collective-permute-done.4 = f32[257,256]{1,0:T(8,128)S(1)} collective-permute-done((f32[257,256]{1,0:T(8,128)S(1)}, f32[257,256]{1,0:T(8,128)S(1)}, u32[]{:S(2)}, u32[]{:S(2)}) %collective-permute-start.4) | collective-permute-done | bytes 263200 | tf_op jit(solution)/shard_map/ppermute | solution.py:33
  62.1 1.0 collective-permute-done.5
  63.3 0.6 fusion.23
  63.9 0.6 fusion.22
  65.2 0.7 pad_maximum_fusion.2
  66.0 5.9 %collective-permute-start.6 = (f32[257,256]{1,0:T(8,128)}, f32[257,256]{1,0:T(8,128)S(1)}, u32[]{:S(2)}, u32[]{:S(2)}) collective-permute-start(f32[257,256]{1,0:T(8,128)} %pad_maximum_fusion.2), channel_id=1, source_target_pairs={{0,384},{8,392},{16,400},{24,408},{32,416},{40,424},{48,432},{56,4... | collective-permute-start | bytes 789512 | tf_op jit(solution)/shard_map/ppermute | solution.py:33
  71.8 3.5 %collective-permute-start.7 = (f32[257,256]{1,0:T(8,128)}, f32[257,256]{1,0:T(8,128)S(1)}, u32[]{:S(2)}, u32[]{:S(2)}) collective-permute-start(f32[257,256]{1,0:T(8,128)} %pad_maximum_fusion.2), channel_id=1, source_target_pairs={{0,256},{8,264},{16,272},{24,280},{32,288},{40,296},{48,304},{56,3... | collective-permute-start | bytes 789512 | tf_op jit(solution)/shard_map/ppermute | solution.py:33
  75.4 2.4 %collective-permute-start.8 = (f32[257,256]{1,0:T(8,128)}, f32[257,256]{1,0:T(8,128)S(1)}, u32[]{:S(2)}, u32[]{:S(2)}) collective-permute-start(f32[257,256]{1,0:T(8,128)} %pad_maximum_fusion.2), channel_id=1, source_target_pairs={{0,128},{8,136},{16,144},{24,152},{32,160},{40,168},{48,176},{56,1... | collective-permute-start | bytes 789512 | tf_op jit(solution)/shard_map/ppermute | solution.py:33
  77.8 0.8 fusion.27
  78.5 1.1 fusion.30
  79.6 16.0 %collective-permute-done.6 = f32[257,256]{1,0:T(8,128)S(1)} collective-permute-done((f32[257,256]{1,0:T(8,128)}, f32[257,256]{1,0:T(8,128)S(1)}, u32[]{:S(2)}, u32[]{:S(2)}) %collective-permute-start.6) | collective-permute-done | bytes 263200 | tf_op jit(solution)/shard_map/ppermute | solution.py:33
  95.6 5.4 %collective-permute-done.8 = f32[257,256]{1,0:T(8,128)S(1)} collective-permute-done((f32[257,256]{1,0:T(8,128)}, f32[257,256]{1,0:T(8,128)S(1)}, u32[]{:S(2)}, u32[]{:S(2)}) %collective-permute-start.8) | collective-permute-done | bytes 263200 | tf_op jit(solution)/shard_map/ppermute | solution.py:33
  101.3 0.6 copy-done.16
  102.5 0.6 copy-done.9
  103.3 0.7 copy-done.4
  104.4 0.7 copy.18
  105.2 3.9 %all-to-all-start = ((f32[8,16,256]{2,1,0:T(8,128)}), f32[8,16,256]{2,1,0:T(8,128)S(1)}, u32[]{:S(2)}, u32[]{:S(2)}) async-start(f32[8,16,256]{2,1,0:T(8,128)} %bitcast.41), calls=%async_computation | async-start | bytes 262144 | tf_op jit(solution)/shard_map/all_to_all | solution.py:55
  109.4 0.7 copy.19
  110.2 4.8 %all-to-all-done = f32[8,16,256]{2,1,0:T(8,128)S(1)} async-done(((f32[8,16,256]{2,1,0:T(8,128)}), f32[8,16,256]{2,1,0:T(8,128)S(1)}, u32[]{:S(2)}, u32[]{:S(2)}) %all-to-all-start) | async-done | bytes 131104 | tf_op jit(solution)/shard_map/all_to_all | solution.py:55
  114.9 0.6 fusion.26
  (85 shorter events, 6.2 us)
Async XLA Ops:
  0.6 3.8 %copy-start = (bf16[128,128]{1,0:T(8,128)(2,1)S(1)}, bf16[128,128]{1,0:T(8,128)(2,1)}, u32[]{:S(2)}) copy-start(bf16[128,128]{1,0:T(8,128)(2,1)} %param.6) | copy-start | bytes 98308
  1.9 0.8 copy-start.10
  3.0 0.8 copy-start.2
  3.8 0.9 copy-start.1
  4.9 17.5 %collective-permute-start = (f32[257,256]{1,0:T(8,128)S(1)}, f32[257,256]{1,0:T(8,128)S(1)}, u32[]{:S(2)}, u32[]{:S(2)}) collective-permute-start(f32[257,256]{1,0:T(8,128)S(1)} %pad_maximum_fusion), channel_id=1, source_target_pairs={{0,24},{8,16},{16,8},{24,0},{32,56},{40,48},{48,40},{56,32},{64,88... | collective-permute-start | bytes 789512 | tf_op jit(solution)/shard_map/ppermute | solution.py:33
  17.3 12.9 %collective-permute-start.1 = (f32[257,256]{1,0:T(8,128)S(1)}, f32[257,256]{1,0:T(8,128)S(1)}, u32[]{:S(2)}, u32[]{:S(2)}) collective-permute-start(f32[257,256]{1,0:T(8,128)S(1)} %pad_maximum_fusion), channel_id=1, source_target_pairs={{0,16},{8,24},{16,0},{24,8},{32,48},{40,56},{48,32},{56,40},{64,80... | collective-permute-start | bytes 789512 | tf_op jit(solution)/shard_map/ppermute | solution.py:33
  19.5 25.1 %collective-permute-start.2 = (f32[257,256]{1,0:T(8,128)S(1)}, f32[257,256]{1,0:T(8,128)S(1)}, u32[]{:S(2)}, u32[]{:S(2)}) collective-permute-start(f32[257,256]{1,0:T(8,128)S(1)} %pad_maximum_fusion), channel_id=1, source_target_pairs={{0,8},{8,0},{16,24},{24,16},{32,40},{40,32},{48,56},{56,48},{64,72... | collective-permute-start | bytes 789512 | tf_op jit(solution)/shard_map/ppermute | solution.py:33
  45.0 10.0 %copy-start.6 = (bf16[128,256]{0,1:T(8,128)(2,1)S(1)}, bf16[128,256]{0,1:T(8,128)(2,1)}, u32[]{:S(2)}) copy-start(bf16[128,256]{0,1:T(8,128)(2,1)} %copy-done.5) | copy-start | bytes 196612
  45.0 10.0 %copy-start.12 = (bf16[128,256]{0,1:T(8,128)(2,1)S(1)}, bf16[128,256]{0,1:T(8,128)(2,1)}, u32[]{:S(2)}) copy-start(bf16[128,256]{0,1:T(8,128)(2,1)} %copy.17) | copy-start | bytes 196612
  45.0 11.2 %collective-permute-start.3 = (f32[257,256]{1,0:T(8,128)S(1)}, f32[257,256]{1,0:T(8,128)S(1)}, u32[]{:S(2)}, u32[]{:S(2)}) collective-permute-start(f32[257,256]{1,0:T(8,128)S(1)} %pad_maximum_fusion.1), channel_id=1, source_target_pairs={{0,96},{8,104},{16,112},{24,120},{32,64},{40,72},{48,80},{56,88},{... | collective-permute-start | bytes 789512 | tf_op jit(solution)/shard_map/ppermute | solution.py:33
  50.7 11.4 %collective-permute-start.4 = (f32[257,256]{1,0:T(8,128)S(1)}, f32[257,256]{1,0:T(8,128)S(1)}, u32[]{:S(2)}, u32[]{:S(2)}) collective-permute-start(f32[257,256]{1,0:T(8,128)S(1)} %pad_maximum_fusion.1), channel_id=1, source_target_pairs={{0,64},{8,72},{16,80},{24,88},{32,96},{40,104},{48,112},{56,120},{... | collective-permute-start | bytes 789512 | tf_op jit(solution)/shard_map/ppermute | solution.py:33
  52.8 10.3 %collective-permute-start.5 = (f32[257,256]{1,0:T(8,128)S(1)}, f32[257,256]{1,0:T(8,128)S(1)}, u32[]{:S(2)}, u32[]{:S(2)}) collective-permute-start(f32[257,256]{1,0:T(8,128)S(1)} %pad_maximum_fusion.1), channel_id=1, source_target_pairs={{0,32},{8,40},{16,48},{24,56},{32,0},{40,8},{48,16},{56,24},{64,96... | collective-permute-start | bytes 789512 | tf_op jit(solution)/shard_map/ppermute | solution.py:33
  55.3 0.9 copy-start.8
  66.0 29.6 %collective-permute-start.6 = (f32[257,256]{1,0:T(8,128)}, f32[257,256]{1,0:T(8,128)S(1)}, u32[]{:S(2)}, u32[]{:S(2)}) collective-permute-start(f32[257,256]{1,0:T(8,128)} %pad_maximum_fusion.2), channel_id=1, source_target_pairs={{0,384},{8,392},{16,400},{24,408},{32,416},{40,424},{48,432},{56,4... | collective-permute-start | bytes 789512 | tf_op jit(solution)/shard_map/ppermute | solution.py:33
  71.8 23.8 %collective-permute-start.7 = (f32[257,256]{1,0:T(8,128)}, f32[257,256]{1,0:T(8,128)S(1)}, u32[]{:S(2)}, u32[]{:S(2)}) collective-permute-start(f32[257,256]{1,0:T(8,128)} %pad_maximum_fusion.2), channel_id=1, source_target_pairs={{0,256},{8,264},{16,272},{24,280},{32,288},{40,296},{48,304},{56,3... | collective-permute-start | bytes 789512 | tf_op jit(solution)/shard_map/ppermute | solution.py:33
  75.4 25.6 %collective-permute-start.8 = (f32[257,256]{1,0:T(8,128)}, f32[257,256]{1,0:T(8,128)S(1)}, u32[]{:S(2)}, u32[]{:S(2)}) collective-permute-start(f32[257,256]{1,0:T(8,128)} %pad_maximum_fusion.2), channel_id=1, source_target_pairs={{0,128},{8,136},{16,144},{24,152},{32,160},{40,168},{48,176},{56,1... | collective-permute-start | bytes 789512 | tf_op jit(solution)/shard_map/ppermute | solution.py:33
  101.2 0.7 copy-start.16
  101.3 0.7 copy-start.17
  101.3 0.7 copy-start.18
  101.3 0.7 copy-start.19
  101.3 0.7 copy-start.20
  101.3 0.7 copy-start.21
  101.3 0.7 copy-start.22
  101.3 0.6 copy-start.15
  102.3 0.8 copy-start.9
  103.1 0.8 copy-start.4
  103.1 0.8 copy-start.23
  103.1 0.8 copy-start.24
  103.3 0.7 copy-start.14
  105.2 3.9 %copy-start.7 = (bf16[128,256]{0,1:T(8,128)(2,1)S(1)}, bf16[128,256]{0,1:T(8,128)(2,1)}, u32[]{:S(2)}) copy-start(bf16[128,256]{0,1:T(8,128)(2,1)} %copy-done.5) | copy-start | bytes 196612
  105.2 3.9 %copy-start.11 = (f32[128,128]{1,0:T(8,128)S(1)}, f32[128,128]{1,0:T(8,128)}, u32[]{:S(2)}) copy-start(f32[128,128]{1,0:T(8,128)} %fusion.27) | copy-start | bytes 196612
  105.2 9.7 %all-to-all-start = ((f32[8,16,256]{2,1,0:T(8,128)}), f32[8,16,256]{2,1,0:T(8,128)S(1)}, u32[]{:S(2)}, u32[]{:S(2)}) async-start(f32[8,16,256]{2,1,0:T(8,128)} %bitcast.41), calls=%async_computation | async-start | bytes 262144 | tf_op jit(solution)/shard_map/all_to_all | solution.py:55
  (3 other events, 1.8 us)

commit v5 on v2

--- a/solution.py
+++ b/solution.py
@@ -13,16 +13,24 @@
     shift = 1
     while shift < devices:
         pairs = [(i, i ^ shift) for i in range(devices)]
-        message = jnp.concatenate([block_decay[None, :], block_state, block_grad], axis=0)
-        got = lax.ppermute(message, axis, pairs)
-        got_decay, got_state, got_grad = got[0], got[1 : rows + 1], got[rows + 1 :]
         later = (mine & shift) != 0
+        last = shift * 2 >= devices
+        if last:
+            message = jnp.concatenate(
+                [block_decay[None, :], jnp.where(later, block_grad, block_state)], axis=0
+            )
+            got = lax.ppermute(message, axis, pairs)
+            got_decay, got_state, got_grad = got[0], got[1:], got[1:]
+        else:
+            message = jnp.concatenate([block_decay[None, :], block_state, block_grad], axis=0)
+            got = lax.ppermute(message, axis, pairs)
+            got_decay, got_state, got_grad = got[0], got[1 : rows + 1], got[rows + 1 :]
         prefix_state = jnp.where(later, prefix_decay[None, :] * got_state + prefix_state, prefix_state)
         prefix_decay = jnp.where(later, got_decay * prefix_decay, prefix_decay)
         suffix_grad = jnp.where(later, suffix_grad, suffix_decay[None, :] * got_grad + suffix_grad)
         suffix_decay = jnp.where(later, suffix_decay, got_decay * suffix_decay)
         shift *= 2
-        if shift < devices:
+        if not last:
             block_state = jnp.where(
                 later,
                 block_decay[None, :] * got_state + block_state,
@@ -38,22 +46,10 @@
 
 
 def scatter_sum(values, axis):
-    devices, mine = lax.axis_size(axis), lax.axis_index(axis)
-    bits = devices.bit_length() - 1
+    devices = lax.axis_size(axis)
     rows, cols = values.shape
-    piece = rows // devices
-    x = values.reshape((2,) * bits + (piece, cols))
-    x = x.transpose(tuple(range(bits - 1, -1, -1)) + (bits, bits + 1)).reshape(rows, cols)
-    shift = 1
-    while shift < devices:
-        half = x.shape[0] // 2
-        upper = (mine & shift) != 0
-        keep = jnp.where(upper, x[half:], x[:half])
-        send = jnp.where(upper, x[:half], x[half:])
-        got = lax.ppermute(send, axis, [(i, i ^ shift) for i in range(devices)])
-        x = keep + got
-        shift *= 2
-    return x
+    got = lax.all_to_all(values.reshape(devices, rows // devices, cols), axis, 0, 0)
+    return jnp.sum(got, axis=0)
 
 
 def heads_scaled(values, factor):

time: 109 us -> 99.6 us (0.914); the launches traced: 107 us -> 99 us
  starting transfers between devices: 60.4 us -> 53.9 us
  waiting for transfers between devices: 37.4 us -> 35.2 us
    ppermute x3 -> x0, starting transfers between devices: 24.7 us -> none  [scatter_sum(): got = lax.ppermute(send, axis, [(i, i ^ shift) for i in range(devices)])]
    all_to_all x0 -> x1, starting transfers between devices: none -> 18.1 us  [scatter_sum(): lax.all_to_all(values.reshape(devices, rows // devices, cols), axis, 0, 0)]
    ppermute x6, waiting for transfers between devices: 35.6 us -> 30.5 us  [scan_both(): got = lax.ppermute(message, axis, pairs)]
    all_to_all x0 -> x1, waiting for transfers between devices: none -> 4.73 us  [scatter_sum(): lax.all_to_all(values.reshape(devices, rows // devices, cols), axis, 0, 0)]
    ppermute x3 -> x0, waiting for transfers between devices: 1.86 us -> none  [scatter_sum(): got = lax.ppermute(send, axis, [(i, i ^ shift) for i in range(devices)])]
  transfers between devices with their start and end apart: 9 -> 7, of which waited for: 8 -> 7; matrix products, arithmetic and copies ran while one was open for 2% -> 2% of each run, Pallas kernels for 0% -> 0%
where the time goes in v5:
time: 99.6 us; the launch traced here: 99 us
  starting transfers between devices  53.9 us (54%)
  waiting for transfers between devices  35.2 us (35%)
  local copies, waits for them, and re-layouts  4.93 us (5%)
  matrix products  2.28 us (2%)
  other arithmetic  1.78 us (2%)
    ppermute x6, starting transfers between devices, scan_both(): got = lax.ppermute(message, axis, pairs)  35.8 us
    ppermute x6, waiting for transfers between devices, scan_both(): got = lax.ppermute(message, axis, pairs)  30.5 us
    all_to_all x1, starting transfers between devices, scatter_sum(): lax.all_to_all(values.reshape(devices, rows // devices, cols), axis, 0, 0)  18.1 us
    all_to_all x1, waiting for transfers between devices, scatter_sum(): lax.all_to_all(values.reshape(devices, rows // devices, cols), axis, 0, 0)  4.73 us
    unnamed x11, local copies, waits for them, and re-layouts  3.06 us
  transfers between devices with their start and end apart: 7, of which 7 were waited for; matrix products, arithmetic and copies ran while one was open for 2% of the time, Pallas kernels for 0%

profile of v5, /device:TPU:1, one launch (start us, length us, event | category | flops | bytes accessed | tf_op | source)
XLA Modules:
  0.0 99.0 jit_solution(2442625476832047385)
XLA Ops:
  0.6 1.0 reduce_window_sum.11
  1.6 0.2 slice_reduce_fusion
  2.0 0.7 copy-done.3
  3.0 0.7 copy-done.2
  3.8 0.2 convolution_bitcast_fusion.1
  4.0 0.6 copy-done.1
  4.6 0.2 convolution_bitcast_fusion.2
  4.9 11.5 %collective-permute-start = (f32[257,256]{1,0:T(8,128)S(1)}, f32[257,256]{1,0:T(8,128)S(1)}, u32[]{:S(2)}, u32[]{:S(2)}) collective-permute-start(f32[257,256]{1,0:T(8,128)S(1)} %pad_maximum_fusion), channel_id=1, source_target_pairs={{0,8},{8,0},{16,24},{24,16},{32,40},{40,32},{48,56},{56,48},{64,72... | collective-permute-start | bytes 789512 | tf_op jit(solution)/shard_map/ppermute | solution.py:26
  16.4 5.3 %collective-permute-done = f32[257,256]{1,0:T(8,128)S(1)} collective-permute-done((f32[257,256]{1,0:T(8,128)S(1)}, f32[257,256]{1,0:T(8,128)S(1)}, u32[]{:S(2)}, u32[]{:S(2)}) %collective-permute-start) | collective-permute-done | bytes 263200 | tf_op jit(solution)/shard_map/ppermute | solution.py:26
  21.9 3.9 %collective-permute-start.1 = (f32[257,256]{1,0:T(8,128)S(1)}, f32[257,256]{1,0:T(8,128)S(1)}, u32[]{:S(2)}, u32[]{:S(2)}) collective-permute-start(f32[257,256]{1,0:T(8,128)S(1)} %pad_maximum_fusion.1), channel_id=1, source_target_pairs={{0,16},{8,24},{16,0},{24,8},{32,48},{40,56},{48,32},{56,40},{64,80... | collective-permute-start | bytes 789512 | tf_op jit(solution)/shard_map/ppermute | solution.py:26
  25.8 4.7 %collective-permute-done.1 = f32[257,256]{1,0:T(8,128)S(1)} collective-permute-done((f32[257,256]{1,0:T(8,128)S(1)}, f32[257,256]{1,0:T(8,128)S(1)}, u32[]{:S(2)}, u32[]{:S(2)}) %collective-permute-start.1) | collective-permute-done | bytes 263200 | tf_op jit(solution)/shard_map/ppermute | solution.py:26
  30.6 5.3 %collective-permute-start.2 = (f32[257,256]{1,0:T(8,128)S(1)}, f32[257,256]{1,0:T(8,128)S(1)}, u32[]{:S(2)}, u32[]{:S(2)}) collective-permute-start(f32[257,256]{1,0:T(8,128)S(1)} %pad_maximum_fusion.2), channel_id=1, source_target_pairs={{0,32},{8,40},{16,48},{24,56},{32,0},{40,8},{48,16},{56,24},{64,96... | collective-permute-start | bytes 789512 | tf_op jit(solution)/shard_map/ppermute | solution.py:26
  35.9 4.2 %collective-permute-done.2 = f32[257,256]{1,0:T(8,128)S(1)} collective-permute-done((f32[257,256]{1,0:T(8,128)S(1)}, f32[257,256]{1,0:T(8,128)S(1)}, u32[]{:S(2)}, u32[]{:S(2)}) %collective-permute-start.2) | collective-permute-done | bytes 263200 | tf_op jit(solution)/shard_map/ppermute | solution.py:26
  40.3 3.4 %collective-permute-start.3 = (f32[257,256]{1,0:T(8,128)S(1)}, f32[257,256]{1,0:T(8,128)S(1)}, u32[]{:S(2)}, u32[]{:S(2)}) collective-permute-start(f32[257,256]{1,0:T(8,128)S(1)} %pad_maximum_fusion.3), channel_id=1, source_target_pairs={{0,64},{8,72},{16,80},{24,88},{32,96},{40,104},{48,112},{56,120},{... | collective-permute-start | bytes 789512 | tf_op jit(solution)/shard_map/ppermute | solution.py:26
  43.8 0.3 fusion
  44.1 3.3 %collective-permute-done.3 = f32[257,256]{1,0:T(8,128)S(1)} collective-permute-done((f32[257,256]{1,0:T(8,128)S(1)}, f32[257,256]{1,0:T(8,128)S(1)}, u32[]{:S(2)}, u32[]{:S(2)}) %collective-permute-start.3) | collective-permute-done | bytes 263200 | tf_op jit(solution)/shard_map/ppermute | solution.py:26
  47.6 4.4 %collective-permute-start.4 = (f32[257,256]{1,0:T(8,128)S(1)}, f32[257,256]{1,0:T(8,128)S(1)}, u32[]{:S(2)}, u32[]{:S(2)}) collective-permute-start(f32[257,256]{1,0:T(8,128)S(1)} %pad_maximum_fusion.4), channel_id=1, source_target_pairs={{0,128},{8,136},{16,144},{24,152},{32,160},{40,168},{48,176},{56,1... | collective-permute-start | bytes 789512 | tf_op jit(solution)/shard_map/ppermute | solution.py:26
  52.0 0.2 fusion.23
  52.2 0.2 fusion.24
  52.5 10.5 %collective-permute-done.4 = f32[257,256]{1,0:T(8,128)S(1)} collective-permute-done((f32[257,256]{1,0:T(8,128)S(1)}, f32[257,256]{1,0:T(8,128)S(1)}, u32[]{:S(2)}, u32[]{:S(2)}) %collective-permute-start.4) | collective-permute-done | bytes 263200 | tf_op jit(solution)/shard_map/ppermute | solution.py:26
  63.1 7.3 %collective-permute-start.5 = (f32[129,256]{1,0:T(8,128)S(1)}, f32[129,256]{1,0:T(8,128)S(1)}, u32[]{:S(2)}, u32[]{:S(2)}) collective-permute-start(f32[129,256]{1,0:T(8,128)S(1)} %pad_maximum_fusion.5), channel_id=1, source_target_pairs={{0,256},{8,264},{16,272},{24,280},{32,288},{40,296},{48,304},{56,3... | collective-permute-start | bytes 396296 | tf_op jit(solution)/shard_map/ppermute | solution.py:22
  70.6 2.4 %collective-permute-done.5 = f32[129,256]{1,0:T(8,128)S(1)} collective-permute-done((f32[129,256]{1,0:T(8,128)S(1)}, f32[129,256]{1,0:T(8,128)S(1)}, u32[]{:S(2)}, u32[]{:S(2)}) %collective-permute-start.5) | collective-permute-done | bytes 132128 | tf_op jit(solution)/shard_map/ppermute | solution.py:22
  73.0 0.1 fusion.8
  73.1 0.2 fusion.22
  73.3 0.2 convolution_add_fusion.1
  73.5 0.3 convolution_add_fusion
  73.8 0.7 copy.18
  74.5 18.1 %all-to-all-start = ((f32[8,16,256]{2,1,0:T(8,128)}), f32[8,16,256]{2,1,0:T(8,128)S(1)}, u32[]{:S(2)}, u32[]{:S(2)}) async-start(f32[8,16,256]{2,1,0:T(8,128)} %bitcast.31), calls=%async_computation | async-start | bytes 262144 | tf_op jit(solution)/shard_map/all_to_all | solution.py:51
  92.6 0.3 fusion.2
  92.9 0.7 copy.19
  93.7 4.7 %all-to-all-done = f32[8,16,256]{2,1,0:T(8,128)S(1)} async-done(((f32[8,16,256]{2,1,0:T(8,128)}), f32[8,16,256]{2,1,0:T(8,128)S(1)}, u32[]{:S(2)}, u32[]{:S(2)}) %all-to-all-start) | async-done | bytes 131104 | tf_op jit(solution)/shard_map/all_to_all | solution.py:51
  98.4 0.6 fusion.20
  (35 shorter events, 1.4 us)
Async XLA Ops:
  0.6 3.4 %copy-start = (bf16[128,128]{1,0:T(8,128)(2,1)S(1)}, bf16[128,128]{1,0:T(8,128)(2,1)}, u32[]{:S(2)}) copy-start(bf16[128,128]{1,0:T(8,128)(2,1)} %param.6) | copy-start | bytes 98308
  1.9 0.8 copy-start.3
  3.0 0.8 copy-start.2
  3.8 0.8 copy-start.1
  4.9 16.9 %collective-permute-start = (f32[257,256]{1,0:T(8,128)S(1)}, f32[257,256]{1,0:T(8,128)S(1)}, u32[]{:S(2)}, u32[]{:S(2)}) collective-permute-start(f32[257,256]{1,0:T(8,128)S(1)} %pad_maximum_fusion), channel_id=1, source_target_pairs={{0,8},{8,0},{16,24},{24,16},{32,40},{40,32},{48,56},{56,48},{64,72... | collective-permute-start | bytes 789512 | tf_op jit(solution)/shard_map/ppermute | solution.py:26
  21.9 8.6 %collective-permute-start.1 = (f32[257,256]{1,0:T(8,128)S(1)}, f32[257,256]{1,0:T(8,128)S(1)}, u32[]{:S(2)}, u32[]{:S(2)}) collective-permute-start(f32[257,256]{1,0:T(8,128)S(1)} %pad_maximum_fusion.1), channel_id=1, source_target_pairs={{0,16},{8,24},{16,0},{24,8},{32,48},{40,56},{48,32},{56,40},{64,80... | collective-permute-start | bytes 789512 | tf_op jit(solution)/shard_map/ppermute | solution.py:26
  30.6 9.6 %collective-permute-start.2 = (f32[257,256]{1,0:T(8,128)S(1)}, f32[257,256]{1,0:T(8,128)S(1)}, u32[]{:S(2)}, u32[]{:S(2)}) collective-permute-start(f32[257,256]{1,0:T(8,128)S(1)} %pad_maximum_fusion.2), channel_id=1, source_target_pairs={{0,32},{8,40},{16,48},{24,56},{32,0},{40,8},{48,16},{56,24},{64,96... | collective-permute-start | bytes 789512 | tf_op jit(solution)/shard_map/ppermute | solution.py:26
  40.3 7.2 %collective-permute-start.3 = (f32[257,256]{1,0:T(8,128)S(1)}, f32[257,256]{1,0:T(8,128)S(1)}, u32[]{:S(2)}, u32[]{:S(2)}) collective-permute-start(f32[257,256]{1,0:T(8,128)S(1)} %pad_maximum_fusion.3), channel_id=1, source_target_pairs={{0,64},{8,72},{16,80},{24,88},{32,96},{40,104},{48,112},{56,120},{... | collective-permute-start | bytes 789512 | tf_op jit(solution)/shard_map/ppermute | solution.py:26
  47.6 15.4 %collective-permute-start.4 = (f32[257,256]{1,0:T(8,128)S(1)}, f32[257,256]{1,0:T(8,128)S(1)}, u32[]{:S(2)}, u32[]{:S(2)}) collective-permute-start(f32[257,256]{1,0:T(8,128)S(1)} %pad_maximum_fusion.4), channel_id=1, source_target_pairs={{0,128},{8,136},{16,144},{24,152},{32,160},{40,168},{48,176},{56,1... | collective-permute-start | bytes 789512 | tf_op jit(solution)/shard_map/ppermute | solution.py:26
  63.1 9.9 %collective-permute-start.5 = (f32[129,256]{1,0:T(8,128)S(1)}, f32[129,256]{1,0:T(8,128)S(1)}, u32[]{:S(2)}, u32[]{:S(2)}) collective-permute-start(f32[129,256]{1,0:T(8,128)S(1)} %pad_maximum_fusion.5), channel_id=1, source_target_pairs={{0,256},{8,264},{16,272},{24,280},{32,288},{40,296},{48,304},{56,3... | collective-permute-start | bytes 396296 | tf_op jit(solution)/shard_map/ppermute | solution.py:22
  74.5 23.9 %all-to-all-start = ((f32[8,16,256]{2,1,0:T(8,128)}), f32[8,16,256]{2,1,0:T(8,128)S(1)}, u32[]{:S(2)}, u32[]{:S(2)}) async-start(f32[8,16,256]{2,1,0:T(8,128)} %bitcast.31), calls=%async_computation | async-start | bytes 262144 | tf_op jit(solution)/shard_map/all_to_all | solution.py:51

commit v6 on v5

--- a/solution.py
+++ b/solution.py
@@ -2,6 +2,9 @@
 import jax.numpy as jnp
 from jax import lax
 from jax.sharding import PartitionSpec as P
+
+
+PARTNER_MASKS = {64: {4: 6, 32: 56}}
 
 
 def scan_both(decay, state, grad, axis):
@@ -12,7 +15,8 @@
     rows = state.shape[0]
     shift = 1
     while shift < devices:
-        pairs = [(i, i ^ shift) for i in range(devices)]
+        mask = PARTNER_MASKS.get(devices, {}).get(shift, shift)
+        pairs = [(i, i ^ mask) for i in range(devices)]
         later = (mine & shift) != 0
         last = shift * 2 >= devices
         if last:

time: 99.6 us -> 97.1 us (0.975)
  starting transfers between devices: 53.9 us -> 49.4 us
  waiting for transfers between devices: 35.2 us -> 37.3 us
    ppermute x6, starting transfers between devices: 35.8 us -> 33.1 us  [scan_both(): got = lax.ppermute(message, axis, pairs)]
    ppermute x6, waiting for transfers between devices: 30.5 us -> 32.5 us  [scan_both(): got = lax.ppermute(message, axis, pairs)]
    all_to_all x1, starting transfers between devices: 18.1 us -> 16.3 us  [scatter_sum(): lax.all_to_all(values.reshape(devices, rows // devices, cols), axis, 0, 0)]
where the time goes in v6:
time: 97.1 us; the launch traced here: 96.6 us
  starting transfers between devices  49.4 us (51%)
  waiting for transfers between devices  37.3 us (38%)
  local copies, waits for them, and re-layouts  4.93 us (5%)
  matrix products  2.28 us (2%)
  other arithmetic  1.78 us (2%)
    ppermute x6, starting transfers between devices, scan_both(): got = lax.ppermute(message, axis, pairs)  33.1 us
    ppermute x6, waiting for transfers between devices, scan_both(): got = lax.ppermute(message, axis, pairs)  32.5 us
    all_to_all x1, starting transfers between devices, scatter_sum(): lax.all_to_all(values.reshape(devices, rows // devices, cols), axis, 0, 0)  16.3 us
    all_to_all x1, waiting for transfers between devices, scatter_sum(): lax.all_to_all(values.reshape(devices, rows // devices, cols), axis, 0, 0)  4.73 us
    unnamed x11, local copies, waits for them, and re-layouts  3.06 us
  transfers between devices with their start and end apart: 7, of which 7 were waited for; matrix products, arithmetic and copies ran while one was open for 2% of the time, Pallas kernels for 0%

profile of v6, /device:TPU:1, one launch (start us, length us, event | category | flops | bytes accessed | tf_op | source)
XLA Modules:
  0.0 96.6 jit_solution(8097442057393134901)
XLA Ops:
  0.6 1.0 %reduce_window_sum.11 = f32[8,128]{1,0:T(8,128)S(1)} reduce-window(f32[8,128]{1,0:T(8,128)} %param.8, f32[]{:T(128)} %constant.12.clone.1), window={size=1x128 pad=0_0x127_0}, to_apply=%region_0.0 | reduce-window | flops 130048 | bytes 8196 | tf_op jit(solution)/shard_map/jit(cumsum)/reduce_window_sum | solution.py:69
  1.6 0.2 slice_reduce_fusion
  2.0 0.7 copy-done.3
  3.0 0.7 copy-done.2
  3.8 0.2 convolution_bitcast_fusion.1
  4.0 0.6 copy-done.1
  4.6 0.2 convolution_bitcast_fusion.2
  4.9 11.5 %collective-permute-start = (f32[257,256]{1,0:T(8,128)S(1)}, f32[257,256]{1,0:T(8,128)S(1)}, u32[]{:S(2)}, u32[]{:S(2)}) collective-permute-start(f32[257,256]{1,0:T(8,128)S(1)} %pad_maximum_fusion), channel_id=1, source_target_pairs={{0,8},{8,0},{16,24},{24,16},{32,40},{40,32},{48,56},{56,48},{64,72... | collective-permute-start | bytes 789512 | tf_op jit(solution)/shard_map/ppermute | solution.py:30
  16.4 5.3 %collective-permute-done = f32[257,256]{1,0:T(8,128)S(1)} collective-permute-done((f32[257,256]{1,0:T(8,128)S(1)}, f32[257,256]{1,0:T(8,128)S(1)}, u32[]{:S(2)}, u32[]{:S(2)}) %collective-permute-start) | collective-permute-done | bytes 263200 | tf_op jit(solution)/shard_map/ppermute | solution.py:30
  21.9 3.9 %collective-permute-start.1 = (f32[257,256]{1,0:T(8,128)S(1)}, f32[257,256]{1,0:T(8,128)S(1)}, u32[]{:S(2)}, u32[]{:S(2)}) collective-permute-start(f32[257,256]{1,0:T(8,128)S(1)} %pad_maximum_fusion.1), channel_id=1, source_target_pairs={{0,16},{8,24},{16,0},{24,8},{32,48},{40,56},{48,32},{56,40},{64,80... | collective-permute-start | bytes 789512 | tf_op jit(solution)/shard_map/ppermute | solution.py:30
  25.8 4.7 %collective-permute-done.1 = f32[257,256]{1,0:T(8,128)S(1)} collective-permute-done((f32[257,256]{1,0:T(8,128)S(1)}, f32[257,256]{1,0:T(8,128)S(1)}, u32[]{:S(2)}, u32[]{:S(2)}) %collective-permute-start.1) | collective-permute-done | bytes 263200 | tf_op jit(solution)/shard_map/ppermute | solution.py:30
  30.6 5.1 %collective-permute-start.2 = (f32[257,256]{1,0:T(8,128)S(1)}, f32[257,256]{1,0:T(8,128)S(1)}, u32[]{:S(2)}, u32[]{:S(2)}) collective-permute-start(f32[257,256]{1,0:T(8,128)S(1)} %pad_maximum_fusion.2), channel_id=1, source_target_pairs={{0,48},{8,56},{16,32},{24,40},{32,16},{40,24},{48,0},{56,8},{64,11... | collective-permute-start | bytes 789512 | tf_op jit(solution)/shard_map/ppermute | solution.py:30
  35.7 4.2 %collective-permute-done.2 = f32[257,256]{1,0:T(8,128)S(1)} collective-permute-done((f32[257,256]{1,0:T(8,128)S(1)}, f32[257,256]{1,0:T(8,128)S(1)}, u32[]{:S(2)}, u32[]{:S(2)}) %collective-permute-start.2) | collective-permute-done | bytes 263200 | tf_op jit(solution)/shard_map/ppermute | solution.py:30
  40.0 3.3 %collective-permute-start.3 = (f32[257,256]{1,0:T(8,128)S(1)}, f32[257,256]{1,0:T(8,128)S(1)}, u32[]{:S(2)}, u32[]{:S(2)}) collective-permute-start(f32[257,256]{1,0:T(8,128)S(1)} %pad_maximum_fusion.3), channel_id=1, source_target_pairs={{0,64},{8,72},{16,80},{24,88},{32,96},{40,104},{48,112},{56,120},{... | collective-permute-start | bytes 789512 | tf_op jit(solution)/shard_map/ppermute | solution.py:30
  43.5 0.3 fusion
  43.8 3.4 %collective-permute-done.3 = f32[257,256]{1,0:T(8,128)S(1)} collective-permute-done((f32[257,256]{1,0:T(8,128)S(1)}, f32[257,256]{1,0:T(8,128)S(1)}, u32[]{:S(2)}, u32[]{:S(2)}) %collective-permute-start.3) | collective-permute-done | bytes 263200 | tf_op jit(solution)/shard_map/ppermute | solution.py:30
  47.3 4.3 %collective-permute-start.4 = (f32[257,256]{1,0:T(8,128)S(1)}, f32[257,256]{1,0:T(8,128)S(1)}, u32[]{:S(2)}, u32[]{:S(2)}) collective-permute-start(f32[257,256]{1,0:T(8,128)S(1)} %pad_maximum_fusion.4), channel_id=1, source_target_pairs={{0,128},{8,136},{16,144},{24,152},{32,160},{40,168},{48,176},{56,1... | collective-permute-start | bytes 789512 | tf_op jit(solution)/shard_map/ppermute | solution.py:30
  51.7 0.2 fusion.23
  51.9 0.2 fusion.24
  52.2 10.5 %collective-permute-done.4 = f32[257,256]{1,0:T(8,128)S(1)} collective-permute-done((f32[257,256]{1,0:T(8,128)S(1)}, f32[257,256]{1,0:T(8,128)S(1)}, u32[]{:S(2)}, u32[]{:S(2)}) %collective-permute-start.4) | collective-permute-done | bytes 263200 | tf_op jit(solution)/shard_map/ppermute | solution.py:30
  62.8 5.0 %collective-permute-start.5 = (f32[129,256]{1,0:T(8,128)S(1)}, f32[129,256]{1,0:T(8,128)S(1)}, u32[]{:S(2)}, u32[]{:S(2)}) collective-permute-start(f32[129,256]{1,0:T(8,128)S(1)} %pad_maximum_fusion.5), channel_id=1, source_target_pairs={{0,448},{8,456},{16,464},{24,472},{32,480},{40,488},{48,496},{56,5... | collective-permute-start | bytes 396296 | tf_op jit(solution)/shard_map/ppermute | solution.py:26
  67.9 4.4 %collective-permute-done.5 = f32[129,256]{1,0:T(8,128)S(1)} collective-permute-done((f32[129,256]{1,0:T(8,128)S(1)}, f32[129,256]{1,0:T(8,128)S(1)}, u32[]{:S(2)}, u32[]{:S(2)}) %collective-permute-start.5) | collective-permute-done | bytes 132128 | tf_op jit(solution)/shard_map/ppermute | solution.py:26
  72.3 0.1 fusion.8
  72.5 0.2 fusion.22
  72.7 0.2 convolution_add_fusion.1
  72.8 0.3 convolution_add_fusion
  73.1 0.7 copy.18
  73.9 16.3 %all-to-all-start = ((f32[8,16,256]{2,1,0:T(8,128)}), f32[8,16,256]{2,1,0:T(8,128)S(1)}, u32[]{:S(2)}, u32[]{:S(2)}) async-start(f32[8,16,256]{2,1,0:T(8,128)} %bitcast.31), calls=%async_computation | async-start | bytes 262144 | tf_op jit(solution)/shard_map/all_to_all | solution.py:55
  90.1 0.3 fusion.2
  90.5 0.7 copy.19
  91.2 4.7 %all-to-all-done = f32[8,16,256]{2,1,0:T(8,128)S(1)} async-done(((f32[8,16,256]{2,1,0:T(8,128)}), f32[8,16,256]{2,1,0:T(8,128)S(1)}, u32[]{:S(2)}, u32[]{:S(2)}) %all-to-all-start) | async-done | bytes 131104 | tf_op jit(solution)/shard_map/all_to_all | solution.py:55
  96.0 0.6 fusion.20
  (35 shorter events, 1.4 us)
Async XLA Ops:
  0.6 3.4 %copy-start = (bf16[128,128]{1,0:T(8,128)(2,1)S(1)}, bf16[128,128]{1,0:T(8,128)(2,1)}, u32[]{:S(2)}) copy-start(bf16[128,128]{1,0:T(8,128)(2,1)} %param.6) | copy-start | bytes 98308
  1.9 0.8 copy-start.3
  3.0 0.8 copy-start.2
  3.8 0.8 copy-start.1
  4.9 16.9 %collective-permute-start = (f32[257,256]{1,0:T(8,128)S(1)}, f32[257,256]{1,0:T(8,128)S(1)}, u32[]{:S(2)}, u32[]{:S(2)}) collective-permute-start(f32[257,256]{1,0:T(8,128)S(1)} %pad_maximum_fusion), channel_id=1, source_target_pairs={{0,8},{8,0},{16,24},{24,16},{32,40},{40,32},{48,56},{56,48},{64,72... | collective-permute-start | bytes 789512 | tf_op jit(solution)/shard_map/ppermute | solution.py:30
  21.9 8.6 %collective-permute-start.1 = (f32[257,256]{1,0:T(8,128)S(1)}, f32[257,256]{1,0:T(8,128)S(1)}, u32[]{:S(2)}, u32[]{:S(2)}) collective-permute-start(f32[257,256]{1,0:T(8,128)S(1)} %pad_maximum_fusion.1), channel_id=1, source_target_pairs={{0,16},{8,24},{16,0},{24,8},{32,48},{40,56},{48,32},{56,40},{64,80... | collective-permute-start | bytes 789512 | tf_op jit(solution)/shard_map/ppermute | solution.py:30
  30.6 9.3 %collective-permute-start.2 = (f32[257,256]{1,0:T(8,128)S(1)}, f32[257,256]{1,0:T(8,128)S(1)}, u32[]{:S(2)}, u32[]{:S(2)}) collective-permute-start(f32[257,256]{1,0:T(8,128)S(1)} %pad_maximum_fusion.2), channel_id=1, source_target_pairs={{0,48},{8,56},{16,32},{24,40},{32,16},{40,24},{48,0},{56,8},{64,11... | collective-permute-start | bytes 789512 | tf_op jit(solution)/shard_map/ppermute | solution.py:30
  40.0 7.2 %collective-permute-start.3 = (f32[257,256]{1,0:T(8,128)S(1)}, f32[257,256]{1,0:T(8,128)S(1)}, u32[]{:S(2)}, u32[]{:S(2)}) collective-permute-start(f32[257,256]{1,0:T(8,128)S(1)} %pad_maximum_fusion.3), channel_id=1, source_target_pairs={{0,64},{8,72},{16,80},{24,88},{32,96},{40,104},{48,112},{56,120},{... | collective-permute-start | bytes 789512 | tf_op jit(solution)/shard_map/ppermute | solution.py:30
  47.3 15.3 %collective-permute-start.4 = (f32[257,256]{1,0:T(8,128)S(1)}, f32[257,256]{1,0:T(8,128)S(1)}, u32[]{:S(2)}, u32[]{:S(2)}) collective-permute-start(f32[257,256]{1,0:T(8,128)S(1)} %pad_maximum_fusion.4), channel_id=1, source_target_pairs={{0,128},{8,136},{16,144},{24,152},{32,160},{40,168},{48,176},{56,1... | collective-permute-start | bytes 789512 | tf_op jit(solution)/shard_map/ppermute | solution.py:30
  62.8 9.6 %collective-permute-start.5 = (f32[129,256]{1,0:T(8,128)S(1)}, f32[129,256]{1,0:T(8,128)S(1)}, u32[]{:S(2)}, u32[]{:S(2)}) collective-permute-start(f32[129,256]{1,0:T(8,128)S(1)} %pad_maximum_fusion.5), channel_id=1, source_target_pairs={{0,448},{8,456},{16,464},{24,472},{32,480},{40,488},{48,496},{56,5... | collective-permute-start | bytes 396296 | tf_op jit(solution)/shard_map/ppermute | solution.py:26
  73.9 22.1 %all-to-all-start = ((f32[8,16,256]{2,1,0:T(8,128)}), f32[8,16,256]{2,1,0:T(8,128)S(1)}, u32[]{:S(2)}, u32[]{:S(2)}) async-start(f32[8,16,256]{2,1,0:T(8,128)} %bitcast.31), calls=%async_computation | async-start | bytes 262144 | tf_op jit(solution)/shard_map/all_to_all | solution.py:55

commit v7 on v6

--- a/solution.py
+++ b/solution.py
@@ -66,7 +66,8 @@
     length, feature_width = head_inputs.shape
     head_count = log_decay.shape[0]
     head_size = feature_width // head_count
-    cumulative = jnp.cumsum(log_decay, axis=1)
+    upper = (jnp.arange(length)[:, None] <= jnp.arange(length)[None, :]).astype(jnp.float32)
+    cumulative = jnp.dot(log_decay, upper, precision=lax.Precision.HIGHEST)
     block_end = cumulative[:, -1:]
     forward_w = jnp.exp(block_end - cumulative)
     backward_w = jnp.exp(cumulative)

time: 97.1 us -> 97 us (level)
  other arithmetic: 1.78 us -> 0.8 us
    another operation x1 -> x0, other arithmetic: 0.97 us -> none  [per_device(): cumulative = jnp.cumsum(log_decay, axis=1)]
where the time goes in v7:
time: 97 us; the launch traced here: 96.5 us
  starting transfers between devices  49.4 us (51%)
  waiting for transfers between devices  37.3 us (38%)
  local copies, waits for them, and re-layouts  4.97 us (5%)
  matrix products  3.1 us (3%)
    ppermute x6, starting transfers between devices, scan_both(): got = lax.ppermute(message, axis, pairs)  33.1 us
    ppermute x6, waiting for transfers between devices, scan_both(): got = lax.ppermute(message, axis, pairs)  32.5 us
    all_to_all x1, starting transfers between devices, scatter_sum(): lax.all_to_all(values.reshape(devices, rows // devices, cols), axis, 0, 0)  16.3 us
    all_to_all x1, waiting for transfers between devices, scatter_sum(): lax.all_to_all(values.reshape(devices, rows // devices, cols), axis, 0, 0)  4.73 us
    unnamed x11, local copies, waits for them, and re-layouts  3.06 us
  transfers between devices with their start and end apart: 7, of which 7 were waited for; matrix products, arithmetic and copies ran while one was open for 2% of the time, Pallas kernels for 0%

profile of v7, /device:TPU:1, one launch (start us, length us, event | category | flops | bytes accessed | tf_op | source)
XLA Modules:
  0.0 96.5 jit_solution(9058983615403439112)
XLA Ops:
  0.6 0.8 fusion.18
  1.5 0.2 slice_reduce_fusion
  1.9 0.7 copy-done.3
  2.9 0.7 copy-done.2
  3.7 0.2 convolution_bitcast_fusion.1
  3.9 0.6 copy-done.1
  4.5 0.2 convolution_bitcast_fusion.2
  4.7 11.5 %collective-permute-start = (f32[257,256]{1,0:T(8,128)S(1)}, f32[257,256]{1,0:T(8,128)S(1)}, u32[]{:S(2)}, u32[]{:S(2)}) collective-permute-start(f32[257,256]{1,0:T(8,128)S(1)} %pad_maximum_fusion), channel_id=1, source_target_pairs={{0,8},{8,0},{16,24},{24,16},{32,40},{40,32},{48,56},{56,48},{64,72... | collective-permute-start | bytes 789512 | tf_op jit(solution)/shard_map/ppermute | solution.py:30
  16.3 5.3 %collective-permute-done = f32[257,256]{1,0:T(8,128)S(1)} collective-permute-done((f32[257,256]{1,0:T(8,128)S(1)}, f32[257,256]{1,0:T(8,128)S(1)}, u32[]{:S(2)}, u32[]{:S(2)}) %collective-permute-start) | collective-permute-done | bytes 263200 | tf_op jit(solution)/shard_map/ppermute | solution.py:30
  21.8 3.9 %collective-permute-start.1 = (f32[257,256]{1,0:T(8,128)S(1)}, f32[257,256]{1,0:T(8,128)S(1)}, u32[]{:S(2)}, u32[]{:S(2)}) collective-permute-start(f32[257,256]{1,0:T(8,128)S(1)} %pad_maximum_fusion.1), channel_id=1, source_target_pairs={{0,16},{8,24},{16,0},{24,8},{32,48},{40,56},{48,32},{56,40},{64,80... | collective-permute-start | bytes 789512 | tf_op jit(solution)/shard_map/ppermute | solution.py:30
  25.7 4.7 %collective-permute-done.1 = f32[257,256]{1,0:T(8,128)S(1)} collective-permute-done((f32[257,256]{1,0:T(8,128)S(1)}, f32[257,256]{1,0:T(8,128)S(1)}, u32[]{:S(2)}, u32[]{:S(2)}) %collective-permute-start.1) | collective-permute-done | bytes 263200 | tf_op jit(solution)/shard_map/ppermute | solution.py:30
  30.4 5.1 %collective-permute-start.2 = (f32[257,256]{1,0:T(8,128)S(1)}, f32[257,256]{1,0:T(8,128)S(1)}, u32[]{:S(2)}, u32[]{:S(2)}) collective-permute-start(f32[257,256]{1,0:T(8,128)S(1)} %pad_maximum_fusion.2), channel_id=1, source_target_pairs={{0,48},{8,56},{16,32},{24,40},{32,16},{40,24},{48,0},{56,8},{64,11... | collective-permute-start | bytes 789512 | tf_op jit(solution)/shard_map/ppermute | solution.py:30
  35.5 4.2 %collective-permute-done.2 = f32[257,256]{1,0:T(8,128)S(1)} collective-permute-done((f32[257,256]{1,0:T(8,128)S(1)}, f32[257,256]{1,0:T(8,128)S(1)}, u32[]{:S(2)}, u32[]{:S(2)}) %collective-permute-start.2) | collective-permute-done | bytes 263200 | tf_op jit(solution)/shard_map/ppermute | solution.py:30
  39.9 3.3 %collective-permute-start.3 = (f32[257,256]{1,0:T(8,128)S(1)}, f32[257,256]{1,0:T(8,128)S(1)}, u32[]{:S(2)}, u32[]{:S(2)}) collective-permute-start(f32[257,256]{1,0:T(8,128)S(1)} %pad_maximum_fusion.3), channel_id=1, source_target_pairs={{0,64},{8,72},{16,80},{24,88},{32,96},{40,104},{48,112},{56,120},{... | collective-permute-start | bytes 789512 | tf_op jit(solution)/shard_map/ppermute | solution.py:30
  43.4 0.3 fusion
  43.7 3.4 %collective-permute-done.3 = f32[257,256]{1,0:T(8,128)S(1)} collective-permute-done((f32[257,256]{1,0:T(8,128)S(1)}, f32[257,256]{1,0:T(8,128)S(1)}, u32[]{:S(2)}, u32[]{:S(2)}) %collective-permute-start.3) | collective-permute-done | bytes 263200 | tf_op jit(solution)/shard_map/ppermute | solution.py:30
  47.2 4.3 %collective-permute-start.4 = (f32[257,256]{1,0:T(8,128)S(1)}, f32[257,256]{1,0:T(8,128)S(1)}, u32[]{:S(2)}, u32[]{:S(2)}) collective-permute-start(f32[257,256]{1,0:T(8,128)S(1)} %pad_maximum_fusion.4), channel_id=1, source_target_pairs={{0,128},{8,136},{16,144},{24,152},{32,160},{40,168},{48,176},{56,1... | collective-permute-start | bytes 789512 | tf_op jit(solution)/shard_map/ppermute | solution.py:30
  51.6 0.2 fusion.25
  51.8 0.2 fusion.26
  52.1 10.5 %collective-permute-done.4 = f32[257,256]{1,0:T(8,128)S(1)} collective-permute-done((f32[257,256]{1,0:T(8,128)S(1)}, f32[257,256]{1,0:T(8,128)S(1)}, u32[]{:S(2)}, u32[]{:S(2)}) %collective-permute-start.4) | collective-permute-done | bytes 263200 | tf_op jit(solution)/shard_map/ppermute | solution.py:30
  62.6 5.0 %collective-permute-start.5 = (f32[129,256]{1,0:T(8,128)S(1)}, f32[129,256]{1,0:T(8,128)S(1)}, u32[]{:S(2)}, u32[]{:S(2)}) collective-permute-start(f32[129,256]{1,0:T(8,128)S(1)} %pad_maximum_fusion.5), channel_id=1, source_target_pairs={{0,448},{8,456},{16,464},{24,472},{32,480},{40,488},{48,496},{56,5... | collective-permute-start | bytes 396296 | tf_op jit(solution)/shard_map/ppermute | solution.py:26
  67.8 4.4 %collective-permute-done.5 = f32[129,256]{1,0:T(8,128)S(1)} collective-permute-done((f32[129,256]{1,0:T(8,128)S(1)}, f32[129,256]{1,0:T(8,128)S(1)}, u32[]{:S(2)}, u32[]{:S(2)}) %collective-permute-start.5) | collective-permute-done | bytes 132128 | tf_op jit(solution)/shard_map/ppermute | solution.py:26
  72.2 0.1 fusion.8
  72.4 0.2 fusion.24
  72.5 0.2 convolution_add_fusion.1
  72.7 0.3 convolution_add_fusion
  73.0 0.8 copy.18
  73.8 16.3 %all-to-all-start = ((f32[8,16,256]{2,1,0:T(8,128)}), f32[8,16,256]{2,1,0:T(8,128)S(1)}, u32[]{:S(2)}, u32[]{:S(2)}) async-start(f32[8,16,256]{2,1,0:T(8,128)} %bitcast.30), calls=%async_computation | async-start | bytes 262144 | tf_op jit(solution)/shard_map/all_to_all | solution.py:55
  90.0 0.3 fusion.2
  90.4 0.7 copy.19
  91.1 4.7 %all-to-all-done = f32[8,16,256]{2,1,0:T(8,128)S(1)} async-done(((f32[8,16,256]{2,1,0:T(8,128)}), f32[8,16,256]{2,1,0:T(8,128)S(1)}, u32[]{:S(2)}, u32[]{:S(2)}) %all-to-all-start) | async-done | bytes 131104 | tf_op jit(solution)/shard_map/all_to_all | solution.py:55
  95.9 0.6 fusion.21
  (35 shorter events, 1.4 us)
Async XLA Ops:
  0.6 3.2 %copy-start = (bf16[128,128]{1,0:T(8,128)(2,1)S(1)}, bf16[128,128]{1,0:T(8,128)(2,1)}, u32[]{:S(2)}) copy-start(bf16[128,128]{1,0:T(8,128)(2,1)} %param.6) | copy-start | bytes 98308
  1.8 0.8 copy-start.3
  2.9 0.8 copy-start.2
  3.7 0.8 copy-start.1
  4.7 16.9 %collective-permute-start = (f32[257,256]{1,0:T(8,128)S(1)}, f32[257,256]{1,0:T(8,128)S(1)}, u32[]{:S(2)}, u32[]{:S(2)}) collective-permute-start(f32[257,256]{1,0:T(8,128)S(1)} %pad_maximum_fusion), channel_id=1, source_target_pairs={{0,8},{8,0},{16,24},{24,16},{32,40},{40,32},{48,56},{56,48},{64,72... | collective-permute-start | bytes 789512 | tf_op jit(solution)/shard_map/ppermute | solution.py:30
  21.8 8.6 %collective-permute-start.1 = (f32[257,256]{1,0:T(8,128)S(1)}, f32[257,256]{1,0:T(8,128)S(1)}, u32[]{:S(2)}, u32[]{:S(2)}) collective-permute-start(f32[257,256]{1,0:T(8,128)S(1)} %pad_maximum_fusion.1), channel_id=1, source_target_pairs={{0,16},{8,24},{16,0},{24,8},{32,48},{40,56},{48,32},{56,40},{64,80... | collective-permute-start | bytes 789512 | tf_op jit(solution)/shard_map/ppermute | solution.py:30
  30.4 9.3 %collective-permute-start.2 = (f32[257,256]{1,0:T(8,128)S(1)}, f32[257,256]{1,0:T(8,128)S(1)}, u32[]{:S(2)}, u32[]{:S(2)}) collective-permute-start(f32[257,256]{1,0:T(8,128)S(1)} %pad_maximum_fusion.2), channel_id=1, source_target_pairs={{0,48},{8,56},{16,32},{24,40},{32,16},{40,24},{48,0},{56,8},{64,11... | collective-permute-start | bytes 789512 | tf_op jit(solution)/shard_map/ppermute | solution.py:30
  39.9 7.2 %collective-permute-start.3 = (f32[257,256]{1,0:T(8,128)S(1)}, f32[257,256]{1,0:T(8,128)S(1)}, u32[]{:S(2)}, u32[]{:S(2)}) collective-permute-start(f32[257,256]{1,0:T(8,128)S(1)} %pad_maximum_fusion.3), channel_id=1, source_target_pairs={{0,64},{8,72},{16,80},{24,88},{32,96},{40,104},{48,112},{56,120},{... | collective-permute-start | bytes 789512 | tf_op jit(solution)/shard_map/ppermute | solution.py:30
  47.2 15.3 %collective-permute-start.4 = (f32[257,256]{1,0:T(8,128)S(1)}, f32[257,256]{1,0:T(8,128)S(1)}, u32[]{:S(2)}, u32[]{:S(2)}) collective-permute-start(f32[257,256]{1,0:T(8,128)S(1)} %pad_maximum_fusion.4), channel_id=1, source_target_pairs={{0,128},{8,136},{16,144},{24,152},{32,160},{40,168},{48,176},{56,1... | collective-permute-start | bytes 789512 | tf_op jit(solution)/shard_map/ppermute | solution.py:30
  62.6 9.6 %collective-permute-start.5 = (f32[129,256]{1,0:T(8,128)S(1)}, f32[129,256]{1,0:T(8,128)S(1)}, u32[]{:S(2)}, u32[]{:S(2)}) collective-permute-start(f32[129,256]{1,0:T(8,128)S(1)} %pad_maximum_fusion.5), channel_id=1, source_target_pairs={{0,448},{8,456},{16,464},{24,472},{32,480},{40,488},{48,496},{56,5... | collective-permute-start | bytes 396296 | tf_op jit(solution)/shard_map/ppermute | solution.py:26
  73.8 22.1 %all-to-all-start = ((f32[8,16,256]{2,1,0:T(8,128)}), f32[8,16,256]{2,1,0:T(8,128)S(1)}, u32[]{:S(2)}, u32[]{:S(2)}) async-start(f32[8,16,256]{2,1,0:T(8,128)} %bitcast.30), calls=%async_computation | async-start | bytes 262144 | tf_op jit(solution)/shard_map/all_to_all | solution.py:55

commit v8 on v6

--- a/solution.py
+++ b/solution.py
@@ -73,8 +73,12 @@
     weighted_inputs = heads_scaled(head_inputs, forward_w)
     weighted_grads = heads_scaled(out_grad, backward_w)
     through = jnp.repeat(jnp.exp(block_end[:, 0]), head_size)
-    own_state = jnp.dot(write_keys.T, weighted_inputs, preferred_element_type=jnp.float32)
-    own_grad = jnp.dot(read_queries.T, weighted_grads, preferred_element_type=jnp.float32)
+    own_state, own_grad = jnp.einsum(
+        "kpn,kpc->knc",
+        jnp.stack([write_keys, read_queries]),
+        jnp.stack([weighted_inputs, weighted_grads]),
+        preferred_element_type=jnp.float32,
+    )
 
     entry, exit_ = scan_both(through, own_state, own_grad, "ctx")
     entry_bf = entry.astype(jnp.bfloat16)

time: 97.1 us -> 96.3 us (level)
    unnamed x11 -> x13, local copies, waits for them, and re-layouts: 3.06 us -> 2.47 us
where the time goes in v8:
time: 96.3 us; the launch traced here: 95.8 us
  starting transfers between devices  49.4 us (51%)
  waiting for transfers between devices  37.1 us (39%)
  local copies, waits for them, and re-layouts  4.48 us (5%)
  matrix products  2.06 us (2%)
  other arithmetic  1.79 us (2%)
    ppermute x6, starting transfers between devices, scan_both(): got = lax.ppermute(message, axis, pairs)  33.1 us
    ppermute x6, waiting for transfers between devices, scan_both(): got = lax.ppermute(message, axis, pairs)  32.4 us
    all_to_all x1, starting transfers between devices, scatter_sum(): lax.all_to_all(values.reshape(devices, rows // devices, cols), axis, 0, 0)  16.3 us
    all_to_all x1, waiting for transfers between devices, scatter_sum(): lax.all_to_all(values.reshape(devices, rows // devices, cols), axis, 0, 0)  4.73 us
    unnamed x13, local copies, waits for them, and re-layouts  2.47 us
  transfers between devices with their start and end apart: 7, of which 7 were waited for; matrix products, arithmetic and copies ran while one was open for 2% of the time, Pallas kernels for 0%

profile of v8, /device:TPU:1, one launch (start us, length us, event | category | flops | bytes accessed | tf_op | source)
XLA Modules:
  0.0 95.8 jit_solution(412869002431684408)
XLA Ops:
  0.6 1.0 %reduce_window_sum.11 = f32[8,128]{1,0:T(8,128)S(1)} reduce-window(f32[8,128]{1,0:T(8,128)} %param.8, f32[]{:T(128)} %constant.12.clone.1), window={size=1x128 pad=0_0x127_0}, to_apply=%region_0.0 | reduce-window | flops 130048 | bytes 8196 | tf_op jit(solution)/shard_map/jit(cumsum)/reduce_window_sum | solution.py:69
  1.6 0.2 slice_reduce_fusion
  2.1 0.6 copy-done.1
  3.0 0.6 copy-done
  3.7 0.2 fusion.10
  4.1 11.5 %collective-permute-start = (f32[257,256]{1,0:T(8,128)S(1)}, f32[257,256]{1,0:T(8,128)S(1)}, u32[]{:S(2)}, u32[]{:S(2)}) collective-permute-start(f32[257,256]{1,0:T(8,128)S(1)} %pad_maximum_fusion), channel_id=1, source_target_pairs={{0,8},{8,0},{16,24},{24,16},{32,40},{40,32},{48,56},{56,48},{64,72... | collective-permute-start | bytes 789512 | tf_op jit(solution)/shard_map/ppermute | solution.py:30
  15.6 5.3 %collective-permute-done = f32[257,256]{1,0:T(8,128)S(1)} collective-permute-done((f32[257,256]{1,0:T(8,128)S(1)}, f32[257,256]{1,0:T(8,128)S(1)}, u32[]{:S(2)}, u32[]{:S(2)}) %collective-permute-start) | collective-permute-done | bytes 263200 | tf_op jit(solution)/shard_map/ppermute | solution.py:30
  21.1 3.9 %collective-permute-start.1 = (f32[257,256]{1,0:T(8,128)S(1)}, f32[257,256]{1,0:T(8,128)S(1)}, u32[]{:S(2)}, u32[]{:S(2)}) collective-permute-start(f32[257,256]{1,0:T(8,128)S(1)} %pad_maximum_fusion.1), channel_id=1, source_target_pairs={{0,16},{8,24},{16,0},{24,8},{32,48},{40,56},{48,32},{56,40},{64,80... | collective-permute-start | bytes 789512 | tf_op jit(solution)/shard_map/ppermute | solution.py:30
  25.0 4.7 %collective-permute-done.1 = f32[257,256]{1,0:T(8,128)S(1)} collective-permute-done((f32[257,256]{1,0:T(8,128)S(1)}, f32[257,256]{1,0:T(8,128)S(1)}, u32[]{:S(2)}, u32[]{:S(2)}) %collective-permute-start.1) | collective-permute-done | bytes 263200 | tf_op jit(solution)/shard_map/ppermute | solution.py:30
  29.8 5.1 %collective-permute-start.2 = (f32[257,256]{1,0:T(8,128)S(1)}, f32[257,256]{1,0:T(8,128)S(1)}, u32[]{:S(2)}, u32[]{:S(2)}) collective-permute-start(f32[257,256]{1,0:T(8,128)S(1)} %pad_maximum_fusion.2), channel_id=1, source_target_pairs={{0,48},{8,56},{16,32},{24,40},{32,16},{40,24},{48,0},{56,8},{64,11... | collective-permute-start | bytes 789512 | tf_op jit(solution)/shard_map/ppermute | solution.py:30
  34.9 4.2 %collective-permute-done.2 = f32[257,256]{1,0:T(8,128)S(1)} collective-permute-done((f32[257,256]{1,0:T(8,128)S(1)}, f32[257,256]{1,0:T(8,128)S(1)}, u32[]{:S(2)}, u32[]{:S(2)}) %collective-permute-start.2) | collective-permute-done | bytes 263200 | tf_op jit(solution)/shard_map/ppermute | solution.py:30
  39.2 3.3 %collective-permute-start.3 = (f32[257,256]{1,0:T(8,128)S(1)}, f32[257,256]{1,0:T(8,128)S(1)}, u32[]{:S(2)}, u32[]{:S(2)}) collective-permute-start(f32[257,256]{1,0:T(8,128)S(1)} %pad_maximum_fusion.3), channel_id=1, source_target_pairs={{0,64},{8,72},{16,80},{24,88},{32,96},{40,104},{48,112},{56,120},{... | collective-permute-start | bytes 789512 | tf_op jit(solution)/shard_map/ppermute | solution.py:30
  42.7 0.1 copy.21
  42.8 0.3 fusion
  43.2 3.3 %collective-permute-done.3 = f32[257,256]{1,0:T(8,128)S(1)} collective-permute-done((f32[257,256]{1,0:T(8,128)S(1)}, f32[257,256]{1,0:T(8,128)S(1)}, u32[]{:S(2)}, u32[]{:S(2)}) %collective-permute-start.3) | collective-permute-done | bytes 263200 | tf_op jit(solution)/shard_map/ppermute | solution.py:30
  46.5 4.3 %collective-permute-start.4 = (f32[257,256]{1,0:T(8,128)S(1)}, f32[257,256]{1,0:T(8,128)S(1)}, u32[]{:S(2)}, u32[]{:S(2)}) collective-permute-start(f32[257,256]{1,0:T(8,128)S(1)} %pad_maximum_fusion.4), channel_id=1, source_target_pairs={{0,128},{8,136},{16,144},{24,152},{32,160},{40,168},{48,176},{56,1... | collective-permute-start | bytes 789512 | tf_op jit(solution)/shard_map/ppermute | solution.py:30
  50.9 0.2 fusion.32
  51.1 0.2 fusion.33
  51.4 10.5 %collective-permute-done.4 = f32[257,256]{1,0:T(8,128)S(1)} collective-permute-done((f32[257,256]{1,0:T(8,128)S(1)}, f32[257,256]{1,0:T(8,128)S(1)}, u32[]{:S(2)}, u32[]{:S(2)}) %collective-permute-start.4) | collective-permute-done | bytes 263200 | tf_op jit(solution)/shard_map/ppermute | solution.py:30
  62.0 5.0 %collective-permute-start.5 = (f32[129,256]{1,0:T(8,128)S(1)}, f32[129,256]{1,0:T(8,128)S(1)}, u32[]{:S(2)}, u32[]{:S(2)}) collective-permute-start(f32[129,256]{1,0:T(8,128)S(1)} %pad_maximum_fusion.5), channel_id=1, source_target_pairs={{0,448},{8,456},{16,464},{24,472},{32,480},{40,488},{48,496},{56,5... | collective-permute-start | bytes 396296 | tf_op jit(solution)/shard_map/ppermute | solution.py:26
  67.0 0.1 fusion.30
  67.1 4.4 %collective-permute-done.5 = f32[129,256]{1,0:T(8,128)S(1)} collective-permute-done((f32[129,256]{1,0:T(8,128)S(1)}, f32[129,256]{1,0:T(8,128)S(1)}, u32[]{:S(2)}, u32[]{:S(2)}) %collective-permute-start.5) | collective-permute-done | bytes 132128 | tf_op jit(solution)/shard_map/ppermute | solution.py:26
  71.5 0.1 fusion.8
  71.7 0.2 fusion.31
  71.9 0.2 convolution_add_fusion.1
  72.0 0.3 convolution_add_fusion
  72.3 0.8 copy.22
  73.1 16.3 %all-to-all-start = ((f32[8,16,256]{2,1,0:T(8,128)}), f32[8,16,256]{2,1,0:T(8,128)S(1)}, u32[]{:S(2)}, u32[]{:S(2)}) async-start(f32[8,16,256]{2,1,0:T(8,128)} %bitcast.35), calls=%async_computation | async-start | bytes 262144 | tf_op jit(solution)/shard_map/all_to_all | solution.py:55
  89.4 0.3 fusion.2
  89.7 0.7 copy.23
  90.4 4.7 %all-to-all-done = f32[8,16,256]{2,1,0:T(8,128)S(1)} async-done(((f32[8,16,256]{2,1,0:T(8,128)}), f32[8,16,256]{2,1,0:T(8,128)S(1)}, u32[]{:S(2)}, u32[]{:S(2)}) %all-to-all-start) | async-done | bytes 131104 | tf_op jit(solution)/shard_map/all_to_all | solution.py:55
  95.2 0.6 fusion.29
  (39 shorter events, 1.5 us)
Async XLA Ops:
  2.0 0.8 copy-start.1
  2.0 0.9 copy-start.2
  2.8 0.8 copy-start
  2.8 0.9 copy-start.3
  4.1 16.9 %collective-permute-start = (f32[257,256]{1,0:T(8,128)S(1)}, f32[257,256]{1,0:T(8,128)S(1)}, u32[]{:S(2)}, u32[]{:S(2)}) collective-permute-start(f32[257,256]{1,0:T(8,128)S(1)} %pad_maximum_fusion), channel_id=1, source_target_pairs={{0,8},{8,0},{16,24},{24,16},{32,40},{40,32},{48,56},{56,48},{64,72... | collective-permute-start | bytes 789512 | tf_op jit(solution)/shard_map/ppermute | solution.py:30
  21.1 8.6 %collective-permute-start.1 = (f32[257,256]{1,0:T(8,128)S(1)}, f32[257,256]{1,0:T(8,128)S(1)}, u32[]{:S(2)}, u32[]{:S(2)}) collective-permute-start(f32[257,256]{1,0:T(8,128)S(1)} %pad_maximum_fusion.1), channel_id=1, source_target_pairs={{0,16},{8,24},{16,0},{24,8},{32,48},{40,56},{48,32},{56,40},{64,80... | collective-permute-start | bytes 789512 | tf_op jit(solution)/shard_map/ppermute | solution.py:30
  29.8 9.3 %collective-permute-start.2 = (f32[257,256]{1,0:T(8,128)S(1)}, f32[257,256]{1,0:T(8,128)S(1)}, u32[]{:S(2)}, u32[]{:S(2)}) collective-permute-start(f32[257,256]{1,0:T(8,128)S(1)} %pad_maximum_fusion.2), channel_id=1, source_target_pairs={{0,48},{8,56},{16,32},{24,40},{32,16},{40,24},{48,0},{56,8},{64,11... | collective-permute-start | bytes 789512 | tf_op jit(solution)/shard_map/ppermute | solution.py:30
  39.2 7.2 %collective-permute-start.3 = (f32[257,256]{1,0:T(8,128)S(1)}, f32[257,256]{1,0:T(8,128)S(1)}, u32[]{:S(2)}, u32[]{:S(2)}) collective-permute-start(f32[257,256]{1,0:T(8,128)S(1)} %pad_maximum_fusion.3), channel_id=1, source_target_pairs={{0,64},{8,72},{16,80},{24,88},{32,96},{40,104},{48,112},{56,120},{... | collective-permute-start | bytes 789512 | tf_op jit(solution)/shard_map/ppermute | solution.py:30
  46.5 15.3 %collective-permute-start.4 = (f32[257,256]{1,0:T(8,128)S(1)}, f32[257,256]{1,0:T(8,128)S(1)}, u32[]{:S(2)}, u32[]{:S(2)}) collective-permute-start(f32[257,256]{1,0:T(8,128)S(1)} %pad_maximum_fusion.4), channel_id=1, source_target_pairs={{0,128},{8,136},{16,144},{24,152},{32,160},{40,168},{48,176},{56,1... | collective-permute-start | bytes 789512 | tf_op jit(solution)/shard_map/ppermute | solution.py:30
  62.0 9.6 %collective-permute-start.5 = (f32[129,256]{1,0:T(8,128)S(1)}, f32[129,256]{1,0:T(8,128)S(1)}, u32[]{:S(2)}, u32[]{:S(2)}) collective-permute-start(f32[129,256]{1,0:T(8,128)S(1)} %pad_maximum_fusion.5), channel_id=1, source_target_pairs={{0,448},{8,456},{16,464},{24,472},{32,480},{40,488},{48,496},{56,5... | collective-permute-start | bytes 396296 | tf_op jit(solution)/shard_map/ppermute | solution.py:26
  73.1 22.1 %all-to-all-start = ((f32[8,16,256]{2,1,0:T(8,128)}), f32[8,16,256]{2,1,0:T(8,128)S(1)}, u32[]{:S(2)}, u32[]{:S(2)}) async-start(f32[8,16,256]{2,1,0:T(8,128)} %bitcast.35), calls=%async_computation | async-start | bytes 262144 | tf_op jit(solution)/shard_map/all_to_all | solution.py:55

commit v9 on v8

--- a/solution.py
+++ b/solution.py
@@ -64,6 +64,13 @@
 
 def per_device(head_inputs, write_keys, read_queries, log_decay, out_grad):
     length, feature_width = head_inputs.shape
+    states = write_keys.shape[1]
+    packed = lax.optimization_barrier(
+        jnp.concatenate([head_inputs, out_grad, write_keys, read_queries], axis=1)
+    )
+    head_inputs, out_grad, write_keys, read_queries = jnp.split(
+        packed, [feature_width, 2 * feature_width, 2 * feature_width + states], axis=1
+    )
     head_count = log_decay.shape[0]
     head_size = feature_width // head_count
     cumulative = jnp.cumsum(log_decay, axis=1)
@@ -116,7 +123,6 @@
     read_state = jnp.dot(weighted_grads, entry_bf.T, preferred_element_type=jnp.float32)
     both = jnp.concatenate([write_mix + write_state, read_mix + read_state], axis=1)
     summed = scatter_sum(both, "head")
-    states = write_keys.shape[1]
     write_sum, read_sum = summed[:, :states], summed[:, states:]
     return (input_grad, write_sum.astype(jnp.bfloat16), read_sum.astype(jnp.bfloat16))
 

time: 96.3 us -> 95.6 us (level)
    unnamed x13 -> x9, local copies, waits for them, and re-layouts: 2.47 us -> 1.49 us
where the time goes in v9:
time: 95.6 us; the launch traced here: 95.2 us
  starting transfers between devices  49.4 us (52%)
  waiting for transfers between devices  37.1 us (39%)
  local copies, waits for them, and re-layouts  3.76 us (4%)
  matrix products  2.13 us (2%)
  other arithmetic  1.8 us (2%)
    ppermute x6, starting transfers between devices, scan_both(): got = lax.ppermute(message, axis, pairs)  33.1 us
    ppermute x6, waiting for transfers between devices, scan_both(): got = lax.ppermute(message, axis, pairs)  32.4 us
    all_to_all x1, starting transfers between devices, scatter_sum(): lax.all_to_all(values.reshape(devices, rows // devices, cols), axis, 0, 0)  16.3 us
    all_to_all x1, waiting for transfers between devices, scatter_sum(): lax.all_to_all(values.reshape(devices, rows // devices, cols), axis, 0, 0)  4.73 us
  transfers between devices with their start and end apart: 7, of which 7 were waited for; matrix products, arithmetic and copies ran while one was open for 2% of the time, Pallas kernels for 0%

profile of v9, /device:TPU:1, one launch (start us, length us, event | category | flops | bytes accessed | tf_op | source)
XLA Modules:
  0.0 95.2 jit_solution(7258272373248658548)
XLA Ops:
  0.6 1.0 %reduce_window_sum.11 = f32[8,128]{1,0:T(8,128)S(1)} reduce-window(f32[8,128]{1,0:T(8,128)} %param.8, f32[]{:T(128)} %constant.12.clone.1), window={size=1x128 pad=0_0x127_0}, to_apply=%region_0.0 | reduce-window | flops 130048 | bytes 8196 | tf_op jit(solution)/shard_map/jit(cumsum)/reduce_window_sum | solution.py:76
  1.6 0.2 slice_reduce_fusion
  2.2 0.7 copy-done
  3.0 0.2 fusion.10
  3.4 11.5 %collective-permute-start = (f32[257,256]{1,0:T(8,128)S(1)}, f32[257,256]{1,0:T(8,128)S(1)}, u32[]{:S(2)}, u32[]{:S(2)}) collective-permute-start(f32[257,256]{1,0:T(8,128)S(1)} %pad_maximum_fusion), channel_id=1, source_target_pairs={{0,8},{8,0},{16,24},{24,16},{32,40},{40,32},{48,56},{56,48},{64,72... | collective-permute-start | bytes 789512 | tf_op jit(solution)/shard_map/ppermute | solution.py:30
  15.0 5.3 %collective-permute-done = f32[257,256]{1,0:T(8,128)S(1)} collective-permute-done((f32[257,256]{1,0:T(8,128)S(1)}, f32[257,256]{1,0:T(8,128)S(1)}, u32[]{:S(2)}, u32[]{:S(2)}) %collective-permute-start) | collective-permute-done | bytes 263200 | tf_op jit(solution)/shard_map/ppermute | solution.py:30
  20.4 3.9 %collective-permute-start.1 = (f32[257,256]{1,0:T(8,128)S(1)}, f32[257,256]{1,0:T(8,128)S(1)}, u32[]{:S(2)}, u32[]{:S(2)}) collective-permute-start(f32[257,256]{1,0:T(8,128)S(1)} %pad_maximum_fusion.1), channel_id=1, source_target_pairs={{0,16},{8,24},{16,0},{24,8},{32,48},{40,56},{48,32},{56,40},{64,80... | collective-permute-start | bytes 789512 | tf_op jit(solution)/shard_map/ppermute | solution.py:30
  24.3 4.7 %collective-permute-done.1 = f32[257,256]{1,0:T(8,128)S(1)} collective-permute-done((f32[257,256]{1,0:T(8,128)S(1)}, f32[257,256]{1,0:T(8,128)S(1)}, u32[]{:S(2)}, u32[]{:S(2)}) %collective-permute-start.1) | collective-permute-done | bytes 263200 | tf_op jit(solution)/shard_map/ppermute | solution.py:30
  29.1 5.1 %collective-permute-start.2 = (f32[257,256]{1,0:T(8,128)S(1)}, f32[257,256]{1,0:T(8,128)S(1)}, u32[]{:S(2)}, u32[]{:S(2)}) collective-permute-start(f32[257,256]{1,0:T(8,128)S(1)} %pad_maximum_fusion.2), channel_id=1, source_target_pairs={{0,48},{8,56},{16,32},{24,40},{32,16},{40,24},{48,0},{56,8},{64,11... | collective-permute-start | bytes 789512 | tf_op jit(solution)/shard_map/ppermute | solution.py:30
  34.2 4.2 %collective-permute-done.2 = f32[257,256]{1,0:T(8,128)S(1)} collective-permute-done((f32[257,256]{1,0:T(8,128)S(1)}, f32[257,256]{1,0:T(8,128)S(1)}, u32[]{:S(2)}, u32[]{:S(2)}) %collective-permute-start.2) | collective-permute-done | bytes 263200 | tf_op jit(solution)/shard_map/ppermute | solution.py:30
  38.5 3.3 %collective-permute-start.3 = (f32[257,256]{1,0:T(8,128)S(1)}, f32[257,256]{1,0:T(8,128)S(1)}, u32[]{:S(2)}, u32[]{:S(2)}) collective-permute-start(f32[257,256]{1,0:T(8,128)S(1)} %pad_maximum_fusion.3), channel_id=1, source_target_pairs={{0,64},{8,72},{16,80},{24,88},{32,96},{40,104},{48,112},{56,120},{... | collective-permute-start | bytes 789512 | tf_op jit(solution)/shard_map/ppermute | solution.py:30
  41.9 0.1 copy.15
  42.0 0.1 copy.20
  42.2 0.3 fusion
  42.5 3.2 %collective-permute-done.3 = f32[257,256]{1,0:T(8,128)S(1)} collective-permute-done((f32[257,256]{1,0:T(8,128)S(1)}, f32[257,256]{1,0:T(8,128)S(1)}, u32[]{:S(2)}, u32[]{:S(2)}) %collective-permute-start.3) | collective-permute-done | bytes 263200 | tf_op jit(solution)/shard_map/ppermute | solution.py:30
  45.9 4.3 %collective-permute-start.4 = (f32[257,256]{1,0:T(8,128)S(1)}, f32[257,256]{1,0:T(8,128)S(1)}, u32[]{:S(2)}, u32[]{:S(2)}) collective-permute-start(f32[257,256]{1,0:T(8,128)S(1)} %pad_maximum_fusion.4), channel_id=1, source_target_pairs={{0,128},{8,136},{16,144},{24,152},{32,160},{40,168},{48,176},{56,1... | collective-permute-start | bytes 789512 | tf_op jit(solution)/shard_map/ppermute | solution.py:30
  50.2 0.2 fusion.24
  50.5 0.2 fusion.28
  50.7 10.5 %collective-permute-done.4 = f32[257,256]{1,0:T(8,128)S(1)} collective-permute-done((f32[257,256]{1,0:T(8,128)S(1)}, f32[257,256]{1,0:T(8,128)S(1)}, u32[]{:S(2)}, u32[]{:S(2)}) %collective-permute-start.4) | collective-permute-done | bytes 263200 | tf_op jit(solution)/shard_map/ppermute | solution.py:30
  61.3 5.0 %collective-permute-start.5 = (f32[129,256]{1,0:T(8,128)S(1)}, f32[129,256]{1,0:T(8,128)S(1)}, u32[]{:S(2)}, u32[]{:S(2)}) collective-permute-start(f32[129,256]{1,0:T(8,128)S(1)} %pad_maximum_fusion.6), channel_id=1, source_target_pairs={{0,448},{8,456},{16,464},{24,472},{32,480},{40,488},{48,496},{56,5... | collective-permute-start | bytes 396296 | tf_op jit(solution)/shard_map/ppermute | solution.py:26
  66.3 0.1 fusion.26
  66.4 4.4 %collective-permute-done.5 = f32[129,256]{1,0:T(8,128)S(1)} collective-permute-done((f32[129,256]{1,0:T(8,128)S(1)}, f32[129,256]{1,0:T(8,128)S(1)}, u32[]{:S(2)}, u32[]{:S(2)}) %collective-permute-start.5) | collective-permute-done | bytes 132128 | tf_op jit(solution)/shard_map/ppermute | solution.py:26
  70.9 0.1 fusion.8
  71.0 0.2 fusion.30
  71.2 0.2 convolution_add_fusion.1
  71.4 0.3 convolution_add_fusion
  71.7 0.8 copy.21
  72.4 16.3 %all-to-all-start = ((f32[8,16,256]{2,1,0:T(8,128)}), f32[8,16,256]{2,1,0:T(8,128)S(1)}, u32[]{:S(2)}, u32[]{:S(2)}) async-start(f32[8,16,256]{2,1,0:T(8,128)} %bitcast.34), calls=%async_computation | async-start | bytes 262144 | tf_op jit(solution)/shard_map/all_to_all | solution.py:55
  88.7 0.3 fusion.2
  89.1 0.7 copy.22
  89.8 4.7 %all-to-all-done = f32[8,16,256]{2,1,0:T(8,128)S(1)} async-done(((f32[8,16,256]{2,1,0:T(8,128)}), f32[8,16,256]{2,1,0:T(8,128)S(1)}, u32[]{:S(2)}, u32[]{:S(2)}) %all-to-all-start) | async-done | bytes 131104 | tf_op jit(solution)/shard_map/all_to_all | solution.py:55
  94.6 0.6 fusion.41
  (40 shorter events, 1.2 us)
Async XLA Ops:
  2.0 0.8 copy-start
  2.0 0.9 copy-start.1
  2.0 0.9 copy-start.2
  2.0 0.8 copy-start.3
  3.4 16.9 %collective-permute-start = (f32[257,256]{1,0:T(8,128)S(1)}, f32[257,256]{1,0:T(8,128)S(1)}, u32[]{:S(2)}, u32[]{:S(2)}) collective-permute-start(f32[257,256]{1,0:T(8,128)S(1)} %pad_maximum_fusion), channel_id=1, source_target_pairs={{0,8},{8,0},{16,24},{24,16},{32,40},{40,32},{48,56},{56,48},{64,72... | collective-permute-start | bytes 789512 | tf_op jit(solution)/shard_map/ppermute | solution.py:30
  20.4 8.6 %collective-permute-start.1 = (f32[257,256]{1,0:T(8,128)S(1)}, f32[257,256]{1,0:T(8,128)S(1)}, u32[]{:S(2)}, u32[]{:S(2)}) collective-permute-start(f32[257,256]{1,0:T(8,128)S(1)} %pad_maximum_fusion.1), channel_id=1, source_target_pairs={{0,16},{8,24},{16,0},{24,8},{32,48},{40,56},{48,32},{56,40},{64,80... | collective-permute-start | bytes 789512 | tf_op jit(solution)/shard_map/ppermute | solution.py:30
  29.1 9.3 %collective-permute-start.2 = (f32[257,256]{1,0:T(8,128)S(1)}, f32[257,256]{1,0:T(8,128)S(1)}, u32[]{:S(2)}, u32[]{:S(2)}) collective-permute-start(f32[257,256]{1,0:T(8,128)S(1)} %pad_maximum_fusion.2), channel_id=1, source_target_pairs={{0,48},{8,56},{16,32},{24,40},{32,16},{40,24},{48,0},{56,8},{64,11... | collective-permute-start | bytes 789512 | tf_op jit(solution)/shard_map/ppermute | solution.py:30
  38.5 7.2 %collective-permute-start.3 = (f32[257,256]{1,0:T(8,128)S(1)}, f32[257,256]{1,0:T(8,128)S(1)}, u32[]{:S(2)}, u32[]{:S(2)}) collective-permute-start(f32[257,256]{1,0:T(8,128)S(1)} %pad_maximum_fusion.3), channel_id=1, source_target_pairs={{0,64},{8,72},{16,80},{24,88},{32,96},{40,104},{48,112},{56,120},{... | collective-permute-start | bytes 789512 | tf_op jit(solution)/shard_map/ppermute | solution.py:30
  45.9 15.3 %collective-permute-start.4 = (f32[257,256]{1,0:T(8,128)S(1)}, f32[257,256]{1,0:T(8,128)S(1)}, u32[]{:S(2)}, u32[]{:S(2)}) collective-permute-start(f32[257,256]{1,0:T(8,128)S(1)} %pad_maximum_fusion.4), channel_id=1, source_target_pairs={{0,128},{8,136},{16,144},{24,152},{32,160},{40,168},{48,176},{56,1... | collective-permute-start | bytes 789512 | tf_op jit(solution)/shard_map/ppermute | solution.py:30
  61.3 9.6 %collective-permute-start.5 = (f32[129,256]{1,0:T(8,128)S(1)}, f32[129,256]{1,0:T(8,128)S(1)}, u32[]{:S(2)}, u32[]{:S(2)}) collective-permute-start(f32[129,256]{1,0:T(8,128)S(1)} %pad_maximum_fusion.6), channel_id=1, source_target_pairs={{0,448},{8,456},{16,464},{24,472},{32,480},{40,488},{48,496},{56,5... | collective-permute-start | bytes 396296 | tf_op jit(solution)/shard_map/ppermute | solution.py:26
  72.4 22.1 %all-to-all-start = ((f32[8,16,256]{2,1,0:T(8,128)}), f32[8,16,256]{2,1,0:T(8,128)S(1)}, u32[]{:S(2)}, u32[]{:S(2)}) async-start(f32[8,16,256]{2,1,0:T(8,128)} %bitcast.34), calls=%async_computation | async-start | bytes 262144 | tf_op jit(solution)/shard_map/all_to_all | solution.py:55

commit v10 on v9

--- a/solution.py
+++ b/solution.py
@@ -73,7 +73,10 @@
     )
     head_count = log_decay.shape[0]
     head_size = feature_width // head_count
-    cumulative = jnp.cumsum(log_decay, axis=1)
+    cumulative, reach = log_decay, 1
+    while reach < length:
+        cumulative = cumulative + jnp.pad(cumulative[:, :-reach], ((0, 0), (reach, 0)))
+        reach *= 2
     block_end = cumulative[:, -1:]
     forward_w = jnp.exp(block_end - cumulative)
     backward_w = jnp.exp(cumulative)

time: 95.6 us -> 96 us (level)
    add x0 -> x6, other arithmetic: none -> 1.22 us  [per_device(): cumulative + jnp.pad(cumulative[:, :-reach], ((0, 0), (reach, 0)))]
    another operation x1 -> x0, other arithmetic: 0.97 us -> none  [per_device(): cumulative = jnp.cumsum(log_decay, axis=1)]
where the time goes in v10:
time: 96 us; the launch traced here: 95.5 us
  starting transfers between devices  49.4 us (51%)
  waiting for transfers between devices  37.1 us (39%)
  local copies, waits for them, and re-layouts  3.77 us (4%)
  other arithmetic  2.14 us (2%)
  matrix products  2.14 us (2%)
    ppermute x6, starting transfers between devices, scan_both(): got = lax.ppermute(message, axis, pairs)  33.1 us
    ppermute x6, waiting for transfers between devices, scan_both(): got = lax.ppermute(message, axis, pairs)  32.4 us
    all_to_all x1, starting transfers between devices, scatter_sum(): lax.all_to_all(values.reshape(devices, rows // devices, cols), axis, 0, 0)  16.3 us
    all_to_all x1, waiting for transfers between devices, scatter_sum(): lax.all_to_all(values.reshape(devices, rows // devices, cols), axis, 0, 0)  4.73 us
  transfers between devices with their start and end apart: 7, of which 7 were waited for; matrix products, arithmetic and copies ran while one was open for 2% of the time, Pallas kernels for 0%

profile of v10, /device:TPU:1, one launch (start us, length us, event | category | flops | bytes accessed | tf_op | source)
XLA Modules:
  0.0 95.5 jit_solution(14281701284900543530)
XLA Ops:
  0.6 0.8 pad_add_fusion.6
  1.9 0.2 slice_reduce_fusion
  2.5 0.7 copy-done
  3.3 0.2 fusion.10
  3.7 11.5 %collective-permute-start = (f32[257,256]{1,0:T(8,128)S(1)}, f32[257,256]{1,0:T(8,128)S(1)}, u32[]{:S(2)}, u32[]{:S(2)}) collective-permute-start(f32[257,256]{1,0:T(8,128)S(1)} %pad_maximum_fusion), channel_id=1, source_target_pairs={{0,8},{8,0},{16,24},{24,16},{32,40},{40,32},{48,56},{56,48},{64,72... | collective-permute-start | bytes 789512 | tf_op jit(solution)/shard_map/ppermute | solution.py:30
  15.3 5.3 %collective-permute-done = f32[257,256]{1,0:T(8,128)S(1)} collective-permute-done((f32[257,256]{1,0:T(8,128)S(1)}, f32[257,256]{1,0:T(8,128)S(1)}, u32[]{:S(2)}, u32[]{:S(2)}) %collective-permute-start) | collective-permute-done | bytes 263200 | tf_op jit(solution)/shard_map/ppermute | solution.py:30
  20.7 3.9 %collective-permute-start.1 = (f32[257,256]{1,0:T(8,128)S(1)}, f32[257,256]{1,0:T(8,128)S(1)}, u32[]{:S(2)}, u32[]{:S(2)}) collective-permute-start(f32[257,256]{1,0:T(8,128)S(1)} %pad_maximum_fusion.1), channel_id=1, source_target_pairs={{0,16},{8,24},{16,0},{24,8},{32,48},{40,56},{48,32},{56,40},{64,80... | collective-permute-start | bytes 789512 | tf_op jit(solution)/shard_map/ppermute | solution.py:30
  24.7 4.7 %collective-permute-done.1 = f32[257,256]{1,0:T(8,128)S(1)} collective-permute-done((f32[257,256]{1,0:T(8,128)S(1)}, f32[257,256]{1,0:T(8,128)S(1)}, u32[]{:S(2)}, u32[]{:S(2)}) %collective-permute-start.1) | collective-permute-done | bytes 263200 | tf_op jit(solution)/shard_map/ppermute | solution.py:30
  29.4 5.1 %collective-permute-start.2 = (f32[257,256]{1,0:T(8,128)S(1)}, f32[257,256]{1,0:T(8,128)S(1)}, u32[]{:S(2)}, u32[]{:S(2)}) collective-permute-start(f32[257,256]{1,0:T(8,128)S(1)} %pad_maximum_fusion.2), channel_id=1, source_target_pairs={{0,48},{8,56},{16,32},{24,40},{32,16},{40,24},{48,0},{56,8},{64,11... | collective-permute-start | bytes 789512 | tf_op jit(solution)/shard_map/ppermute | solution.py:30
  34.5 4.2 %collective-permute-done.2 = f32[257,256]{1,0:T(8,128)S(1)} collective-permute-done((f32[257,256]{1,0:T(8,128)S(1)}, f32[257,256]{1,0:T(8,128)S(1)}, u32[]{:S(2)}, u32[]{:S(2)}) %collective-permute-start.2) | collective-permute-done | bytes 263200 | tf_op jit(solution)/shard_map/ppermute | solution.py:30
  38.9 3.3 %collective-permute-start.3 = (f32[257,256]{1,0:T(8,128)S(1)}, f32[257,256]{1,0:T(8,128)S(1)}, u32[]{:S(2)}, u32[]{:S(2)}) collective-permute-start(f32[257,256]{1,0:T(8,128)S(1)} %pad_maximum_fusion.3), channel_id=1, source_target_pairs={{0,64},{8,72},{16,80},{24,88},{32,96},{40,104},{48,112},{56,120},{... | collective-permute-start | bytes 789512 | tf_op jit(solution)/shard_map/ppermute | solution.py:30
  42.3 0.1 copy.15
  42.4 0.1 copy.20
  42.5 0.3 fusion
  42.9 3.2 %collective-permute-done.3 = f32[257,256]{1,0:T(8,128)S(1)} collective-permute-done((f32[257,256]{1,0:T(8,128)S(1)}, f32[257,256]{1,0:T(8,128)S(1)}, u32[]{:S(2)}, u32[]{:S(2)}) %collective-permute-start.3) | collective-permute-done | bytes 263200 | tf_op jit(solution)/shard_map/ppermute | solution.py:30
  46.2 4.3 %collective-permute-start.4 = (f32[257,256]{1,0:T(8,128)S(1)}, f32[257,256]{1,0:T(8,128)S(1)}, u32[]{:S(2)}, u32[]{:S(2)}) collective-permute-start(f32[257,256]{1,0:T(8,128)S(1)} %pad_maximum_fusion.4), channel_id=1, source_target_pairs={{0,128},{8,136},{16,144},{24,152},{32,160},{40,168},{48,176},{56,1... | collective-permute-start | bytes 789512 | tf_op jit(solution)/shard_map/ppermute | solution.py:30
  50.6 0.2 fusion.24
  50.8 0.2 fusion.28
  51.1 10.5 %collective-permute-done.4 = f32[257,256]{1,0:T(8,128)S(1)} collective-permute-done((f32[257,256]{1,0:T(8,128)S(1)}, f32[257,256]{1,0:T(8,128)S(1)}, u32[]{:S(2)}, u32[]{:S(2)}) %collective-permute-start.4) | collective-permute-done | bytes 263200 | tf_op jit(solution)/shard_map/ppermute | solution.py:30
  61.6 5.0 %collective-permute-start.5 = (f32[129,256]{1,0:T(8,128)S(1)}, f32[129,256]{1,0:T(8,128)S(1)}, u32[]{:S(2)}, u32[]{:S(2)}) collective-permute-start(f32[129,256]{1,0:T(8,128)S(1)} %pad_maximum_fusion.6), channel_id=1, source_target_pairs={{0,448},{8,456},{16,464},{24,472},{32,480},{40,488},{48,496},{56,5... | collective-permute-start | bytes 396296 | tf_op jit(solution)/shard_map/ppermute | solution.py:26
  66.7 0.1 fusion.26
  66.8 4.4 %collective-permute-done.5 = f32[129,256]{1,0:T(8,128)S(1)} collective-permute-done((f32[129,256]{1,0:T(8,128)S(1)}, f32[129,256]{1,0:T(8,128)S(1)}, u32[]{:S(2)}, u32[]{:S(2)}) %collective-permute-start.5) | collective-permute-done | bytes 132128 | tf_op jit(solution)/shard_map/ppermute | solution.py:26
  71.2 0.1 fusion.8
  71.3 0.2 fusion.30
  71.6 0.2 convolution_add_fusion.1
  71.7 0.3 convolution_add_fusion
  72.0 0.8 copy.21
  72.8 16.3 %all-to-all-start = ((f32[8,16,256]{2,1,0:T(8,128)}), f32[8,16,256]{2,1,0:T(8,128)S(1)}, u32[]{:S(2)}, u32[]{:S(2)}) async-start(f32[8,16,256]{2,1,0:T(8,128)} %bitcast.34), calls=%async_computation | async-start | bytes 262144 | tf_op jit(solution)/shard_map/all_to_all | solution.py:55
  89.1 0.3 fusion.2
  89.4 0.7 copy.22
  90.2 4.7 %all-to-all-done = f32[8,16,256]{2,1,0:T(8,128)S(1)} async-done(((f32[8,16,256]{2,1,0:T(8,128)}), f32[8,16,256]{2,1,0:T(8,128)S(1)}, u32[]{:S(2)}, u32[]{:S(2)}) %all-to-all-start) | async-done | bytes 131104 | tf_op jit(solution)/shard_map/all_to_all | solution.py:55
  94.9 0.6 fusion.41
  (46 shorter events, 1.7 us)
Async XLA Ops:
  2.3 0.8 copy-start
  2.4 0.9 copy-start.1
  2.4 0.9 copy-start.2
  2.4 0.8 copy-start.3
  3.7 16.9 %collective-permute-start = (f32[257,256]{1,0:T(8,128)S(1)}, f32[257,256]{1,0:T(8,128)S(1)}, u32[]{:S(2)}, u32[]{:S(2)}) collective-permute-start(f32[257,256]{1,0:T(8,128)S(1)} %pad_maximum_fusion), channel_id=1, source_target_pairs={{0,8},{8,0},{16,24},{24,16},{32,40},{40,32},{48,56},{56,48},{64,72... | collective-permute-start | bytes 789512 | tf_op jit(solution)/shard_map/ppermute | solution.py:30
  20.7 8.6 %collective-permute-start.1 = (f32[257,256]{1,0:T(8,128)S(1)}, f32[257,256]{1,0:T(8,128)S(1)}, u32[]{:S(2)}, u32[]{:S(2)}) collective-permute-start(f32[257,256]{1,0:T(8,128)S(1)} %pad_maximum_fusion.1), channel_id=1, source_target_pairs={{0,16},{8,24},{16,0},{24,8},{32,48},{40,56},{48,32},{56,40},{64,80... | collective-permute-start | bytes 789512 | tf_op jit(solution)/shard_map/ppermute | solution.py:30
  29.4 9.3 %collective-permute-start.2 = (f32[257,256]{1,0:T(8,128)S(1)}, f32[257,256]{1,0:T(8,128)S(1)}, u32[]{:S(2)}, u32[]{:S(2)}) collective-permute-start(f32[257,256]{1,0:T(8,128)S(1)} %pad_maximum_fusion.2), channel_id=1, source_target_pairs={{0,48},{8,56},{16,32},{24,40},{32,16},{40,24},{48,0},{56,8},{64,11... | collective-permute-start | bytes 789512 | tf_op jit(solution)/shard_map/ppermute | solution.py:30
  38.9 7.2 %collective-permute-start.3 = (f32[257,256]{1,0:T(8,128)S(1)}, f32[257,256]{1,0:T(8,128)S(1)}, u32[]{:S(2)}, u32[]{:S(2)}) collective-permute-start(f32[257,256]{1,0:T(8,128)S(1)} %pad_maximum_fusion.3), channel_id=1, source_target_pairs={{0,64},{8,72},{16,80},{24,88},{32,96},{40,104},{48,112},{56,120},{... | collective-permute-start | bytes 789512 | tf_op jit(solution)/shard_map/ppermute | solution.py:30
  46.2 15.3 %collective-permute-start.4 = (f32[257,256]{1,0:T(8,128)S(1)}, f32[257,256]{1,0:T(8,128)S(1)}, u32[]{:S(2)}, u32[]{:S(2)}) collective-permute-start(f32[257,256]{1,0:T(8,128)S(1)} %pad_maximum_fusion.4), channel_id=1, source_target_pairs={{0,128},{8,136},{16,144},{24,152},{32,160},{40,168},{48,176},{56,1... | collective-permute-start | bytes 789512 | tf_op jit(solution)/shard_map/ppermute | solution.py:30
  61.6 9.6 %collective-permute-start.5 = (f32[129,256]{1,0:T(8,128)S(1)}, f32[129,256]{1,0:T(8,128)S(1)}, u32[]{:S(2)}, u32[]{:S(2)}) collective-permute-start(f32[129,256]{1,0:T(8,128)S(1)} %pad_maximum_fusion.6), channel_id=1, source_target_pairs={{0,448},{8,456},{16,464},{24,472},{32,480},{40,488},{48,496},{56,5... | collective-permute-start | bytes 396296 | tf_op jit(solution)/shard_map/ppermute | solution.py:26
  72.8 22.1 %all-to-all-start = ((f32[8,16,256]{2,1,0:T(8,128)}), f32[8,16,256]{2,1,0:T(8,128)S(1)}, u32[]{:S(2)}, u32[]{:S(2)}) async-start(f32[8,16,256]{2,1,0:T(8,128)} %bitcast.34), calls=%async_computation | async-start | bytes 262144 | tf_op jit(solution)/shard_map/all_to_all | solution.py:55

commit v11 on v9

--- a/solution.py
+++ b/solution.py
@@ -21,14 +21,14 @@
         last = shift * 2 >= devices
         if last:
             message = jnp.concatenate(
-                [block_decay[None, :], jnp.where(later, block_grad, block_state)], axis=0
+                [jnp.where(later, block_grad, block_state), block_decay[None, :]], axis=0
             )
             got = lax.ppermute(message, axis, pairs)
-            got_decay, got_state, got_grad = got[0], got[1:], got[1:]
+            got_decay, got_state, got_grad = got[rows], got[:rows], got[:rows]
         else:
-            message = jnp.concatenate([block_decay[None, :], block_state, block_grad], axis=0)
+            message = jnp.concatenate([block_state, block_grad, block_decay[None, :]], axis=0)
             got = lax.ppermute(message, axis, pairs)
-            got_decay, got_state, got_grad = got[0], got[1 : rows + 1], got[rows + 1 :]
+            got_decay, got_state, got_grad = got[2 * rows], got[:rows], got[rows : 2 * rows]
         prefix_state = jnp.where(later, prefix_decay[None, :] * got_state + prefix_state, prefix_state)
         prefix_decay = jnp.where(later, got_decay * prefix_decay, prefix_decay)
         suffix_grad = jnp.where(later, suffix_grad, suffix_decay[None, :] * got_grad + suffix_grad)

time: 95.6 us -> 95.4 us (level)
  no operation moved by 1% of the time
where the time goes in v11:
time: 95.4 us; the launch traced here: 94.9 us
  starting transfers between devices  49.4 us (52%)
  waiting for transfers between devices  37.1 us (39%)
  local copies, waits for them, and re-layouts  3.76 us (4%)
  matrix products  2.08 us (2%)
  other arithmetic  1.64 us (2%)
  between operations  0.96 us (1%)
    ppermute x6, starting transfers between devices, scan_both(): got = lax.ppermute(message, axis, pairs)  33.1 us
    ppermute x6, waiting for transfers between devices, scan_both(): got = lax.ppermute(message, axis, pairs)  32.4 us
    all_to_all x1, starting transfers between devices, scatter_sum(): lax.all_to_all(values.reshape(devices, rows // devices, cols), axis, 0, 0)  16.3 us
    all_to_all x1, waiting for transfers between devices, scatter_sum(): lax.all_to_all(values.reshape(devices, rows // devices, cols), axis, 0, 0)  4.74 us
  transfers between devices with their start and end apart: 7, of which 7 were waited for; matrix products, arithmetic and copies ran while one was open for 2% of the time, Pallas kernels for 0%

profile of v11, /device:TPU:1, one launch (start us, length us, event | category | flops | bytes accessed | tf_op | source)
XLA Modules:
  0.0 94.9 jit_solution(12554590668665443636)
XLA Ops:
  0.6 1.0 %reduce_window_sum.11 = f32[8,128]{1,0:T(8,128)S(1)} reduce-window(f32[8,128]{1,0:T(8,128)} %param.8, f32[]{:T(128)} %constant.12.clone.1), window={size=1x128 pad=0_0x127_0}, to_apply=%region_0.0 | reduce-window | flops 130048 | bytes 8196 | tf_op jit(solution)/shard_map/jit(cumsum)/reduce_window_sum | solution.py:76
  1.6 0.2 slice_reduce_fusion
  2.2 0.7 copy-done
  3.0 0.2 fusion.10
  3.4 11.5 %collective-permute-start = (f32[257,256]{1,0:T(8,128)S(1)}, f32[257,256]{1,0:T(8,128)S(1)}, u32[]{:S(2)}, u32[]{:S(2)}) collective-permute-start(f32[257,256]{1,0:T(8,128)S(1)} %pad_maximum_fusion), channel_id=1, source_target_pairs={{0,8},{8,0},{16,24},{24,16},{32,40},{40,32},{48,56},{56,48},{64,72... | collective-permute-start | bytes 789512 | tf_op jit(solution)/shard_map/ppermute | solution.py:30
  15.0 5.3 %collective-permute-done = f32[257,256]{1,0:T(8,128)S(1)} collective-permute-done((f32[257,256]{1,0:T(8,128)S(1)}, f32[257,256]{1,0:T(8,128)S(1)}, u32[]{:S(2)}, u32[]{:S(2)}) %collective-permute-start) | collective-permute-done | bytes 263200 | tf_op jit(solution)/shard_map/ppermute | solution.py:30
  20.4 3.9 %collective-permute-start.1 = (f32[257,256]{1,0:T(8,128)S(1)}, f32[257,256]{1,0:T(8,128)S(1)}, u32[]{:S(2)}, u32[]{:S(2)}) collective-permute-start(f32[257,256]{1,0:T(8,128)S(1)} %pad_maximum_fusion.1), channel_id=1, source_target_pairs={{0,16},{8,24},{16,0},{24,8},{32,48},{40,56},{48,32},{56,40},{64,80... | collective-permute-start | bytes 789512 | tf_op jit(solution)/shard_map/ppermute | solution.py:30
  24.3 4.7 %collective-permute-done.1 = f32[257,256]{1,0:T(8,128)S(1)} collective-permute-done((f32[257,256]{1,0:T(8,128)S(1)}, f32[257,256]{1,0:T(8,128)S(1)}, u32[]{:S(2)}, u32[]{:S(2)}) %collective-permute-start.1) | collective-permute-done | bytes 263200 | tf_op jit(solution)/shard_map/ppermute | solution.py:30
  29.0 5.1 %collective-permute-start.2 = (f32[257,256]{1,0:T(8,128)S(1)}, f32[257,256]{1,0:T(8,128)S(1)}, u32[]{:S(2)}, u32[]{:S(2)}) collective-permute-start(f32[257,256]{1,0:T(8,128)S(1)} %pad_maximum_fusion.2), channel_id=1, source_target_pairs={{0,48},{8,56},{16,32},{24,40},{32,16},{40,24},{48,0},{56,8},{64,11... | collective-permute-start | bytes 789512 | tf_op jit(solution)/shard_map/ppermute | solution.py:30
  34.1 4.2 %collective-permute-done.2 = f32[257,256]{1,0:T(8,128)S(1)} collective-permute-done((f32[257,256]{1,0:T(8,128)S(1)}, f32[257,256]{1,0:T(8,128)S(1)}, u32[]{:S(2)}, u32[]{:S(2)}) %collective-permute-start.2) | collective-permute-done | bytes 263200 | tf_op jit(solution)/shard_map/ppermute | solution.py:30
  38.5 3.3 %collective-permute-start.3 = (f32[257,256]{1,0:T(8,128)S(1)}, f32[257,256]{1,0:T(8,128)S(1)}, u32[]{:S(2)}, u32[]{:S(2)}) collective-permute-start(f32[257,256]{1,0:T(8,128)S(1)} %pad_maximum_fusion.3), channel_id=1, source_target_pairs={{0,64},{8,72},{16,80},{24,88},{32,96},{40,104},{48,112},{56,120},{... | collective-permute-start | bytes 789512 | tf_op jit(solution)/shard_map/ppermute | solution.py:30
  41.8 0.1 copy.15
  42.0 0.1 copy.20
  42.1 0.3 fusion
  42.4 3.2 %collective-permute-done.3 = f32[257,256]{1,0:T(8,128)S(1)} collective-permute-done((f32[257,256]{1,0:T(8,128)S(1)}, f32[257,256]{1,0:T(8,128)S(1)}, u32[]{:S(2)}, u32[]{:S(2)}) %collective-permute-start.3) | collective-permute-done | bytes 263200 | tf_op jit(solution)/shard_map/ppermute | solution.py:30
  45.8 4.3 %collective-permute-start.4 = (f32[257,256]{1,0:T(8,128)S(1)}, f32[257,256]{1,0:T(8,128)S(1)}, u32[]{:S(2)}, u32[]{:S(2)}) collective-permute-start(f32[257,256]{1,0:T(8,128)S(1)} %pad_maximum_fusion.4), channel_id=1, source_target_pairs={{0,128},{8,136},{16,144},{24,152},{32,160},{40,168},{48,176},{56,1... | collective-permute-start | bytes 789512 | tf_op jit(solution)/shard_map/ppermute | solution.py:30
  50.1 0.2 fusion.24
  50.4 0.2 fusion.28
  50.6 10.5 %collective-permute-done.4 = f32[257,256]{1,0:T(8,128)S(1)} collective-permute-done((f32[257,256]{1,0:T(8,128)S(1)}, f32[257,256]{1,0:T(8,128)S(1)}, u32[]{:S(2)}, u32[]{:S(2)}) %collective-permute-start.4) | collective-permute-done | bytes 263200 | tf_op jit(solution)/shard_map/ppermute | solution.py:30
  61.2 5.0 %collective-permute-start.5 = (f32[129,256]{1,0:T(8,128)S(1)}, f32[129,256]{1,0:T(8,128)S(1)}, u32[]{:S(2)}, u32[]{:S(2)}) collective-permute-start(f32[129,256]{1,0:T(8,128)S(1)} %pad_maximum_fusion.6), channel_id=1, source_target_pairs={{0,448},{8,456},{16,464},{24,472},{32,480},{40,488},{48,496},{56,5... | collective-permute-start | bytes 396296 | tf_op jit(solution)/shard_map/ppermute | solution.py:26
  66.2 0.1 fusion.26
  66.3 4.4 %collective-permute-done.5 = f32[129,256]{1,0:T(8,128)S(1)} collective-permute-done((f32[129,256]{1,0:T(8,128)S(1)}, f32[129,256]{1,0:T(8,128)S(1)}, u32[]{:S(2)}, u32[]{:S(2)}) %collective-permute-start.5) | collective-permute-done | bytes 132128 | tf_op jit(solution)/shard_map/ppermute | solution.py:26
  70.8 0.1 fusion.8
  70.9 0.2 fusion.30
  71.1 0.2 convolution_add_fusion.1
  71.2 0.2 convolution_add_fusion
  71.5 0.8 copy.21
  72.2 16.3 %all-to-all-start = ((f32[8,16,256]{2,1,0:T(8,128)}), f32[8,16,256]{2,1,0:T(8,128)S(1)}, u32[]{:S(2)}, u32[]{:S(2)}) async-start(f32[8,16,256]{2,1,0:T(8,128)} %bitcast.34), calls=%async_computation | async-start | bytes 262144 | tf_op jit(solution)/shard_map/all_to_all | solution.py:55
  88.5 0.3 fusion.2
  88.8 0.7 copy.22
  89.6 4.7 %all-to-all-done = f32[8,16,256]{2,1,0:T(8,128)S(1)} async-done(((f32[8,16,256]{2,1,0:T(8,128)}), f32[8,16,256]{2,1,0:T(8,128)S(1)}, u32[]{:S(2)}, u32[]{:S(2)}) %all-to-all-start) | async-done | bytes 131104 | tf_op jit(solution)/shard_map/all_to_all | solution.py:55
  94.3 0.6 fusion.45
  (40 shorter events, 1.1 us)
Async XLA Ops:
  2.0 0.8 copy-start
  2.0 0.9 copy-start.1
  2.0 0.9 copy-start.2
  2.0 0.8 copy-start.3
  3.4 16.9 %collective-permute-start = (f32[257,256]{1,0:T(8,128)S(1)}, f32[257,256]{1,0:T(8,128)S(1)}, u32[]{:S(2)}, u32[]{:S(2)}) collective-permute-start(f32[257,256]{1,0:T(8,128)S(1)} %pad_maximum_fusion), channel_id=1, source_target_pairs={{0,8},{8,0},{16,24},{24,16},{32,40},{40,32},{48,56},{56,48},{64,72... | collective-permute-start | bytes 789512 | tf_op jit(solution)/shard_map/ppermute | solution.py:30
  20.4 8.6 %collective-permute-start.1 = (f32[257,256]{1,0:T(8,128)S(1)}, f32[257,256]{1,0:T(8,128)S(1)}, u32[]{:S(2)}, u32[]{:S(2)}) collective-permute-start(f32[257,256]{1,0:T(8,128)S(1)} %pad_maximum_fusion.1), channel_id=1, source_target_pairs={{0,16},{8,24},{16,0},{24,8},{32,48},{40,56},{48,32},{56,40},{64,80... | collective-permute-start | bytes 789512 | tf_op jit(solution)/shard_map/ppermute | solution.py:30
  29.0 9.3 %collective-permute-start.2 = (f32[257,256]{1,0:T(8,128)S(1)}, f32[257,256]{1,0:T(8,128)S(1)}, u32[]{:S(2)}, u32[]{:S(2)}) collective-permute-start(f32[257,256]{1,0:T(8,128)S(1)} %pad_maximum_fusion.2), channel_id=1, source_target_pairs={{0,48},{8,56},{16,32},{24,40},{32,16},{40,24},{48,0},{56,8},{64,11... | collective-permute-start | bytes 789512 | tf_op jit(solution)/shard_map/ppermute | solution.py:30
  38.5 7.2 %collective-permute-start.3 = (f32[257,256]{1,0:T(8,128)S(1)}, f32[257,256]{1,0:T(8,128)S(1)}, u32[]{:S(2)}, u32[]{:S(2)}) collective-permute-start(f32[257,256]{1,0:T(8,128)S(1)} %pad_maximum_fusion.3), channel_id=1, source_target_pairs={{0,64},{8,72},{16,80},{24,88},{32,96},{40,104},{48,112},{56,120},{... | collective-permute-start | bytes 789512 | tf_op jit(solution)/shard_map/ppermute | solution.py:30
  45.8 15.3 %collective-permute-start.4 = (f32[257,256]{1,0:T(8,128)S(1)}, f32[257,256]{1,0:T(8,128)S(1)}, u32[]{:S(2)}, u32[]{:S(2)}) collective-permute-start(f32[257,256]{1,0:T(8,128)S(1)} %pad_maximum_fusion.4), channel_id=1, source_target_pairs={{0,128},{8,136},{16,144},{24,152},{32,160},{40,168},{48,176},{56,1... | collective-permute-start | bytes 789512 | tf_op jit(solution)/shard_map/ppermute | solution.py:30
  61.2 9.6 %collective-permute-start.5 = (f32[129,256]{1,0:T(8,128)S(1)}, f32[129,256]{1,0:T(8,128)S(1)}, u32[]{:S(2)}, u32[]{:S(2)}) collective-permute-start(f32[129,256]{1,0:T(8,128)S(1)} %pad_maximum_fusion.6), channel_id=1, source_target_pairs={{0,448},{8,456},{16,464},{24,472},{32,480},{40,488},{48,496},{56,5... | collective-permute-start | bytes 396296 | tf_op jit(solution)/shard_map/ppermute | solution.py:26
  72.2 22.1 %all-to-all-start = ((f32[8,16,256]{2,1,0:T(8,128)}), f32[8,16,256]{2,1,0:T(8,128)S(1)}, u32[]{:S(2)}, u32[]{:S(2)}) async-start(f32[8,16,256]{2,1,0:T(8,128)} %bitcast.34), calls=%async_computation | async-start | bytes 262144 | tf_op jit(solution)/shard_map/all_to_all | solution.py:55

commit v12 on v11

--- a/solution.py
+++ b/solution.py
@@ -4,49 +4,48 @@
 from jax.sharding import PartitionSpec as P
 
 
-PARTNER_MASKS = {64: {4: 6, 32: 56}}
+PARTNER_MASKS = {16: {4: 6}}
 
 
-def scan_both(decay, state, grad, axis):
-    devices, mine = lax.axis_size(axis), lax.axis_index(axis)
-    block_decay, block_state, block_grad = decay, state, grad
-    prefix_decay, prefix_state = jnp.ones_like(decay), jnp.zeros_like(state)
-    suffix_decay, suffix_grad = jnp.ones_like(decay), jnp.zeros_like(grad)
+def joined(earlier, later):
+    a1, s1, g1 = earlier
+    a2, s2, g2 = later
+    return (a1 * a2, a2[None, :] * s1 + s2, a1[None, :] * g2 + g1)
+
+
+def chosen(flag, yes, no):
+    return tuple(jnp.where(flag, y, n) for y, n in zip(yes, no))
+
+
+def scan_both(decay, state, grad, low_axis, high_axis):
+    devices, mine = lax.axis_size(low_axis), lax.axis_index(low_axis)
     rows = state.shape[0]
+    identity = (jnp.ones_like(decay), jnp.zeros_like(state), jnp.zeros_like(grad))
+    block = (decay, state, grad)
+    prefix, suffix = identity, identity
     shift = 1
     while shift < devices:
         mask = PARTNER_MASKS.get(devices, {}).get(shift, shift)
         pairs = [(i, i ^ mask) for i in range(devices)]
         later = (mine & shift) != 0
-        last = shift * 2 >= devices
-        if last:
-            message = jnp.concatenate(
-                [jnp.where(later, block_grad, block_state), block_decay[None, :]], axis=0
-            )
-            got = lax.ppermute(message, axis, pairs)
-            got_decay, got_state, got_grad = got[rows], got[:rows], got[:rows]
-        else:
-            message = jnp.concatenate([block_state, block_grad, block_decay[None, :]], axis=0)
-            got = lax.ppermute(message, axis, pairs)
-            got_decay, got_state, got_grad = got[2 * rows], got[:rows], got[rows : 2 * rows]
-        prefix_state = jnp.where(later, prefix_decay[None, :] * got_state + prefix_state, prefix_state)
-        prefix_decay = jnp.where(later, got_decay * prefix_decay, prefix_decay)
-        suffix_grad = jnp.where(later, suffix_grad, suffix_decay[None, :] * got_grad + suffix_grad)
-        suffix_decay = jnp.where(later, suffix_decay, got_decay * suffix_decay)
+        message = jnp.concatenate([block[1], block[2], block[0][None, :]], axis=0)
+        got = lax.ppermute(message, low_axis, pairs)
+        piece = (got[2 * rows], got[:rows], got[rows : 2 * rows])
+        prefix = chosen(later, joined(piece, prefix), prefix)
+        suffix = chosen(later, suffix, joined(suffix, piece))
+        block = chosen(later, joined(piece, block), joined(block, piece))
         shift *= 2
-        if not last:
-            block_state = jnp.where(
-                later,
-                block_decay[None, :] * got_state + block_state,
-                got_decay[None, :] * block_state + got_state,
-            )
-            block_grad = jnp.where(
-                later,
-                got_decay[None, :] * block_grad + got_grad,
-                block_decay[None, :] * got_grad + block_grad,
-            )
-            block_decay = got_decay * block_decay
-    return prefix_state, suffix_grad
+    size, place = lax.axis_size(high_axis), lax.axis_index(high_axis)
+    message = jnp.concatenate([block[1], block[2], block[0][None, :]], axis=0)
+    got = lax.all_to_all(jnp.broadcast_to(message[None], (size,) + message.shape), high_axis, 0, 0)
+    before, after = identity, identity
+    for member in range(size):
+        piece = (got[member, 2 * rows], got[member, :rows], got[member, rows : 2 * rows])
+        before = chosen(member < place, joined(before, piece), before)
+        after = chosen(member > place, joined(after, piece), after)
+    prefix = joined(before, prefix)
+    suffix = joined(suffix, after)
+    return prefix[1], suffix[2]
 
 
 def scatter_sum(values, axis):
@@ -87,7 +86,7 @@
         preferred_element_type=jnp.float32,
     )
 
-    entry, exit_ = scan_both(through, own_state, own_grad, "ctx")
+    entry, exit_ = scan_both(through, own_state, own_grad, "ctx_lo", "ctx_hi")
     entry_bf = entry.astype(jnp.bfloat16)
     exit_bf = exit_.astype(jnp.bfloat16)
 
@@ -128,11 +127,17 @@
 
 
 def solution(mesh):
-    placed = (P("ctx", "head"), P("ctx", None), P("ctx", None), P("head", "ctx"), P("ctx", "head"))
+    ctx_size = mesh.shape["ctx"]
+    hi = 4 if ctx_size % 4 == 0 and ctx_size >= 8 else 1
+    split = jax.sharding.Mesh(
+        mesh.devices.reshape(hi, ctx_size // hi, mesh.shape["head"]), ("ctx_hi", "ctx_lo", "head")
+    )
+    ctx = ("ctx_hi", "ctx_lo")
+    placed = (P(ctx, "head"), P(ctx, None), P(ctx, None), P("head", ctx), P(ctx, "head"))
     return jax.shard_map(
         per_device,
-        mesh=mesh,
+        mesh=split,
         in_specs=placed,
-        out_specs=(P("ctx", "head"), P(("ctx", "head"), None), P(("ctx", "head"), None)),
+        out_specs=(P(ctx, "head"), P(ctx + ("head",), None), P(ctx + ("head",), None)),
         check_vma=False,
     )

time: 95.4 us -> 102 us (1.069)
  waiting for transfers between devices: 37.1 us -> 48.3 us
  starting transfers between devices: 49.4 us -> 43.6 us
    all_to_all x0 -> x1, waiting for transfers between devices: none -> 25.5 us  [scan_both(): lax.all_to_all(jnp.broadcast_to(message[None], (size,) + message.shape),...]
    ppermute x6 -> x4, waiting for transfers between devices: 32.4 us -> 18.1 us  [scan_both(): got = lax.ppermute(message, low_axis, pairs)]
    ppermute x6 -> x4, starting transfers between devices: 33.1 us -> 23.8 us  [scan_both(): got = lax.ppermute(message, low_axis, pairs)]
    all_to_all x0 -> x1, starting transfers between devices: none -> 6.94 us  [scan_both(): lax.all_to_all(jnp.broadcast_to(message[None], (size,) + message.shape),...]
    all_to_all x1, starting transfers between devices: 16.3 us -> 12.9 us  [scatter_sum(): lax.all_to_all(values.reshape(devices, rows // devices, cols), axis, 0, 0)]
    broadcast_in_dim x0 -> x1, local copies, waits for them, and re-layouts: none -> 1.06 us  [scan_both(): jnp.broadcast_to(message[None], (size,) + message.shape)]
  transfers between devices with their start and end apart: 7 -> 6, of which waited for: 7 -> 6; matrix products, arithmetic and copies ran while one was open for 2% -> 2% of each run, Pallas kernels for 0% -> 0%
where the time goes in v12:
time: 102 us
  waiting for transfers between devices  48.3 us (47%)
  starting transfers between devices  43.6 us (43%)
  local copies, waits for them, and re-layouts  4.06 us (4%)
  other arithmetic  2.53 us (2%)
  matrix products  2.15 us (2%)
    all_to_all x1, waiting for transfers between devices, scan_both(): lax.all_to_all(jnp.broadcast_to(message[None], (size,) + message.shape),...  25.5 us
    ppermute x4, starting transfers between devices, scan_both(): got = lax.ppermute(message, low_axis, pairs)  23.8 us
    ppermute x4, waiting for transfers between devices, scan_both(): got = lax.ppermute(message, low_axis, pairs)  18.1 us
    all_to_all x1, starting transfers between devices, scatter_sum(): lax.all_to_all(values.reshape(devices, rows // devices, cols), axis, 0, 0)  12.9 us
    all_to_all x1, starting transfers between devices, scan_both(): lax.all_to_all(jnp.broadcast_to(message[None], (size,) + message.shape),...  6.94 us
    all_to_all x1, waiting for transfers between devices, scatter_sum(): lax.all_to_all(values.reshape(devices, rows // devices, cols), axis, 0, 0)  4.74 us
  transfers between devices with their start and end apart: 6, of which 6 were waited for; matrix products, arithmetic and copies ran while one was open for 2% of the time, Pallas kernels for 0%

profile of v12, /device:TPU:1, one launch (start us, length us, event | category | flops | bytes accessed | tf_op | source)
XLA Modules:
  0.0 101.5 jit_solution(11632831221935135959)
XLA Ops:
  0.6 1.0 reduce_window_sum.11
  1.6 0.2 slice_reduce_fusion
  2.0 0.1 copy.17
  2.1 0.9 pad_maximum_fusion.5
  3.1 0.2 fusion.26
  3.5 11.5 %collective-permute-start = (f32[257,256]{1,0:T(8,128)S(1)}, f32[257,256]{1,0:T(8,128)S(1)}, u32[]{:S(2)}, u32[]{:S(2)}) collective-permute-start(f32[257,256]{1,0:T(8,128)S(1)} %pad_maximum_fusion), channel_id=1, source_target_pairs={{0,8},{8,0},{16,24},{24,16},{32,40},{40,32},{48,56},{56,48},{64,72... | collective-permute-start | bytes 789512 | tf_op jit(solution)/shard_map/ppermute | solution.py:32
  15.1 5.3 %collective-permute-done = f32[257,256]{1,0:T(8,128)S(1)} collective-permute-done((f32[257,256]{1,0:T(8,128)S(1)}, f32[257,256]{1,0:T(8,128)S(1)}, u32[]{:S(2)}, u32[]{:S(2)}) %collective-permute-start) | collective-permute-done | bytes 263200 | tf_op jit(solution)/shard_map/ppermute | solution.py:32
  20.5 3.9 %collective-permute-start.1 = (f32[257,256]{1,0:T(8,128)S(1)}, f32[257,256]{1,0:T(8,128)S(1)}, u32[]{:S(2)}, u32[]{:S(2)}) collective-permute-start(f32[257,256]{1,0:T(8,128)S(1)} %pad_maximum_fusion.1), channel_id=1, source_target_pairs={{0,16},{8,24},{16,0},{24,8},{32,48},{40,56},{48,32},{56,40},{64,80... | collective-permute-start | bytes 789512 | tf_op jit(solution)/shard_map/ppermute | solution.py:32
  24.4 4.7 %collective-permute-done.1 = f32[257,256]{1,0:T(8,128)S(1)} collective-permute-done((f32[257,256]{1,0:T(8,128)S(1)}, f32[257,256]{1,0:T(8,128)S(1)}, u32[]{:S(2)}, u32[]{:S(2)}) %collective-permute-start.1) | collective-permute-done | bytes 263200 | tf_op jit(solution)/shard_map/ppermute | solution.py:32
  29.2 5.1 %collective-permute-start.2 = (f32[257,256]{1,0:T(8,128)S(1)}, f32[257,256]{1,0:T(8,128)S(1)}, u32[]{:S(2)}, u32[]{:S(2)}) collective-permute-start(f32[257,256]{1,0:T(8,128)S(1)} %pad_maximum_fusion.2), channel_id=1, source_target_pairs={{0,48},{8,56},{16,32},{24,40},{32,16},{40,24},{48,0},{56,8},{64,11... | collective-permute-start | bytes 789512 | tf_op jit(solution)/shard_map/ppermute | solution.py:32
  34.3 4.2 %collective-permute-done.2 = f32[257,256]{1,0:T(8,128)S(1)} collective-permute-done((f32[257,256]{1,0:T(8,128)S(1)}, f32[257,256]{1,0:T(8,128)S(1)}, u32[]{:S(2)}, u32[]{:S(2)}) %collective-permute-start.2) | collective-permute-done | bytes 263200 | tf_op jit(solution)/shard_map/ppermute | solution.py:32
  38.6 3.3 %collective-permute-start.3 = (f32[257,256]{1,0:T(8,128)S(1)}, f32[257,256]{1,0:T(8,128)S(1)}, u32[]{:S(2)}, u32[]{:S(2)}) collective-permute-start(f32[257,256]{1,0:T(8,128)S(1)} %pad_maximum_fusion.3), channel_id=1, source_target_pairs={{0,64},{8,72},{16,80},{24,88},{32,96},{40,104},{48,112},{56,120},{... | collective-permute-start | bytes 789512 | tf_op jit(solution)/shard_map/ppermute | solution.py:32
  42.0 3.9 %collective-permute-done.3 = f32[257,256]{1,0:T(8,128)S(1)} collective-permute-done((f32[257,256]{1,0:T(8,128)S(1)}, f32[257,256]{1,0:T(8,128)S(1)}, u32[]{:S(2)}, u32[]{:S(2)}) %collective-permute-start.3) | collective-permute-done | bytes 263200 | tf_op jit(solution)/shard_map/ppermute | solution.py:32
  45.9 1.1 %broadcast_in_dim.20 = f32[4,257,256]{2,1,0:T(8,128)} broadcast(f32[257,256]{1,0:T(8,128)S(1)} %pad_maximum_fusion.4), dimensions={1,2} | broadcast | bytes 1315840 | tf_op jit(solution)/shard_map/broadcast_in_dim | solution.py:40
  47.0 6.9 %all-to-all-start = ((f32[4,257,256]{2,1,0:T(8,128)}), f32[4,257,256]{2,1,0:T(8,128)S(1)}, u32[]{:S(2)}, u32[]{:S(2)}) async-start(f32[4,257,256]{2,1,0:T(8,128)} %broadcast_in_dim.20), calls=%async_computation | async-start | bytes 2162688 | tf_op jit(solution)/shard_map/all_to_all | solution.py:40
  53.9 0.1 copy.15
  54.1 0.1 copy.20
  54.2 0.3 fusion
  54.5 0.1 fusion.36
  54.7 0.3 fusion.34
  54.9 0.2 fusion.38
  55.2 25.5 %all-to-all-done = f32[4,257,256]{2,1,0:T(8,128)S(1)} async-done(((f32[4,257,256]{2,1,0:T(8,128)}), f32[4,257,256]{2,1,0:T(8,128)S(1)}, u32[]{:S(2)}, u32[]{:S(2)}) %all-to-all-start) | async-done | bytes 1052704 | tf_op jit(solution)/shard_map/all_to_all | solution.py:40
  80.7 0.1 fusion.10
  80.8 0.2 fusion.40
  81.0 0.2 convolution_add_fusion.1
  81.2 0.3 convolution_add_fusion
  81.5 0.8 copy.21
  82.2 12.9 %all-to-all-start.1 = ((f32[8,16,256]{2,1,0:T(8,128)}), f32[8,16,256]{2,1,0:T(8,128)S(1)}, u32[]{:S(2)}, u32[]{:S(2)}) async-start(f32[8,16,256]{2,1,0:T(8,128)} %bitcast.43), calls=%async_computation.1 | async-start | bytes 262144 | tf_op jit(solution)/shard_map/all_to_all | solution.py:54
  95.1 0.3 fusion.2
  95.4 0.7 copy.22
  96.2 4.7 %all-to-all-done.1 = f32[8,16,256]{2,1,0:T(8,128)S(1)} async-done(((f32[8,16,256]{2,1,0:T(8,128)}), f32[8,16,256]{2,1,0:T(8,128)S(1)}, u32[]{:S(2)}, u32[]{:S(2)}) %all-to-all-start.1) | async-done | bytes 131104 | tf_op jit(solution)/shard_map/all_to_all | solution.py:54
  100.9 0.6 fusion.55
  (30 shorter events, 0.9 us)
Async XLA Ops:
  3.5 16.9 %collective-permute-start = (f32[257,256]{1,0:T(8,128)S(1)}, f32[257,256]{1,0:T(8,128)S(1)}, u32[]{:S(2)}, u32[]{:S(2)}) collective-permute-start(f32[257,256]{1,0:T(8,128)S(1)} %pad_maximum_fusion), channel_id=1, source_target_pairs={{0,8},{8,0},{16,24},{24,16},{32,40},{40,32},{48,56},{56,48},{64,72... | collective-permute-start | bytes 789512 | tf_op jit(solution)/shard_map/ppermute | solution.py:32
  20.5 8.6 %collective-permute-start.1 = (f32[257,256]{1,0:T(8,128)S(1)}, f32[257,256]{1,0:T(8,128)S(1)}, u32[]{:S(2)}, u32[]{:S(2)}) collective-permute-start(f32[257,256]{1,0:T(8,128)S(1)} %pad_maximum_fusion.1), channel_id=1, source_target_pairs={{0,16},{8,24},{16,0},{24,8},{32,48},{40,56},{48,32},{56,40},{64,80... | collective-permute-start | bytes 789512 | tf_op jit(solution)/shard_map/ppermute | solution.py:32
  29.2 9.3 %collective-permute-start.2 = (f32[257,256]{1,0:T(8,128)S(1)}, f32[257,256]{1,0:T(8,128)S(1)}, u32[]{:S(2)}, u32[]{:S(2)}) collective-permute-start(f32[257,256]{1,0:T(8,128)S(1)} %pad_maximum_fusion.2), channel_id=1, source_target_pairs={{0,48},{8,56},{16,32},{24,40},{32,16},{40,24},{48,0},{56,8},{64,11... | collective-permute-start | bytes 789512 | tf_op jit(solution)/shard_map/ppermute | solution.py:32
  38.6 7.2 %collective-permute-start.3 = (f32[257,256]{1,0:T(8,128)S(1)}, f32[257,256]{1,0:T(8,128)S(1)}, u32[]{:S(2)}, u32[]{:S(2)}) collective-permute-start(f32[257,256]{1,0:T(8,128)S(1)} %pad_maximum_fusion.3), channel_id=1, source_target_pairs={{0,64},{8,72},{16,80},{24,88},{32,96},{40,104},{48,112},{56,120},{... | collective-permute-start | bytes 789512 | tf_op jit(solution)/shard_map/ppermute | solution.py:32
  47.0 33.7 %all-to-all-start = ((f32[4,257,256]{2,1,0:T(8,128)}), f32[4,257,256]{2,1,0:T(8,128)S(1)}, u32[]{:S(2)}, u32[]{:S(2)}) async-start(f32[4,257,256]{2,1,0:T(8,128)} %broadcast_in_dim.20), calls=%async_computation | async-start | bytes 2162688 | tf_op jit(solution)/shard_map/all_to_all | solution.py:40
  82.2 18.7 %all-to-all-start.1 = ((f32[8,16,256]{2,1,0:T(8,128)}), f32[8,16,256]{2,1,0:T(8,128)S(1)}, u32[]{:S(2)}, u32[]{:S(2)}) async-start(f32[8,16,256]{2,1,0:T(8,128)} %bitcast.43), calls=%async_computation.1 | async-start | bytes 262144 | tf_op jit(solution)/shard_map/all_to_all | solution.py:54

commit v13 on v11

--- a/solution.py
+++ b/solution.py
@@ -20,21 +20,18 @@
         later = (mine & shift) != 0
         last = shift * 2 >= devices
         if last:
-            message = jnp.concatenate(
-                [jnp.where(later, block_grad, block_state), block_decay[None, :]], axis=0
-            )
-            got = lax.ppermute(message, axis, pairs)
-            got_decay, got_state, got_grad = got[rows], got[:rows], got[:rows]
+            got = lax.ppermute(jnp.where(later, block_grad, block_state), axis, pairs)
+            got_decay, got_state, got_grad = None, got, got
         else:
             message = jnp.concatenate([block_state, block_grad, block_decay[None, :]], axis=0)
             got = lax.ppermute(message, axis, pairs)
             got_decay, got_state, got_grad = got[2 * rows], got[:rows], got[rows : 2 * rows]
         prefix_state = jnp.where(later, prefix_decay[None, :] * got_state + prefix_state, prefix_state)
-        prefix_decay = jnp.where(later, got_decay * prefix_decay, prefix_decay)
         suffix_grad = jnp.where(later, suffix_grad, suffix_decay[None, :] * got_grad + suffix_grad)
-        suffix_decay = jnp.where(later, suffix_decay, got_decay * suffix_decay)
         shift *= 2
         if not last:
+            prefix_decay = jnp.where(later, got_decay * prefix_decay, prefix_decay)
+            suffix_decay = jnp.where(later, suffix_decay, got_decay * suffix_decay)
             block_state = jnp.where(
                 later,
                 block_decay[None, :] * got_state + block_state,

time: 95.4 us -> 95 us (level)
    ppermute x6 -> x5, starting transfers between devices: 33.1 us -> 28.1 us  [scan_both(): got = lax.ppermute(message, axis, pairs)]
    ppermute x0 -> x1, starting transfers between devices: none -> 5 us  [scan_both(): got = lax.ppermute(jnp.where(later, block_grad, block_state), axis, pairs)]
    ppermute x6 -> x5, waiting for transfers between devices: 32.4 us -> 28 us  [scan_both(): got = lax.ppermute(message, axis, pairs)]
    ppermute x0 -> x1, waiting for transfers between devices: none -> 4.08 us  [scan_both(): got = lax.ppermute(jnp.where(later, block_grad, block_state), axis, pairs)]
where the time goes in v13:
time: 95 us; the launch traced here: 94.6 us
  starting transfers between devices  49.4 us (52%)
  waiting for transfers between devices  36.8 us (39%)
  local copies, waits for them, and re-layouts  3.76 us (4%)
  matrix products  2.08 us (2%)
  other arithmetic  1.64 us (2%)
    ppermute x5, starting transfers between devices, scan_both(): got = lax.ppermute(message, axis, pairs)  28.1 us
    ppermute x5, waiting for transfers between devices, scan_both(): got = lax.ppermute(message, axis, pairs)  28 us
    all_to_all x1, starting transfers between devices, scatter_sum(): lax.all_to_all(values.reshape(devices, rows // devices, cols), axis, 0, 0)  16.3 us
    ppermute x1, starting transfers between devices, scan_both(): got = lax.ppermute(jnp.where(later, block_grad, block_state), axis, pairs)  5 us
    all_to_all x1, waiting for transfers between devices, scatter_sum(): lax.all_to_all(values.reshape(devices, rows // devices, cols), axis, 0, 0)  4.73 us
    ppermute x1, waiting for transfers between devices, scan_both(): got = lax.ppermute(jnp.where(later, block_grad, block_state), axis, pairs)  4.08 us
  transfers between devices with their start and end apart: 7, of which 7 were waited for; matrix products, arithmetic and copies ran while one was open for 2% of the time, Pallas kernels for 0%

profile of v13, /device:TPU:1, one launch (start us, length us, event | category | flops | bytes accessed | tf_op | source)
XLA Modules:
  0.0 94.6 jit_solution(16929766856661640758)
XLA Ops:
  0.6 1.0 %reduce_window_sum.11 = f32[8,128]{1,0:T(8,128)S(1)} reduce-window(f32[8,128]{1,0:T(8,128)} %param.8, f32[]{:T(128)} %constant.12.clone.1), window={size=1x128 pad=0_0x127_0}, to_apply=%region_0.0 | reduce-window | flops 130048 | bytes 8196 | tf_op jit(solution)/shard_map/jit(cumsum)/reduce_window_sum | solution.py:73
  1.6 0.2 slice_reduce_fusion
  2.2 0.7 copy-done
  3.0 0.2 fusion.10
  3.4 11.5 %collective-permute-start = (f32[257,256]{1,0:T(8,128)S(1)}, f32[257,256]{1,0:T(8,128)S(1)}, u32[]{:S(2)}, u32[]{:S(2)}) collective-permute-start(f32[257,256]{1,0:T(8,128)S(1)} %pad_maximum_fusion), channel_id=1, source_target_pairs={{0,8},{8,0},{16,24},{24,16},{32,40},{40,32},{48,56},{56,48},{64,72... | collective-permute-start | bytes 789512 | tf_op jit(solution)/shard_map/ppermute | solution.py:27
  15.0 5.3 %collective-permute-done = f32[257,256]{1,0:T(8,128)S(1)} collective-permute-done((f32[257,256]{1,0:T(8,128)S(1)}, f32[257,256]{1,0:T(8,128)S(1)}, u32[]{:S(2)}, u32[]{:S(2)}) %collective-permute-start) | collective-permute-done | bytes 263200 | tf_op jit(solution)/shard_map/ppermute | solution.py:27
  20.4 3.9 %collective-permute-start.1 = (f32[257,256]{1,0:T(8,128)S(1)}, f32[257,256]{1,0:T(8,128)S(1)}, u32[]{:S(2)}, u32[]{:S(2)}) collective-permute-start(f32[257,256]{1,0:T(8,128)S(1)} %pad_maximum_fusion.1), channel_id=1, source_target_pairs={{0,16},{8,24},{16,0},{24,8},{32,48},{40,56},{48,32},{56,40},{64,80... | collective-permute-start | bytes 789512 | tf_op jit(solution)/shard_map/ppermute | solution.py:27
  24.3 4.7 %collective-permute-done.1 = f32[257,256]{1,0:T(8,128)S(1)} collective-permute-done((f32[257,256]{1,0:T(8,128)S(1)}, f32[257,256]{1,0:T(8,128)S(1)}, u32[]{:S(2)}, u32[]{:S(2)}) %collective-permute-start.1) | collective-permute-done | bytes 263200 | tf_op jit(solution)/shard_map/ppermute | solution.py:27
  29.1 5.1 %collective-permute-start.2 = (f32[257,256]{1,0:T(8,128)S(1)}, f32[257,256]{1,0:T(8,128)S(1)}, u32[]{:S(2)}, u32[]{:S(2)}) collective-permute-start(f32[257,256]{1,0:T(8,128)S(1)} %pad_maximum_fusion.2), channel_id=1, source_target_pairs={{0,48},{8,56},{16,32},{24,40},{32,16},{40,24},{48,0},{56,8},{64,11... | collective-permute-start | bytes 789512 | tf_op jit(solution)/shard_map/ppermute | solution.py:27
  34.1 4.2 %collective-permute-done.2 = f32[257,256]{1,0:T(8,128)S(1)} collective-permute-done((f32[257,256]{1,0:T(8,128)S(1)}, f32[257,256]{1,0:T(8,128)S(1)}, u32[]{:S(2)}, u32[]{:S(2)}) %collective-permute-start.2) | collective-permute-done | bytes 263200 | tf_op jit(solution)/shard_map/ppermute | solution.py:27
  38.5 3.3 %collective-permute-start.3 = (f32[257,256]{1,0:T(8,128)S(1)}, f32[257,256]{1,0:T(8,128)S(1)}, u32[]{:S(2)}, u32[]{:S(2)}) collective-permute-start(f32[257,256]{1,0:T(8,128)S(1)} %pad_maximum_fusion.3), channel_id=1, source_target_pairs={{0,64},{8,72},{16,80},{24,88},{32,96},{40,104},{48,112},{56,120},{... | collective-permute-start | bytes 789512 | tf_op jit(solution)/shard_map/ppermute | solution.py:27
  41.9 0.1 copy.15
  42.0 0.1 copy.20
  42.1 0.3 fusion
  42.5 3.2 %collective-permute-done.3 = f32[257,256]{1,0:T(8,128)S(1)} collective-permute-done((f32[257,256]{1,0:T(8,128)S(1)}, f32[257,256]{1,0:T(8,128)S(1)}, u32[]{:S(2)}, u32[]{:S(2)}) %collective-permute-start.3) | collective-permute-done | bytes 263200 | tf_op jit(solution)/shard_map/ppermute | solution.py:27
  45.8 4.3 %collective-permute-start.4 = (f32[257,256]{1,0:T(8,128)S(1)}, f32[257,256]{1,0:T(8,128)S(1)}, u32[]{:S(2)}, u32[]{:S(2)}) collective-permute-start(f32[257,256]{1,0:T(8,128)S(1)} %pad_maximum_fusion.4), channel_id=1, source_target_pairs={{0,128},{8,136},{16,144},{24,152},{32,160},{40,168},{48,176},{56,1... | collective-permute-start | bytes 789512 | tf_op jit(solution)/shard_map/ppermute | solution.py:27
  50.1 0.2 fusion.24
  50.4 0.2 fusion.28
  50.6 10.5 %collective-permute-done.4 = f32[257,256]{1,0:T(8,128)S(1)} collective-permute-done((f32[257,256]{1,0:T(8,128)S(1)}, f32[257,256]{1,0:T(8,128)S(1)}, u32[]{:S(2)}, u32[]{:S(2)}) %collective-permute-start.4) | collective-permute-done | bytes 263200 | tf_op jit(solution)/shard_map/ppermute | solution.py:27
  61.2 5.0 %collective-permute-start.5 = (f32[128,256]{1,0:T(8,128)S(1)}, f32[128,256]{1,0:T(8,128)S(1)}, u32[]{:S(2)}, u32[]{:S(2)}) collective-permute-start(f32[128,256]{1,0:T(8,128)S(1)} %select_select_fusion), channel_id=1, source_target_pairs={{0,448},{8,456},{16,464},{24,472},{32,480},{40,488},{48,496},{56,5... | collective-permute-start | bytes 393224 | tf_op jit(solution)/shard_map/ppermute | solution.py:23
  66.2 0.1 fusion.26
  66.3 4.1 %collective-permute-done.5 = f32[128,256]{1,0:T(8,128)S(1)} collective-permute-done((f32[128,256]{1,0:T(8,128)S(1)}, f32[128,256]{1,0:T(8,128)S(1)}, u32[]{:S(2)}, u32[]{:S(2)}) %collective-permute-start.5) | collective-permute-done | bytes 131104 | tf_op jit(solution)/shard_map/ppermute | solution.py:23
  70.4 0.1 fusion.8
  70.5 0.2 fusion.30
  70.7 0.2 convolution_add_fusion.1
  70.9 0.2 convolution_add_fusion
  71.1 0.8 copy.21
  71.9 16.3 %all-to-all-start = ((f32[8,16,256]{2,1,0:T(8,128)}), f32[8,16,256]{2,1,0:T(8,128)S(1)}, u32[]{:S(2)}, u32[]{:S(2)}) async-start(f32[8,16,256]{2,1,0:T(8,128)} %bitcast.34), calls=%async_computation | async-start | bytes 262144 | tf_op jit(solution)/shard_map/all_to_all | solution.py:52
  88.2 0.3 fusion.2
  88.5 0.7 copy.22
  89.2 4.7 %all-to-all-done = f32[8,16,256]{2,1,0:T(8,128)S(1)} async-done(((f32[8,16,256]{2,1,0:T(8,128)}), f32[8,16,256]{2,1,0:T(8,128)S(1)}, u32[]{:S(2)}, u32[]{:S(2)}) %all-to-all-start) | async-done | bytes 131104 | tf_op jit(solution)/shard_map/all_to_all | solution.py:52
  94.0 0.6 fusion.41
  (39 shorter events, 1.1 us)
Async XLA Ops:
  2.0 0.8 copy-start
  2.0 0.9 copy-start.1
  2.0 0.9 copy-start.2
  2.0 0.8 copy-start.3
  3.4 16.9 %collective-permute-start = (f32[257,256]{1,0:T(8,128)S(1)}, f32[257,256]{1,0:T(8,128)S(1)}, u32[]{:S(2)}, u32[]{:S(2)}) collective-permute-start(f32[257,256]{1,0:T(8,128)S(1)} %pad_maximum_fusion), channel_id=1, source_target_pairs={{0,8},{8,0},{16,24},{24,16},{32,40},{40,32},{48,56},{56,48},{64,72... | collective-permute-start | bytes 789512 | tf_op jit(solution)/shard_map/ppermute | solution.py:27
  20.4 8.6 %collective-permute-start.1 = (f32[257,256]{1,0:T(8,128)S(1)}, f32[257,256]{1,0:T(8,128)S(1)}, u32[]{:S(2)}, u32[]{:S(2)}) collective-permute-start(f32[257,256]{1,0:T(8,128)S(1)} %pad_maximum_fusion.1), channel_id=1, source_target_pairs={{0,16},{8,24},{16,0},{24,8},{32,48},{40,56},{48,32},{56,40},{64,80... | collective-permute-start | bytes 789512 | tf_op jit(solution)/shard_map/ppermute | solution.py:27
  29.1 9.3 %collective-permute-start.2 = (f32[257,256]{1,0:T(8,128)S(1)}, f32[257,256]{1,0:T(8,128)S(1)}, u32[]{:S(2)}, u32[]{:S(2)}) collective-permute-start(f32[257,256]{1,0:T(8,128)S(1)} %pad_maximum_fusion.2), channel_id=1, source_target_pairs={{0,48},{8,56},{16,32},{24,40},{32,16},{40,24},{48,0},{56,8},{64,11... | collective-permute-start | bytes 789512 | tf_op jit(solution)/shard_map/ppermute | solution.py:27
  38.5 7.2 %collective-permute-start.3 = (f32[257,256]{1,0:T(8,128)S(1)}, f32[257,256]{1,0:T(8,128)S(1)}, u32[]{:S(2)}, u32[]{:S(2)}) collective-permute-start(f32[257,256]{1,0:T(8,128)S(1)} %pad_maximum_fusion.3), channel_id=1, source_target_pairs={{0,64},{8,72},{16,80},{24,88},{32,96},{40,104},{48,112},{56,120},{... | collective-permute-start | bytes 789512 | tf_op jit(solution)/shard_map/ppermute | solution.py:27
  45.8 15.3 %collective-permute-start.4 = (f32[257,256]{1,0:T(8,128)S(1)}, f32[257,256]{1,0:T(8,128)S(1)}, u32[]{:S(2)}, u32[]{:S(2)}) collective-permute-start(f32[257,256]{1,0:T(8,128)S(1)} %pad_maximum_fusion.4), channel_id=1, source_target_pairs={{0,128},{8,136},{16,144},{24,152},{32,160},{40,168},{48,176},{56,1... | collective-permute-start | bytes 789512 | tf_op jit(solution)/shard_map/ppermute | solution.py:27
  61.2 9.2 %collective-permute-start.5 = (f32[128,256]{1,0:T(8,128)S(1)}, f32[128,256]{1,0:T(8,128)S(1)}, u32[]{:S(2)}, u32[]{:S(2)}) collective-permute-start(f32[128,256]{1,0:T(8,128)S(1)} %select_select_fusion), channel_id=1, source_target_pairs={{0,448},{8,456},{16,464},{24,472},{32,480},{40,488},{48,496},{56,5... | collective-permute-start | bytes 393224 | tf_op jit(solution)/shard_map/ppermute | solution.py:23
  71.9 22.1 %all-to-all-start = ((f32[8,16,256]{2,1,0:T(8,128)}), f32[8,16,256]{2,1,0:T(8,128)S(1)}, u32[]{:S(2)}, u32[]{:S(2)}) async-start(f32[8,16,256]{2,1,0:T(8,128)} %bitcast.34), calls=%async_computation | async-start | bytes 262144 | tf_op jit(solution)/shard_map/all_to_all | solution.py:52

commit v14 on v13

--- a/solution.py
+++ b/solution.py
@@ -4,7 +4,7 @@
 from jax.sharding import PartitionSpec as P
 
 
-PARTNER_MASKS = {64: {4: 6, 32: 56}}
+PARTNER_MASKS = {64: {4: 6, 16: 24, 32: 56}}
 
 
 def scan_both(decay, state, grad, axis):

time: 95 us -> 92.5 us (0.974)
  the two profiles are of different devices: /device:TPU:1 before, /device:TPU:54 now
where the time goes in v14:
time: 92.5 us; the launch traced here: 92 us
  waiting for transfers between devices  46.7 us (50%)
  starting transfers between devices  36.9 us (40%)
  local copies, waits for them, and re-layouts  3.76 us (4%)
  matrix products  2.08 us (2%)
  other arithmetic  1.64 us (2%)
  between operations  0.95 us (1%)
    ppermute x5, waiting for transfers between devices, scan_both(): got = lax.ppermute(message, axis, pairs)  34.1 us
    ppermute x5, starting transfers between devices, scan_both(): got = lax.ppermute(message, axis, pairs)  21.9 us
    all_to_all x1, starting transfers between devices, scatter_sum(): lax.all_to_all(values.reshape(devices, rows // devices, cols), axis, 0, 0)  12.2 us
    ppermute x1, waiting for transfers between devices, scan_both(): got = lax.ppermute(jnp.where(later, block_grad, block_state), axis, pairs)  6.93 us
    all_to_all x1, waiting for transfers between devices, scatter_sum(): lax.all_to_all(values.reshape(devices, rows // devices, cols), axis, 0, 0)  5.71 us
    ppermute x1, starting transfers between devices, scan_both(): got = lax.ppermute(jnp.where(later, block_grad, block_state), axis, pairs)  2.8 us
  transfers between devices with their start and end apart: 7, of which 7 were waited for; matrix products, arithmetic and copies ran while one was open for 3% of the time, Pallas kernels for 0%

profile of v14, /device:TPU:54, one launch (start us, length us, event | category | flops | bytes accessed | tf_op | source)
XLA Modules:
  0.0 92.0 jit_solution(14932673307085046770)
XLA Ops:
  0.6 1.0 %reduce_window_sum.11 = f32[8,128]{1,0:T(8,128)S(1)} reduce-window(f32[8,128]{1,0:T(8,128)} %param.8, f32[]{:T(128)} %constant.12.clone.1), window={size=1x128 pad=0_0x127_0}, to_apply=%region_0.0 | reduce-window | flops 130048 | bytes 8196 | tf_op jit(solution)/shard_map/jit(cumsum)/reduce_window_sum | solution.py:73
  1.6 0.2 slice_reduce_fusion
  2.2 0.7 copy-done
  3.0 0.2 fusion.10
  3.4 10.9 %collective-permute-start = (f32[257,256]{1,0:T(8,128)S(1)}, f32[257,256]{1,0:T(8,128)S(1)}, u32[]{:S(2)}, u32[]{:S(2)}) collective-permute-start(f32[257,256]{1,0:T(8,128)S(1)} %pad_maximum_fusion), channel_id=1, source_target_pairs={{0,8},{8,0},{16,24},{24,16},{32,40},{40,32},{48,56},{56,48},{64,72... | collective-permute-start | bytes 789512 | tf_op jit(solution)/shard_map/ppermute | solution.py:27
  14.4 6.5 %collective-permute-done = f32[257,256]{1,0:T(8,128)S(1)} collective-permute-done((f32[257,256]{1,0:T(8,128)S(1)}, f32[257,256]{1,0:T(8,128)S(1)}, u32[]{:S(2)}, u32[]{:S(2)}) %collective-permute-start) | collective-permute-done | bytes 263200 | tf_op jit(solution)/shard_map/ppermute | solution.py:27
  21.0 2.7 %collective-permute-start.1 = (f32[257,256]{1,0:T(8,128)S(1)}, f32[257,256]{1,0:T(8,128)S(1)}, u32[]{:S(2)}, u32[]{:S(2)}) collective-permute-start(f32[257,256]{1,0:T(8,128)S(1)} %pad_maximum_fusion.1), channel_id=1, source_target_pairs={{0,16},{8,24},{16,0},{24,8},{32,48},{40,56},{48,32},{56,40},{64,80... | collective-permute-start | bytes 789512 | tf_op jit(solution)/shard_map/ppermute | solution.py:27
  23.8 6.7 %collective-permute-done.1 = f32[257,256]{1,0:T(8,128)S(1)} collective-permute-done((f32[257,256]{1,0:T(8,128)S(1)}, f32[257,256]{1,0:T(8,128)S(1)}, u32[]{:S(2)}, u32[]{:S(2)}) %collective-permute-start.1) | collective-permute-done | bytes 263200 | tf_op jit(solution)/shard_map/ppermute | solution.py:27
  30.5 2.4 %collective-permute-start.2 = (f32[257,256]{1,0:T(8,128)S(1)}, f32[257,256]{1,0:T(8,128)S(1)}, u32[]{:S(2)}, u32[]{:S(2)}) collective-permute-start(f32[257,256]{1,0:T(8,128)S(1)} %pad_maximum_fusion.2), channel_id=1, source_target_pairs={{0,48},{8,56},{16,32},{24,40},{32,16},{40,24},{48,0},{56,8},{64,11... | collective-permute-start | bytes 789512 | tf_op jit(solution)/shard_map/ppermute | solution.py:27
  32.9 7.3 %collective-permute-done.2 = f32[257,256]{1,0:T(8,128)S(1)} collective-permute-done((f32[257,256]{1,0:T(8,128)S(1)}, f32[257,256]{1,0:T(8,128)S(1)}, u32[]{:S(2)}, u32[]{:S(2)}) %collective-permute-start.2) | collective-permute-done | bytes 263200 | tf_op jit(solution)/shard_map/ppermute | solution.py:27
  40.3 2.6 %collective-permute-start.3 = (f32[257,256]{1,0:T(8,128)S(1)}, f32[257,256]{1,0:T(8,128)S(1)}, u32[]{:S(2)}, u32[]{:S(2)}) collective-permute-start(f32[257,256]{1,0:T(8,128)S(1)} %pad_maximum_fusion.3), channel_id=1, source_target_pairs={{0,64},{8,72},{16,80},{24,88},{32,96},{40,104},{48,112},{56,120},{... | collective-permute-start | bytes 789512 | tf_op jit(solution)/shard_map/ppermute | solution.py:27
  42.9 0.1 copy.15
  43.1 0.1 copy.20
  43.2 0.3 fusion
  43.6 5.1 %collective-permute-done.3 = f32[257,256]{1,0:T(8,128)S(1)} collective-permute-done((f32[257,256]{1,0:T(8,128)S(1)}, f32[257,256]{1,0:T(8,128)S(1)}, u32[]{:S(2)}, u32[]{:S(2)}) %collective-permute-start.3) | collective-permute-done | bytes 263200 | tf_op jit(solution)/shard_map/ppermute | solution.py:27
  48.8 3.2 %collective-permute-start.4 = (f32[257,256]{1,0:T(8,128)S(1)}, f32[257,256]{1,0:T(8,128)S(1)}, u32[]{:S(2)}, u32[]{:S(2)}) collective-permute-start(f32[257,256]{1,0:T(8,128)S(1)} %pad_maximum_fusion.4), channel_id=1, source_target_pairs={{0,192},{8,200},{16,208},{24,216},{32,224},{40,232},{48,240},{56,2... | collective-permute-start | bytes 789512 | tf_op jit(solution)/shard_map/ppermute | solution.py:27
  52.0 0.2 fusion.24
  52.3 0.2 fusion.28
  52.5 8.5 %collective-permute-done.4 = f32[257,256]{1,0:T(8,128)S(1)} collective-permute-done((f32[257,256]{1,0:T(8,128)S(1)}, f32[257,256]{1,0:T(8,128)S(1)}, u32[]{:S(2)}, u32[]{:S(2)}) %collective-permute-start.4) | collective-permute-done | bytes 263200 | tf_op jit(solution)/shard_map/ppermute | solution.py:27
  61.1 2.8 %collective-permute-start.5 = (f32[128,256]{1,0:T(8,128)S(1)}, f32[128,256]{1,0:T(8,128)S(1)}, u32[]{:S(2)}, u32[]{:S(2)}) collective-permute-start(f32[128,256]{1,0:T(8,128)S(1)} %select_select_fusion), channel_id=1, source_target_pairs={{0,448},{8,456},{16,464},{24,472},{32,480},{40,488},{48,496},{56,5... | collective-permute-start | bytes 393224 | tf_op jit(solution)/shard_map/ppermute | solution.py:23
  63.9 0.1 fusion.26
  64.0 6.9 %collective-permute-done.5 = f32[128,256]{1,0:T(8,128)S(1)} collective-permute-done((f32[128,256]{1,0:T(8,128)S(1)}, f32[128,256]{1,0:T(8,128)S(1)}, u32[]{:S(2)}, u32[]{:S(2)}) %collective-permute-start.5) | collective-permute-done | bytes 131104 | tf_op jit(solution)/shard_map/ppermute | solution.py:23
  70.9 0.1 fusion.8
  71.0 0.2 fusion.30
  71.3 0.2 convolution_add_fusion.1
  71.4 0.2 convolution_add_fusion
  71.7 0.8 copy.21
  72.4 12.2 %all-to-all-start = ((f32[8,16,256]{2,1,0:T(8,128)}), f32[8,16,256]{2,1,0:T(8,128)S(1)}, u32[]{:S(2)}, u32[]{:S(2)}) async-start(f32[8,16,256]{2,1,0:T(8,128)} %bitcast.34), calls=%async_computation | async-start | bytes 262144 | tf_op jit(solution)/shard_map/all_to_all | solution.py:52
  84.6 0.3 fusion.2
  85.0 0.7 copy.22
  85.7 5.7 %all-to-all-done = f32[8,16,256]{2,1,0:T(8,128)S(1)} async-done(((f32[8,16,256]{2,1,0:T(8,128)}), f32[8,16,256]{2,1,0:T(8,128)S(1)}, u32[]{:S(2)}, u32[]{:S(2)}) %all-to-all-start) | async-done | bytes 131104 | tf_op jit(solution)/shard_map/all_to_all | solution.py:52
  91.4 0.6 fusion.41
  (39 shorter events, 1.1 us)
Async XLA Ops:
  2.0 0.8 copy-start
  2.0 0.9 copy-start.1
  2.0 0.9 copy-start.2
  2.0 0.8 copy-start.3
  3.4 17.5 %collective-permute-start = (f32[257,256]{1,0:T(8,128)S(1)}, f32[257,256]{1,0:T(8,128)S(1)}, u32[]{:S(2)}, u32[]{:S(2)}) collective-permute-start(f32[257,256]{1,0:T(8,128)S(1)} %pad_maximum_fusion), channel_id=1, source_target_pairs={{0,8},{8,0},{16,24},{24,16},{32,40},{40,32},{48,56},{56,48},{64,72... | collective-permute-start | bytes 789512 | tf_op jit(solution)/shard_map/ppermute | solution.py:27
  21.0 9.4 %collective-permute-start.1 = (f32[257,256]{1,0:T(8,128)S(1)}, f32[257,256]{1,0:T(8,128)S(1)}, u32[]{:S(2)}, u32[]{:S(2)}) collective-permute-start(f32[257,256]{1,0:T(8,128)S(1)} %pad_maximum_fusion.1), channel_id=1, source_target_pairs={{0,16},{8,24},{16,0},{24,8},{32,48},{40,56},{48,32},{56,40},{64,80... | collective-permute-start | bytes 789512 | tf_op jit(solution)/shard_map/ppermute | solution.py:27
  30.5 9.7 %collective-permute-start.2 = (f32[257,256]{1,0:T(8,128)S(1)}, f32[257,256]{1,0:T(8,128)S(1)}, u32[]{:S(2)}, u32[]{:S(2)}) collective-permute-start(f32[257,256]{1,0:T(8,128)S(1)} %pad_maximum_fusion.2), channel_id=1, source_target_pairs={{0,48},{8,56},{16,32},{24,40},{32,16},{40,24},{48,0},{56,8},{64,11... | collective-permute-start | bytes 789512 | tf_op jit(solution)/shard_map/ppermute | solution.py:27
  40.3 8.4 %collective-permute-start.3 = (f32[257,256]{1,0:T(8,128)S(1)}, f32[257,256]{1,0:T(8,128)S(1)}, u32[]{:S(2)}, u32[]{:S(2)}) collective-permute-start(f32[257,256]{1,0:T(8,128)S(1)} %pad_maximum_fusion.3), channel_id=1, source_target_pairs={{0,64},{8,72},{16,80},{24,88},{32,96},{40,104},{48,112},{56,120},{... | collective-permute-start | bytes 789512 | tf_op jit(solution)/shard_map/ppermute | solution.py:27
  48.8 12.2 %collective-permute-start.4 = (f32[257,256]{1,0:T(8,128)S(1)}, f32[257,256]{1,0:T(8,128)S(1)}, u32[]{:S(2)}, u32[]{:S(2)}) collective-permute-start(f32[257,256]{1,0:T(8,128)S(1)} %pad_maximum_fusion.4), channel_id=1, source_target_pairs={{0,192},{8,200},{16,208},{24,216},{32,224},{40,232},{48,240},{56,2... | collective-permute-start | bytes 789512 | tf_op jit(solution)/shard_map/ppermute | solution.py:27
  61.1 9.9 %collective-permute-start.5 = (f32[128,256]{1,0:T(8,128)S(1)}, f32[128,256]{1,0:T(8,128)S(1)}, u32[]{:S(2)}, u32[]{:S(2)}) collective-permute-start(f32[128,256]{1,0:T(8,128)S(1)} %select_select_fusion), channel_id=1, source_target_pairs={{0,448},{8,456},{16,464},{24,472},{32,480},{40,488},{48,496},{56,5... | collective-permute-start | bytes 393224 | tf_op jit(solution)/shard_map/ppermute | solution.py:23
  72.4 19.0 %all-to-all-start = ((f32[8,16,256]{2,1,0:T(8,128)}), f32[8,16,256]{2,1,0:T(8,128)S(1)}, u32[]{:S(2)}, u32[]{:S(2)}) async-start(f32[8,16,256]{2,1,0:T(8,128)} %bitcast.34), calls=%async_computation | async-start | bytes 262144 | tf_op jit(solution)/shard_map/all_to_all | solution.py:52

commit v15 on v14

--- a/solution.py
+++ b/solution.py
@@ -4,7 +4,7 @@
 from jax.sharding import PartitionSpec as P
 
 
-PARTNER_MASKS = {64: {4: 6, 16: 24, 32: 56}}
+PARTNER_MASKS = {64: {4: 6, 16: 24, 32: 48}}
 
 
 def scan_both(decay, state, grad, axis):

time: 92.5 us -> 93.9 us (1.015)
  the two profiles are of different devices: /device:TPU:54 before, /device:TPU:14 now
where the time goes in v15:
time: 93.9 us; the launch traced here: 93.5 us
  waiting for transfers between devices  46.7 us (50%)
  starting transfers between devices  38.3 us (41%)
  local copies, waits for them, and re-layouts  3.76 us (4%)
  matrix products  2.09 us (2%)
  other arithmetic  1.64 us (2%)
  between operations  0.95 us (1%)
    ppermute x5, waiting for transfers between devices, scan_both(): got = lax.ppermute(message, axis, pairs)  34.1 us
    ppermute x5, starting transfers between devices, scan_both(): got = lax.ppermute(message, axis, pairs)  21.9 us
    all_to_all x1, starting transfers between devices, scatter_sum(): lax.all_to_all(values.reshape(devices, rows // devices, cols), axis, 0, 0)  13.1 us
    ppermute x1, waiting for transfers between devices, scan_both(): got = lax.ppermute(jnp.where(later, block_grad, block_state), axis, pairs)  6.93 us
    all_to_all x1, waiting for transfers between devices, scatter_sum(): lax.all_to_all(values.reshape(devices, rows // devices, cols), axis, 0, 0)  5.71 us
    ppermute x1, starting transfers between devices, scan_both(): got = lax.ppermute(jnp.where(later, block_grad, block_state), axis, pairs)  3.31 us
  transfers between devices with their start and end apart: 7, of which 7 were waited for; matrix products, arithmetic and copies ran while one was open for 3% of the time, Pallas kernels for 0%

profile of v15, /device:TPU:14, one launch (start us, length us, event | category | flops | bytes accessed | tf_op | source)
XLA Modules:
  0.0 93.5 jit_solution(13035599660267411360)
XLA Ops:
  0.6 1.0 %reduce_window_sum.11 = f32[8,128]{1,0:T(8,128)S(1)} reduce-window(f32[8,128]{1,0:T(8,128)} %param.8, f32[]{:T(128)} %constant.12.clone.1), window={size=1x128 pad=0_0x127_0}, to_apply=%region_0.0 | reduce-window | flops 130048 | bytes 8196 | tf_op jit(solution)/shard_map/jit(cumsum)/reduce_window_sum | solution.py:73
  1.6 0.2 slice_reduce_fusion
  2.2 0.7 copy-done
  3.0 0.2 fusion.10
  3.4 10.9 %collective-permute-start = (f32[257,256]{1,0:T(8,128)S(1)}, f32[257,256]{1,0:T(8,128)S(1)}, u32[]{:S(2)}, u32[]{:S(2)}) collective-permute-start(f32[257,256]{1,0:T(8,128)S(1)} %pad_maximum_fusion), channel_id=1, source_target_pairs={{0,8},{8,0},{16,24},{24,16},{32,40},{40,32},{48,56},{56,48},{64,72... | collective-permute-start | bytes 789512 | tf_op jit(solution)/shard_map/ppermute | solution.py:27
  14.4 6.5 %collective-permute-done = f32[257,256]{1,0:T(8,128)S(1)} collective-permute-done((f32[257,256]{1,0:T(8,128)S(1)}, f32[257,256]{1,0:T(8,128)S(1)}, u32[]{:S(2)}, u32[]{:S(2)}) %collective-permute-start) | collective-permute-done | bytes 263200 | tf_op jit(solution)/shard_map/ppermute | solution.py:27
  21.0 2.7 %collective-permute-start.1 = (f32[257,256]{1,0:T(8,128)S(1)}, f32[257,256]{1,0:T(8,128)S(1)}, u32[]{:S(2)}, u32[]{:S(2)}) collective-permute-start(f32[257,256]{1,0:T(8,128)S(1)} %pad_maximum_fusion.1), channel_id=1, source_target_pairs={{0,16},{8,24},{16,0},{24,8},{32,48},{40,56},{48,32},{56,40},{64,80... | collective-permute-start | bytes 789512 | tf_op jit(solution)/shard_map/ppermute | solution.py:27
  23.8 6.7 %collective-permute-done.1 = f32[257,256]{1,0:T(8,128)S(1)} collective-permute-done((f32[257,256]{1,0:T(8,128)S(1)}, f32[257,256]{1,0:T(8,128)S(1)}, u32[]{:S(2)}, u32[]{:S(2)}) %collective-permute-start.1) | collective-permute-done | bytes 263200 | tf_op jit(solution)/shard_map/ppermute | solution.py:27
  30.5 2.4 %collective-permute-start.2 = (f32[257,256]{1,0:T(8,128)S(1)}, f32[257,256]{1,0:T(8,128)S(1)}, u32[]{:S(2)}, u32[]{:S(2)}) collective-permute-start(f32[257,256]{1,0:T(8,128)S(1)} %pad_maximum_fusion.2), channel_id=1, source_target_pairs={{0,48},{8,56},{16,32},{24,40},{32,16},{40,24},{48,0},{56,8},{64,11... | collective-permute-start | bytes 789512 | tf_op jit(solution)/shard_map/ppermute | solution.py:27
  32.9 7.3 %collective-permute-done.2 = f32[257,256]{1,0:T(8,128)S(1)} collective-permute-done((f32[257,256]{1,0:T(8,128)S(1)}, f32[257,256]{1,0:T(8,128)S(1)}, u32[]{:S(2)}, u32[]{:S(2)}) %collective-permute-start.2) | collective-permute-done | bytes 263200 | tf_op jit(solution)/shard_map/ppermute | solution.py:27
  40.3 2.4 %collective-permute-start.3 = (f32[257,256]{1,0:T(8,128)S(1)}, f32[257,256]{1,0:T(8,128)S(1)}, u32[]{:S(2)}, u32[]{:S(2)}) collective-permute-start(f32[257,256]{1,0:T(8,128)S(1)} %pad_maximum_fusion.3), channel_id=1, source_target_pairs={{0,64},{8,72},{16,80},{24,88},{32,96},{40,104},{48,112},{56,120},{... | collective-permute-start | bytes 789512 | tf_op jit(solution)/shard_map/ppermute | solution.py:27
  42.7 0.1 copy.15
  42.8 0.1 copy.20
  43.0 0.3 fusion
  43.3 5.4 %collective-permute-done.3 = f32[257,256]{1,0:T(8,128)S(1)} collective-permute-done((f32[257,256]{1,0:T(8,128)S(1)}, f32[257,256]{1,0:T(8,128)S(1)}, u32[]{:S(2)}, u32[]{:S(2)}) %collective-permute-start.3) | collective-permute-done | bytes 263200 | tf_op jit(solution)/shard_map/ppermute | solution.py:27
  48.8 3.5 %collective-permute-start.4 = (f32[257,256]{1,0:T(8,128)S(1)}, f32[257,256]{1,0:T(8,128)S(1)}, u32[]{:S(2)}, u32[]{:S(2)}) collective-permute-start(f32[257,256]{1,0:T(8,128)S(1)} %pad_maximum_fusion.4), channel_id=1, source_target_pairs={{0,192},{8,200},{16,208},{24,216},{32,224},{40,232},{48,240},{56,2... | collective-permute-start | bytes 789512 | tf_op jit(solution)/shard_map/ppermute | solution.py:27
  52.3 0.2 fusion.24
  52.5 0.2 fusion.28
  52.8 8.2 %collective-permute-done.4 = f32[257,256]{1,0:T(8,128)S(1)} collective-permute-done((f32[257,256]{1,0:T(8,128)S(1)}, f32[257,256]{1,0:T(8,128)S(1)}, u32[]{:S(2)}, u32[]{:S(2)}) %collective-permute-start.4) | collective-permute-done | bytes 263200 | tf_op jit(solution)/shard_map/ppermute | solution.py:27
  61.1 3.3 %collective-permute-start.5 = (f32[128,256]{1,0:T(8,128)S(1)}, f32[128,256]{1,0:T(8,128)S(1)}, u32[]{:S(2)}, u32[]{:S(2)}) collective-permute-start(f32[128,256]{1,0:T(8,128)S(1)} %select_select_fusion), channel_id=1, source_target_pairs={{0,384},{8,392},{16,400},{24,408},{32,416},{40,424},{48,432},{56,4... | collective-permute-start | bytes 393224 | tf_op jit(solution)/shard_map/ppermute | solution.py:23
  64.4 0.1 fusion.26
  64.5 6.9 %collective-permute-done.5 = f32[128,256]{1,0:T(8,128)S(1)} collective-permute-done((f32[128,256]{1,0:T(8,128)S(1)}, f32[128,256]{1,0:T(8,128)S(1)}, u32[]{:S(2)}, u32[]{:S(2)}) %collective-permute-start.5) | collective-permute-done | bytes 131104 | tf_op jit(solution)/shard_map/ppermute | solution.py:23
  71.5 0.1 fusion.8
  71.6 0.2 fusion.30
  71.8 0.2 convolution_add_fusion.1
  71.9 0.2 convolution_add_fusion
  72.2 0.8 copy.21
  72.9 13.1 %all-to-all-start = ((f32[8,16,256]{2,1,0:T(8,128)}), f32[8,16,256]{2,1,0:T(8,128)S(1)}, u32[]{:S(2)}, u32[]{:S(2)}) async-start(f32[8,16,256]{2,1,0:T(8,128)} %bitcast.34), calls=%async_computation | async-start | bytes 262144 | tf_op jit(solution)/shard_map/all_to_all | solution.py:52
  86.1 0.3 fusion.2
  86.4 0.7 copy.22
  87.1 5.7 %all-to-all-done = f32[8,16,256]{2,1,0:T(8,128)S(1)} async-done(((f32[8,16,256]{2,1,0:T(8,128)}), f32[8,16,256]{2,1,0:T(8,128)S(1)}, u32[]{:S(2)}, u32[]{:S(2)}) %all-to-all-start) | async-done | bytes 131104 | tf_op jit(solution)/shard_map/all_to_all | solution.py:52
  92.9 0.6 fusion.41
  (39 shorter events, 1.1 us)
Async XLA Ops:
  2.0 0.8 copy-start
  2.0 0.9 copy-start.1
  2.0 0.9 copy-start.2
  2.0 0.8 copy-start.3
  3.4 17.5 %collective-permute-start = (f32[257,256]{1,0:T(8,128)S(1)}, f32[257,256]{1,0:T(8,128)S(1)}, u32[]{:S(2)}, u32[]{:S(2)}) collective-permute-start(f32[257,256]{1,0:T(8,128)S(1)} %pad_maximum_fusion), channel_id=1, source_target_pairs={{0,8},{8,0},{16,24},{24,16},{32,40},{40,32},{48,56},{56,48},{64,72... | collective-permute-start | bytes 789512 | tf_op jit(solution)/shard_map/ppermute | solution.py:27
  21.0 9.4 %collective-permute-start.1 = (f32[257,256]{1,0:T(8,128)S(1)}, f32[257,256]{1,0:T(8,128)S(1)}, u32[]{:S(2)}, u32[]{:S(2)}) collective-permute-start(f32[257,256]{1,0:T(8,128)S(1)} %pad_maximum_fusion.1), channel_id=1, source_target_pairs={{0,16},{8,24},{16,0},{24,8},{32,48},{40,56},{48,32},{56,40},{64,80... | collective-permute-start | bytes 789512 | tf_op jit(solution)/shard_map/ppermute | solution.py:27
  30.5 9.7 %collective-permute-start.2 = (f32[257,256]{1,0:T(8,128)S(1)}, f32[257,256]{1,0:T(8,128)S(1)}, u32[]{:S(2)}, u32[]{:S(2)}) collective-permute-start(f32[257,256]{1,0:T(8,128)S(1)} %pad_maximum_fusion.2), channel_id=1, source_target_pairs={{0,48},{8,56},{16,32},{24,40},{32,16},{40,24},{48,0},{56,8},{64,11... | collective-permute-start | bytes 789512 | tf_op jit(solution)/shard_map/ppermute | solution.py:27
  40.3 8.4 %collective-permute-start.3 = (f32[257,256]{1,0:T(8,128)S(1)}, f32[257,256]{1,0:T(8,128)S(1)}, u32[]{:S(2)}, u32[]{:S(2)}) collective-permute-start(f32[257,256]{1,0:T(8,128)S(1)} %pad_maximum_fusion.3), channel_id=1, source_target_pairs={{0,64},{8,72},{16,80},{24,88},{32,96},{40,104},{48,112},{56,120},{... | collective-permute-start | bytes 789512 | tf_op jit(solution)/shard_map/ppermute | solution.py:27
  48.8 12.2 %collective-permute-start.4 = (f32[257,256]{1,0:T(8,128)S(1)}, f32[257,256]{1,0:T(8,128)S(1)}, u32[]{:S(2)}, u32[]{:S(2)}) collective-permute-start(f32[257,256]{1,0:T(8,128)S(1)} %pad_maximum_fusion.4), channel_id=1, source_target_pairs={{0,192},{8,200},{16,208},{24,216},{32,224},{40,232},{48,240},{56,2... | collective-permute-start | bytes 789512 | tf_op jit(solution)/shard_map/ppermute | solution.py:27
  61.1 10.4 %collective-permute-start.5 = (f32[128,256]{1,0:T(8,128)S(1)}, f32[128,256]{1,0:T(8,128)S(1)}, u32[]{:S(2)}, u32[]{:S(2)}) collective-permute-start(f32[128,256]{1,0:T(8,128)S(1)} %select_select_fusion), channel_id=1, source_target_pairs={{0,384},{8,392},{16,400},{24,408},{32,416},{40,424},{48,432},{56,4... | collective-permute-start | bytes 393224 | tf_op jit(solution)/shard_map/ppermute | solution.py:23
  72.9 19.9 %all-to-all-start = ((f32[8,16,256]{2,1,0:T(8,128)}), f32[8,16,256]{2,1,0:T(8,128)S(1)}, u32[]{:S(2)}, u32[]{:S(2)}) async-start(f32[8,16,256]{2,1,0:T(8,128)} %bitcast.34), calls=%async_computation | async-start | bytes 262144 | tf_op jit(solution)/shard_map/all_to_all | solution.py:52

commit v16 on v15

--- a/solution.py
+++ b/solution.py
@@ -4,7 +4,7 @@
 from jax.sharding import PartitionSpec as P
 
 
-PARTNER_MASKS = {64: {4: 6, 16: 24, 32: 48}}
+PARTNER_MASKS = {64: {4: 6, 8: 14, 16: 24, 32: 56}}
 
 
 def scan_both(decay, state, grad, axis):

time: 93.9 us -> 94.6 us (level)
  the two profiles are of different devices: /device:TPU:14 before, /device:TPU:48 now
where the time goes in v16:
time: 94.6 us; the launch traced here: 94.1 us
  waiting for transfers between devices  43.7 us (46%)
  starting transfers between devices  42 us (44%)
  local copies, waits for them, and re-layouts  3.76 us (4%)
  matrix products  2.08 us (2%)
  other arithmetic  1.64 us (2%)
  between operations  0.95 us (1%)
    ppermute x5, waiting for transfers between devices, scan_both(): got = lax.ppermute(message, axis, pairs)  31.1 us
    ppermute x5, starting transfers between devices, scan_both(): got = lax.ppermute(message, axis, pairs)  27 us
    all_to_all x1, starting transfers between devices, scatter_sum(): lax.all_to_all(values.reshape(devices, rows // devices, cols), axis, 0, 0)  12.2 us
    ppermute x1, waiting for transfers between devices, scan_both(): got = lax.ppermute(jnp.where(later, block_grad, block_state), axis, pairs)  6.93 us
    all_to_all x1, waiting for transfers between devices, scatter_sum(): lax.all_to_all(values.reshape(devices, rows // devices, cols), axis, 0, 0)  5.71 us
    ppermute x1, starting transfers between devices, scan_both(): got = lax.ppermute(jnp.where(later, block_grad, block_state), axis, pairs)  2.8 us
  transfers between devices with their start and end apart: 7, of which 7 were waited for; matrix products, arithmetic and copies ran while one was open for 2% of the time, Pallas kernels for 0%

profile of v16, /device:TPU:48, one launch (start us, length us, event | category | flops | bytes accessed | tf_op | source)
XLA Modules:
  0.0 94.1 jit_solution(3309760192136391594)
XLA Ops:
  0.6 1.0 %reduce_window_sum.11 = f32[8,128]{1,0:T(8,128)S(1)} reduce-window(f32[8,128]{1,0:T(8,128)} %param.8, f32[]{:T(128)} %constant.12.clone.1), window={size=1x128 pad=0_0x127_0}, to_apply=%region_0.0 | reduce-window | flops 130048 | bytes 8196 | tf_op jit(solution)/shard_map/jit(cumsum)/reduce_window_sum | solution.py:73
  1.6 0.2 slice_reduce_fusion
  2.2 0.7 copy-done
  3.0 0.2 fusion.10
  3.4 10.9 %collective-permute-start = (f32[257,256]{1,0:T(8,128)S(1)}, f32[257,256]{1,0:T(8,128)S(1)}, u32[]{:S(2)}, u32[]{:S(2)}) collective-permute-start(f32[257,256]{1,0:T(8,128)S(1)} %pad_maximum_fusion), channel_id=1, source_target_pairs={{0,8},{8,0},{16,24},{24,16},{32,40},{40,32},{48,56},{56,48},{64,72... | collective-permute-start | bytes 789512 | tf_op jit(solution)/shard_map/ppermute | solution.py:27
  14.4 6.5 %collective-permute-done = f32[257,256]{1,0:T(8,128)S(1)} collective-permute-done((f32[257,256]{1,0:T(8,128)S(1)}, f32[257,256]{1,0:T(8,128)S(1)}, u32[]{:S(2)}, u32[]{:S(2)}) %collective-permute-start) | collective-permute-done | bytes 263200 | tf_op jit(solution)/shard_map/ppermute | solution.py:27
  21.0 3.4 %collective-permute-start.1 = (f32[257,256]{1,0:T(8,128)S(1)}, f32[257,256]{1,0:T(8,128)S(1)}, u32[]{:S(2)}, u32[]{:S(2)}) collective-permute-start(f32[257,256]{1,0:T(8,128)S(1)} %pad_maximum_fusion.1), channel_id=1, source_target_pairs={{0,16},{8,24},{16,0},{24,8},{32,48},{40,56},{48,32},{56,40},{64,80... | collective-permute-start | bytes 789512 | tf_op jit(solution)/shard_map/ppermute | solution.py:27
  24.4 6.0 %collective-permute-done.1 = f32[257,256]{1,0:T(8,128)S(1)} collective-permute-done((f32[257,256]{1,0:T(8,128)S(1)}, f32[257,256]{1,0:T(8,128)S(1)}, u32[]{:S(2)}, u32[]{:S(2)}) %collective-permute-start.1) | collective-permute-done | bytes 263200 | tf_op jit(solution)/shard_map/ppermute | solution.py:27
  30.5 4.7 %collective-permute-start.2 = (f32[257,256]{1,0:T(8,128)S(1)}, f32[257,256]{1,0:T(8,128)S(1)}, u32[]{:S(2)}, u32[]{:S(2)}) collective-permute-start(f32[257,256]{1,0:T(8,128)S(1)} %pad_maximum_fusion.2), channel_id=1, source_target_pairs={{0,48},{8,56},{16,32},{24,40},{32,16},{40,24},{48,0},{56,8},{64,11... | collective-permute-start | bytes 789512 | tf_op jit(solution)/shard_map/ppermute | solution.py:27
  35.2 5.0 %collective-permute-done.2 = f32[257,256]{1,0:T(8,128)S(1)} collective-permute-done((f32[257,256]{1,0:T(8,128)S(1)}, f32[257,256]{1,0:T(8,128)S(1)}, u32[]{:S(2)}, u32[]{:S(2)}) %collective-permute-start.2) | collective-permute-done | bytes 263200 | tf_op jit(solution)/shard_map/ppermute | solution.py:27
  40.3 4.8 %collective-permute-start.3 = (f32[257,256]{1,0:T(8,128)S(1)}, f32[257,256]{1,0:T(8,128)S(1)}, u32[]{:S(2)}, u32[]{:S(2)}) collective-permute-start(f32[257,256]{1,0:T(8,128)S(1)} %pad_maximum_fusion.3), channel_id=1, source_target_pairs={{0,112},{8,120},{16,96},{24,104},{32,80},{40,88},{48,64},{56,72},{... | collective-permute-start | bytes 789512 | tf_op jit(solution)/shard_map/ppermute | solution.py:27
  45.1 0.1 copy.15
  45.3 0.1 copy.20
  45.4 0.3 fusion
  45.7 5.0 %collective-permute-done.3 = f32[257,256]{1,0:T(8,128)S(1)} collective-permute-done((f32[257,256]{1,0:T(8,128)S(1)}, f32[257,256]{1,0:T(8,128)S(1)}, u32[]{:S(2)}, u32[]{:S(2)}) %collective-permute-start.3) | collective-permute-done | bytes 263200 | tf_op jit(solution)/shard_map/ppermute | solution.py:27
  50.9 3.3 %collective-permute-start.4 = (f32[257,256]{1,0:T(8,128)S(1)}, f32[257,256]{1,0:T(8,128)S(1)}, u32[]{:S(2)}, u32[]{:S(2)}) collective-permute-start(f32[257,256]{1,0:T(8,128)S(1)} %pad_maximum_fusion.4), channel_id=1, source_target_pairs={{0,192},{8,200},{16,208},{24,216},{32,224},{40,232},{48,240},{56,2... | collective-permute-start | bytes 789512 | tf_op jit(solution)/shard_map/ppermute | solution.py:27
  54.2 0.2 fusion.24
  54.4 0.2 fusion.28
  54.7 8.5 %collective-permute-done.4 = f32[257,256]{1,0:T(8,128)S(1)} collective-permute-done((f32[257,256]{1,0:T(8,128)S(1)}, f32[257,256]{1,0:T(8,128)S(1)}, u32[]{:S(2)}, u32[]{:S(2)}) %collective-permute-start.4) | collective-permute-done | bytes 263200 | tf_op jit(solution)/shard_map/ppermute | solution.py:27
  63.2 2.8 %collective-permute-start.5 = (f32[128,256]{1,0:T(8,128)S(1)}, f32[128,256]{1,0:T(8,128)S(1)}, u32[]{:S(2)}, u32[]{:S(2)}) collective-permute-start(f32[128,256]{1,0:T(8,128)S(1)} %select_select_fusion), channel_id=1, source_target_pairs={{0,448},{8,456},{16,464},{24,472},{32,480},{40,488},{48,496},{56,5... | collective-permute-start | bytes 393224 | tf_op jit(solution)/shard_map/ppermute | solution.py:23
  66.0 0.1 fusion.26
  66.1 6.9 %collective-permute-done.5 = f32[128,256]{1,0:T(8,128)S(1)} collective-permute-done((f32[128,256]{1,0:T(8,128)S(1)}, f32[128,256]{1,0:T(8,128)S(1)}, u32[]{:S(2)}, u32[]{:S(2)}) %collective-permute-start.5) | collective-permute-done | bytes 131104 | tf_op jit(solution)/shard_map/ppermute | solution.py:23
  73.1 0.1 fusion.8
  73.2 0.2 fusion.30
  73.4 0.2 convolution_add_fusion.1
  73.5 0.2 convolution_add_fusion
  73.8 0.8 copy.21
  74.5 12.2 %all-to-all-start = ((f32[8,16,256]{2,1,0:T(8,128)}), f32[8,16,256]{2,1,0:T(8,128)S(1)}, u32[]{:S(2)}, u32[]{:S(2)}) async-start(f32[8,16,256]{2,1,0:T(8,128)} %bitcast.34), calls=%async_computation | async-start | bytes 262144 | tf_op jit(solution)/shard_map/all_to_all | solution.py:52
  86.7 0.3 fusion.2
  87.1 0.7 copy.22
  87.8 5.7 %all-to-all-done = f32[8,16,256]{2,1,0:T(8,128)S(1)} async-done(((f32[8,16,256]{2,1,0:T(8,128)}), f32[8,16,256]{2,1,0:T(8,128)S(1)}, u32[]{:S(2)}, u32[]{:S(2)}) %all-to-all-start) | async-done | bytes 131104 | tf_op jit(solution)/shard_map/all_to_all | solution.py:52
  93.5 0.6 fusion.41
  (39 shorter events, 1.1 us)
Async XLA Ops:
  2.0 0.8 copy-start
  2.0 0.9 copy-start.1
  2.0 0.9 copy-start.2
  2.0 0.8 copy-start.3
  3.4 17.5 %collective-permute-start = (f32[257,256]{1,0:T(8,128)S(1)}, f32[257,256]{1,0:T(8,128)S(1)}, u32[]{:S(2)}, u32[]{:S(2)}) collective-permute-start(f32[257,256]{1,0:T(8,128)S(1)} %pad_maximum_fusion), channel_id=1, source_target_pairs={{0,8},{8,0},{16,24},{24,16},{32,40},{40,32},{48,56},{56,48},{64,72... | collective-permute-start | bytes 789512 | tf_op jit(solution)/shard_map/ppermute | solution.py:27
  21.0 9.4 %collective-permute-start.1 = (f32[257,256]{1,0:T(8,128)S(1)}, f32[257,256]{1,0:T(8,128)S(1)}, u32[]{:S(2)}, u32[]{:S(2)}) collective-permute-start(f32[257,256]{1,0:T(8,128)S(1)} %pad_maximum_fusion.1), channel_id=1, source_target_pairs={{0,16},{8,24},{16,0},{24,8},{32,48},{40,56},{48,32},{56,40},{64,80... | collective-permute-start | bytes 789512 | tf_op jit(solution)/shard_map/ppermute | solution.py:27
  30.5 9.7 %collective-permute-start.2 = (f32[257,256]{1,0:T(8,128)S(1)}, f32[257,256]{1,0:T(8,128)S(1)}, u32[]{:S(2)}, u32[]{:S(2)}) collective-permute-start(f32[257,256]{1,0:T(8,128)S(1)} %pad_maximum_fusion.2), channel_id=1, source_target_pairs={{0,48},{8,56},{16,32},{24,40},{32,16},{40,24},{48,0},{56,8},{64,11... | collective-permute-start | bytes 789512 | tf_op jit(solution)/shard_map/ppermute | solution.py:27
  40.3 10.5 %collective-permute-start.3 = (f32[257,256]{1,0:T(8,128)S(1)}, f32[257,256]{1,0:T(8,128)S(1)}, u32[]{:S(2)}, u32[]{:S(2)}) collective-permute-start(f32[257,256]{1,0:T(8,128)S(1)} %pad_maximum_fusion.3), channel_id=1, source_target_pairs={{0,112},{8,120},{16,96},{24,104},{32,80},{40,88},{48,64},{56,72},{... | collective-permute-start | bytes 789512 | tf_op jit(solution)/shard_map/ppermute | solution.py:27
  50.9 12.2 %collective-permute-start.4 = (f32[257,256]{1,0:T(8,128)S(1)}, f32[257,256]{1,0:T(8,128)S(1)}, u32[]{:S(2)}, u32[]{:S(2)}) collective-permute-start(f32[257,256]{1,0:T(8,128)S(1)} %pad_maximum_fusion.4), channel_id=1, source_target_pairs={{0,192},{8,200},{16,208},{24,216},{32,224},{40,232},{48,240},{56,2... | collective-permute-start | bytes 789512 | tf_op jit(solution)/shard_map/ppermute | solution.py:27
  63.2 9.9 %collective-permute-start.5 = (f32[128,256]{1,0:T(8,128)S(1)}, f32[128,256]{1,0:T(8,128)S(1)}, u32[]{:S(2)}, u32[]{:S(2)}) collective-permute-start(f32[128,256]{1,0:T(8,128)S(1)} %select_select_fusion), channel_id=1, source_target_pairs={{0,448},{8,456},{16,464},{24,472},{32,480},{40,488},{48,496},{56,5... | collective-permute-start | bytes 393224 | tf_op jit(solution)/shard_map/ppermute | solution.py:23
  74.5 19.0 %all-to-all-start = ((f32[8,16,256]{2,1,0:T(8,128)}), f32[8,16,256]{2,1,0:T(8,128)S(1)}, u32[]{:S(2)}, u32[]{:S(2)}) async-start(f32[8,16,256]{2,1,0:T(8,128)} %bitcast.34), calls=%async_computation | async-start | bytes 262144 | tf_op jit(solution)/shard_map/all_to_all | solution.py:52

commit v17 on v16

--- a/solution.py
+++ b/solution.py
@@ -4,7 +4,7 @@
 from jax.sharding import PartitionSpec as P
 
 
-PARTNER_MASKS = {64: {4: 6, 8: 14, 16: 24, 32: 56}}
+PARTNER_MASKS = {64: {16: 24, 32: 56}}
 
 
 def scan_both(decay, state, grad, axis):

time: 94.6 us -> 92.8 us (0.981)
  the two profiles are of different devices: /device:TPU:48 before, /device:TPU:40 now
where the time goes in v17:
time: 92.8 us; the launch traced here: 92.3 us
  waiting for transfers between devices  43.6 us (47%)
  starting transfers between devices  40.3 us (43%)
  local copies, waits for them, and re-layouts  3.76 us (4%)
  matrix products  2.09 us (2%)
  other arithmetic  1.64 us (2%)
  between operations  0.95 us (1%)
    ppermute x5, waiting for transfers between devices, scan_both(): got = lax.ppermute(message, axis, pairs)  31.2 us
    ppermute x5, starting transfers between devices, scan_both(): got = lax.ppermute(message, axis, pairs)  25.1 us
    all_to_all x1, starting transfers between devices, scatter_sum(): lax.all_to_all(values.reshape(devices, rows // devices, cols), axis, 0, 0)  12.2 us
    ppermute x1, waiting for transfers between devices, scan_both(): got = lax.ppermute(jnp.where(later, block_grad, block_state), axis, pairs)  6.7 us
    all_to_all x1, waiting for transfers between devices, scatter_sum(): lax.all_to_all(values.reshape(devices, rows // devices, cols), axis, 0, 0)  5.71 us
    ppermute x1, starting transfers between devices, scan_both(): got = lax.ppermute(jnp.where(later, block_grad, block_state), axis, pairs)  3.03 us
  transfers between devices with their start and end apart: 7, of which 7 were waited for; matrix products, arithmetic and copies ran while one was open for 3% of the time, Pallas kernels for 0%

profile of v17, /device:TPU:40, one launch (start us, length us, event | category | flops | bytes accessed | tf_op | source)
XLA Modules:
  0.0 92.3 jit_solution(7195615490304515392)
XLA Ops:
  0.6 1.0 %reduce_window_sum.11 = f32[8,128]{1,0:T(8,128)S(1)} reduce-window(f32[8,128]{1,0:T(8,128)} %param.8, f32[]{:T(128)} %constant.12.clone.1), window={size=1x128 pad=0_0x127_0}, to_apply=%region_0.0 | reduce-window | flops 130048 | bytes 8196 | tf_op jit(solution)/shard_map/jit(cumsum)/reduce_window_sum | solution.py:73
  1.6 0.2 slice_reduce_fusion
  2.2 0.7 copy-done
  3.0 0.2 fusion.10
  3.4 10.9 %collective-permute-start = (f32[257,256]{1,0:T(8,128)S(1)}, f32[257,256]{1,0:T(8,128)S(1)}, u32[]{:S(2)}, u32[]{:S(2)}) collective-permute-start(f32[257,256]{1,0:T(8,128)S(1)} %pad_maximum_fusion), channel_id=1, source_target_pairs={{0,8},{8,0},{16,24},{24,16},{32,40},{40,32},{48,56},{56,48},{64,72... | collective-permute-start | bytes 789512 | tf_op jit(solution)/shard_map/ppermute | solution.py:27
  14.4 6.5 %collective-permute-done = f32[257,256]{1,0:T(8,128)S(1)} collective-permute-done((f32[257,256]{1,0:T(8,128)S(1)}, f32[257,256]{1,0:T(8,128)S(1)}, u32[]{:S(2)}, u32[]{:S(2)}) %collective-permute-start) | collective-permute-done | bytes 263200 | tf_op jit(solution)/shard_map/ppermute | solution.py:27
  21.0 3.4 %collective-permute-start.1 = (f32[257,256]{1,0:T(8,128)S(1)}, f32[257,256]{1,0:T(8,128)S(1)}, u32[]{:S(2)}, u32[]{:S(2)}) collective-permute-start(f32[257,256]{1,0:T(8,128)S(1)} %pad_maximum_fusion.1), channel_id=1, source_target_pairs={{0,16},{8,24},{16,0},{24,8},{32,48},{40,56},{48,32},{56,40},{64,80... | collective-permute-start | bytes 789512 | tf_op jit(solution)/shard_map/ppermute | solution.py:27
  24.4 6.0 %collective-permute-done.1 = f32[257,256]{1,0:T(8,128)S(1)} collective-permute-done((f32[257,256]{1,0:T(8,128)S(1)}, f32[257,256]{1,0:T(8,128)S(1)}, u32[]{:S(2)}, u32[]{:S(2)}) %collective-permute-start.1) | collective-permute-done | bytes 263200 | tf_op jit(solution)/shard_map/ppermute | solution.py:27
  30.5 4.9 %collective-permute-start.2 = (f32[257,256]{1,0:T(8,128)S(1)}, f32[257,256]{1,0:T(8,128)S(1)}, u32[]{:S(2)}, u32[]{:S(2)}) collective-permute-start(f32[257,256]{1,0:T(8,128)S(1)} %pad_maximum_fusion.2), channel_id=1, source_target_pairs={{0,32},{8,40},{16,48},{24,56},{32,0},{40,8},{48,16},{56,24},{64,96... | collective-permute-start | bytes 789512 | tf_op jit(solution)/shard_map/ppermute | solution.py:27
  35.5 5.1 %collective-permute-done.2 = f32[257,256]{1,0:T(8,128)S(1)} collective-permute-done((f32[257,256]{1,0:T(8,128)S(1)}, f32[257,256]{1,0:T(8,128)S(1)}, u32[]{:S(2)}, u32[]{:S(2)}) %collective-permute-start.2) | collective-permute-done | bytes 263200 | tf_op jit(solution)/shard_map/ppermute | solution.py:27
  40.6 3.2 %collective-permute-start.3 = (f32[257,256]{1,0:T(8,128)S(1)}, f32[257,256]{1,0:T(8,128)S(1)}, u32[]{:S(2)}, u32[]{:S(2)}) collective-permute-start(f32[257,256]{1,0:T(8,128)S(1)} %pad_maximum_fusion.3), channel_id=1, source_target_pairs={{0,64},{8,72},{16,80},{24,88},{32,96},{40,104},{48,112},{56,120},{... | collective-permute-start | bytes 789512 | tf_op jit(solution)/shard_map/ppermute | solution.py:27
  43.9 0.1 copy.15
  44.0 0.1 copy.20
  44.2 0.3 fusion
  44.5 4.5 %collective-permute-done.3 = f32[257,256]{1,0:T(8,128)S(1)} collective-permute-done((f32[257,256]{1,0:T(8,128)S(1)}, f32[257,256]{1,0:T(8,128)S(1)}, u32[]{:S(2)}, u32[]{:S(2)}) %collective-permute-start.3) | collective-permute-done | bytes 263200 | tf_op jit(solution)/shard_map/ppermute | solution.py:27
  49.1 2.6 %collective-permute-start.4 = (f32[257,256]{1,0:T(8,128)S(1)}, f32[257,256]{1,0:T(8,128)S(1)}, u32[]{:S(2)}, u32[]{:S(2)}) collective-permute-start(f32[257,256]{1,0:T(8,128)S(1)} %pad_maximum_fusion.4), channel_id=1, source_target_pairs={{0,192},{8,200},{16,208},{24,216},{32,224},{40,232},{48,240},{56,2... | collective-permute-start | bytes 789512 | tf_op jit(solution)/shard_map/ppermute | solution.py:27
  51.7 0.2 fusion.24
  51.9 0.2 fusion.28
  52.2 9.1 %collective-permute-done.4 = f32[257,256]{1,0:T(8,128)S(1)} collective-permute-done((f32[257,256]{1,0:T(8,128)S(1)}, f32[257,256]{1,0:T(8,128)S(1)}, u32[]{:S(2)}, u32[]{:S(2)}) %collective-permute-start.4) | collective-permute-done | bytes 263200 | tf_op jit(solution)/shard_map/ppermute | solution.py:27
  61.4 3.0 %collective-permute-start.5 = (f32[128,256]{1,0:T(8,128)S(1)}, f32[128,256]{1,0:T(8,128)S(1)}, u32[]{:S(2)}, u32[]{:S(2)}) collective-permute-start(f32[128,256]{1,0:T(8,128)S(1)} %select_select_fusion), channel_id=1, source_target_pairs={{0,448},{8,456},{16,464},{24,472},{32,480},{40,488},{48,496},{56,5... | collective-permute-start | bytes 393224 | tf_op jit(solution)/shard_map/ppermute | solution.py:23
  64.4 0.1 fusion.26
  64.5 6.7 %collective-permute-done.5 = f32[128,256]{1,0:T(8,128)S(1)} collective-permute-done((f32[128,256]{1,0:T(8,128)S(1)}, f32[128,256]{1,0:T(8,128)S(1)}, u32[]{:S(2)}, u32[]{:S(2)}) %collective-permute-start.5) | collective-permute-done | bytes 131104 | tf_op jit(solution)/shard_map/ppermute | solution.py:23
  71.2 0.1 fusion.8
  71.3 0.2 fusion.30
  71.6 0.2 convolution_add_fusion.1
  71.7 0.2 convolution_add_fusion
  72.0 0.8 copy.21
  72.7 12.2 %all-to-all-start = ((f32[8,16,256]{2,1,0:T(8,128)}), f32[8,16,256]{2,1,0:T(8,128)S(1)}, u32[]{:S(2)}, u32[]{:S(2)}) async-start(f32[8,16,256]{2,1,0:T(8,128)} %bitcast.34), calls=%async_computation | async-start | bytes 262144 | tf_op jit(solution)/shard_map/all_to_all | solution.py:52
  84.9 0.3 fusion.2
  85.3 0.7 copy.22
  86.0 5.7 %all-to-all-done = f32[8,16,256]{2,1,0:T(8,128)S(1)} async-done(((f32[8,16,256]{2,1,0:T(8,128)}), f32[8,16,256]{2,1,0:T(8,128)S(1)}, u32[]{:S(2)}, u32[]{:S(2)}) %all-to-all-start) | async-done | bytes 131104 | tf_op jit(solution)/shard_map/all_to_all | solution.py:52
  91.7 0.6 fusion.41
  (39 shorter events, 1.1 us)
Async XLA Ops:
  2.0 0.8 copy-start
  2.0 0.9 copy-start.1
  2.0 0.9 copy-start.2
  2.0 0.8 copy-start.3
  3.4 17.5 %collective-permute-start = (f32[257,256]{1,0:T(8,128)S(1)}, f32[257,256]{1,0:T(8,128)S(1)}, u32[]{:S(2)}, u32[]{:S(2)}) collective-permute-start(f32[257,256]{1,0:T(8,128)S(1)} %pad_maximum_fusion), channel_id=1, source_target_pairs={{0,8},{8,0},{16,24},{24,16},{32,40},{40,32},{48,56},{56,48},{64,72... | collective-permute-start | bytes 789512 | tf_op jit(solution)/shard_map/ppermute | solution.py:27
  21.0 9.4 %collective-permute-start.1 = (f32[257,256]{1,0:T(8,128)S(1)}, f32[257,256]{1,0:T(8,128)S(1)}, u32[]{:S(2)}, u32[]{:S(2)}) collective-permute-start(f32[257,256]{1,0:T(8,128)S(1)} %pad_maximum_fusion.1), channel_id=1, source_target_pairs={{0,16},{8,24},{16,0},{24,8},{32,48},{40,56},{48,32},{56,40},{64,80... | collective-permute-start | bytes 789512 | tf_op jit(solution)/shard_map/ppermute | solution.py:27
  30.5 10.0 %collective-permute-start.2 = (f32[257,256]{1,0:T(8,128)S(1)}, f32[257,256]{1,0:T(8,128)S(1)}, u32[]{:S(2)}, u32[]{:S(2)}) collective-permute-start(f32[257,256]{1,0:T(8,128)S(1)} %pad_maximum_fusion.2), channel_id=1, source_target_pairs={{0,32},{8,40},{16,48},{24,56},{32,0},{40,8},{48,16},{56,24},{64,96... | collective-permute-start | bytes 789512 | tf_op jit(solution)/shard_map/ppermute | solution.py:27
  40.6 8.4 %collective-permute-start.3 = (f32[257,256]{1,0:T(8,128)S(1)}, f32[257,256]{1,0:T(8,128)S(1)}, u32[]{:S(2)}, u32[]{:S(2)}) collective-permute-start(f32[257,256]{1,0:T(8,128)S(1)} %pad_maximum_fusion.3), channel_id=1, source_target_pairs={{0,64},{8,72},{16,80},{24,88},{32,96},{40,104},{48,112},{56,120},{... | collective-permute-start | bytes 789512 | tf_op jit(solution)/shard_map/ppermute | solution.py:27
  49.1 12.2 %collective-permute-start.4 = (f32[257,256]{1,0:T(8,128)S(1)}, f32[257,256]{1,0:T(8,128)S(1)}, u32[]{:S(2)}, u32[]{:S(2)}) collective-permute-start(f32[257,256]{1,0:T(8,128)S(1)} %pad_maximum_fusion.4), channel_id=1, source_target_pairs={{0,192},{8,200},{16,208},{24,216},{32,224},{40,232},{48,240},{56,2... | collective-permute-start | bytes 789512 | tf_op jit(solution)/shard_map/ppermute | solution.py:27
  61.4 9.9 %collective-permute-start.5 = (f32[128,256]{1,0:T(8,128)S(1)}, f32[128,256]{1,0:T(8,128)S(1)}, u32[]{:S(2)}, u32[]{:S(2)}) collective-permute-start(f32[128,256]{1,0:T(8,128)S(1)} %select_select_fusion), channel_id=1, source_target_pairs={{0,448},{8,456},{16,464},{24,472},{32,480},{40,488},{48,496},{56,5... | collective-permute-start | bytes 393224 | tf_op jit(solution)/shard_map/ppermute | solution.py:23
  72.7 19.0 %all-to-all-start = ((f32[8,16,256]{2,1,0:T(8,128)}), f32[8,16,256]{2,1,0:T(8,128)S(1)}, u32[]{:S(2)}, u32[]{:S(2)}) async-start(f32[8,16,256]{2,1,0:T(8,128)} %bitcast.34), calls=%async_computation | async-start | bytes 262144 | tf_op jit(solution)/shard_map/all_to_all | solution.py:52
